TPU v7x, 512 devices: a whole 4x8x8 slice. The times are simulated.
512 devices in a mesh: dp: 16 (over y, x_lo), table: 32 (over z, x_hi, core).
Axes of the slice: x: 4 (x_hi: 2, x_lo: 2; x = x_hi * 2 + x_lo), y: 8, z: 8, core: 2. Of those that a mesh axis runs over, the one named last changes fastest.
Arguments:
- id_table: bfloat16 [32768, 256], P('table'), may hold values from -2 to 2
- lookup_ids: int32 [65536, 8, 2], P(('dp', 'table')), may hold values from 0 to 32767, as said below
- row_owner: int32 [32768], replicated, may hold values from 0 to 32767, as said below
- query_tower: bfloat16 [1024, 256], replicated, may hold values from -1 to 1
- item_tower: bfloat16 [1024, 256], replicated, may hold values from -1 to 1
- row_seeds: int32 [32768], P('table'), may hold values from 0 to 1073741823
- tower_seeds: int32 [2, 1024], replicated, may hold values from 0 to 1073741823
Outputs:
- table_update: float32 [32768, 256], P('table')
- tower_update: float32 [2, 1024, 256], replicated
Inputs may be any that keep to these rules, and one draw needn't show every extreme that they name: `lookup_ids`: in every aligned block of 128 examples (the examples of one device), at most 96 of the lookups have row_owner[id] // 1024 equal to any one table shard, and exactly 96 do for some shard. A permutation: the row of id i lies at position row_owner[i] of id_table, on table shard row_owner[i] // 1024.
All inputs are finite; a program needn't handle non-finite values.
Results may differ from a plain program's by a relative error of at most 0.0073.
The roundings to bfloat16 on the way count: a program that leaves them out, or rounds other values in their place, can miss the bound.
Values may be sent and summed in bfloat16 or wider, within the bound.
No kernel may reach another device: no remote copies, remote signals or barrier semaphores. Data moves between devices by JAX's collectives and lax.ppermute only.
A program may use at most 64 MiB of HBM per device.

v0:
```python
import math

import jax
import jax.numpy as jnp
from jax import lax
from jax.sharding import PartitionSpec as P

NOISE_MULT = 0.1


def hashed_noise(seed_rows, width):
    columns = jnp.arange(width, dtype=jnp.int32)
    summed = jnp.zeros(seed_rows.shape + (width,), jnp.float32)
    for section in range(2):
        mixed = seed_rows[..., None] + (columns * 2 + section) * 1013904223
        mixed = mixed ^ mixed >> 15 & 131071
        mixed = mixed * 73244475
        mixed = mixed ^ mixed >> 13 & 524287
        mixed = mixed * 1597334677
        mixed = mixed ^ mixed >> 16 & 65535
        lower = (mixed & 65535).astype(jnp.float32) / 65536.0 - 0.5
        upper = (mixed >> 16 & 65535).astype(jnp.float32) / 65536.0 - 0.5
        summed = summed + lower + upper
    return summed * math.sqrt(3.0)


def squares(values):
    return jnp.sum(jnp.square(values.astype(jnp.float32)), axis=1)


def body(id_table, lookup_ids, row_owner, query_tower, item_tower, row_seeds, tower_seeds):
    shards = lax.axis_size("table")
    rows_dev, emb_width = id_table.shape
    batch, slots, bags = lookup_ids.shape
    feats = slots // 2
    hidden_width, out_width = query_tower.shape
    scale = 200.0 / math.sqrt(out_width)
    clip_norm = 0.9 * math.sqrt(2.0 * hidden_width + 400.0)
    requests = batch * slots * bags
    capacity = 3 * requests // (2 * shards)
    positions = row_owner[lookup_ids.reshape(-1)]
    owners = positions // rows_dev
    local_rows = positions - owners * rows_dev
    one_hot = (owners[:, None] == jnp.arange(shards, dtype=jnp.int32)[None, :]).astype(jnp.int32)
    ranks = jnp.sum((jnp.cumsum(one_hot, axis=0) - one_hot) * one_hot, axis=1)
    targets = owners * capacity + ranks
    outgoing = jnp.full((shards * capacity,), -1, jnp.int32).at[targets].set(local_rows)
    outgoing = outgoing.reshape(shards, capacity)
    incoming = lax.all_to_all(outgoing, "table", split_axis=0, concat_axis=0, tiled=True)
    valid = incoming >= 0
    fetched = id_table[jnp.where(valid, incoming, 0)]
    fetched = jnp.where(valid[:, :, None], fetched, jnp.zeros((), jnp.bfloat16))
    returned = lax.all_to_all(fetched, "table", split_axis=0, concat_axis=0, tiled=True)
    returned, incoming = (returned, incoming)
    looked = returned.reshape(shards * capacity, emb_width)[targets]
    pooled = jnp.sum(looked.reshape(batch, slots, bags, emb_width).astype(jnp.float32), axis=2)
    pooled = pooled.astype(jnp.bfloat16)
    query_in = pooled[:, :feats].reshape(batch, hidden_width)
    item_in = pooled[:, feats:].reshape(batch, hidden_width)
    query_vec = jnp.dot(query_in, query_tower, preferred_element_type=jnp.float32).astype(
        jnp.bfloat16
    )
    item_vec = jnp.dot(item_in, item_tower, preferred_element_type=jnp.float32).astype(jnp.bfloat16)
    all_items = lax.all_gather(item_vec, "dp", axis=0, tiled=True)
    scores = scale * lax.dot_general(
        query_vec, all_items, (((1,), (1,)), ((), ())), preferred_element_type=jnp.float32
    )
    peak = jnp.max(scores, axis=1, keepdims=True)
    log_total = peak + jnp.log(jnp.sum(jnp.exp(scores - peak), axis=1, keepdims=True))
    probs = jnp.exp(scores - log_total).astype(jnp.bfloat16)
    query_grad = (
        scale
        * (
            jnp.dot(probs, all_items, preferred_element_type=jnp.float32)
            - item_vec.astype(jnp.float32)
        )
    ).astype(jnp.bfloat16)
    weighted = lax.psum_scatter(
        lax.dot_general(
            probs, query_vec, (((0,), (0,)), ((), ())), preferred_element_type=jnp.float32
        ),
        "dp",
        scatter_dimension=0,
        tiled=True,
    )
    item_grad = (scale * (weighted - query_vec.astype(jnp.float32))).astype(jnp.bfloat16)
    query_back = lax.dot_general(
        query_grad, query_tower, (((1,), (1,)), ((), ())), preferred_element_type=jnp.float32
    )
    item_back = lax.dot_general(
        item_grad, item_tower, (((1,), (1,)), ((), ())), preferred_element_type=jnp.float32
    )
    norm_sq = (
        squares(query_in) * squares(query_grad)
        + squares(item_in) * squares(item_grad)
        + squares(query_back)
        + squares(item_back)
    )
    factor = jnp.minimum(1.0, clip_norm / jnp.sqrt(norm_sq + 1e-06))
    clipped_query = (factor[:, None] * query_grad.astype(jnp.float32)).astype(jnp.bfloat16)
    clipped_item = (factor[:, None] * item_grad.astype(jnp.float32)).astype(jnp.bfloat16)
    tower_part = jnp.stack(
        [
            lax.dot_general(
                query_in,
                clipped_query,
                (((0,), (0,)), ((), ())),
                preferred_element_type=jnp.float32,
            ),
            lax.dot_general(
                item_in, clipped_item, (((0,), (0,)), ((), ())), preferred_element_type=jnp.float32
            ),
        ]
    )
    tower_sum = lax.psum(tower_part, ("dp", "table"))
    back_all = jnp.concatenate(
        [query_back.reshape(batch, feats, emb_width), item_back.reshape(batch, feats, emb_width)],
        axis=1,
    )
    lookup_grad = (factor[:, None, None] * back_all).astype(jnp.bfloat16)
    spread = jnp.broadcast_to(lookup_grad[:, :, None, :], (batch, slots, bags, emb_width))
    spread = spread.reshape(requests, emb_width)
    grad_out = jnp.zeros((shards * capacity, emb_width), jnp.bfloat16).at[targets].set(spread)
    grad_in = lax.all_to_all(
        grad_out.reshape(shards, capacity, emb_width),
        "table",
        split_axis=0,
        concat_axis=0,
        tiled=True,
    )
    flat_in = incoming.reshape(-1)
    slot_rows = jnp.where(flat_in >= 0, flat_in, rows_dev)
    row_sum = (
        jnp.zeros((rows_dev, emb_width), jnp.float32)
        .at[slot_rows]
        .add(grad_in.reshape(shards * capacity, emb_width).astype(jnp.float32), mode="drop")
    )
    row_count = (
        jnp.zeros((rows_dev,), jnp.float32)
        .at[slot_rows]
        .add((flat_in >= 0).astype(jnp.float32), mode="drop")
    )
    row_sum, row_count = lax.psum((row_sum, row_count), "dp")
    row_noise = hashed_noise(row_seeds, emb_width)
    table_update = row_sum / clip_norm + NOISE_MULT * jnp.where(
        row_count[:, None] > 0.0, row_noise, 0.0
    )
    tower_update = tower_sum / clip_norm + NOISE_MULT * hashed_noise(tower_seeds, out_width)
    return (table_update, tower_update)


def solution(mesh):
    in_specs = (P("table", None), P(("dp", "table"), None, None), P(), P(), P(), P("table"), P())
    out_specs = (P("table", None), P())
    return jax.shard_map(body, mesh=mesh, in_specs=in_specs, out_specs=out_specs, check_vma=False)
```

profile of v0, /device:TPU:1, one launch (start us, length us, event | category | flops | bytes accessed | tf_op | source)
XLA Modules:
  0.0 740.1 jit_solution(12677365749732896167)
XLA Ops:
  7.2 1.0 copy.37
  8.2 0.3 reshape.312
  8.6 11.8 %gather_fusion = s32[2048]{0:T(1024)S(1)} fusion(s32[32768]{0:T(1024)S(1)} %copy-done.1, s32[2048]{0:T(1024)S(1)} %broadcast_clamp_fusion.2), kind=kCustom, calls=%fused_computation | custom fusion | bytes 24576 | tf_op jit(solution)/shard_map/gather | solution.py:41
  20.4 9.1 %reduce-window.6 = s32[32,16,128]{2,1,0:T(8,128)S(1)} reduce-window(s32[32,16,128]{2,1,0:T(8,128)S(1)} %fusion.35, s32[]{:T(128)} %constant.35.clone.1), window={size=1x1x128 pad=0_0x0_0x127_0}, to_apply=%region_0.1 | reduce-window | flops 8323072 | bytes 524292 | tf_op jit(solution)/shard_map/reduce-window
  29.6 0.2 copy.45
  30.4 8.1 %scatter_custom_fusion = s32[3072]{0:T(1024)S(1)} fusion(s32[2048]{0:T(1024)S(1)} %bitcast.90, s32[2048]{0:T(1024)S(1)} %get-tuple-element.8, s32[]{:T(128)} %constant.34.clone.1), kind=kCustom, calls=%fused_computation.112 | custom fusion | bytes 12292 | tf_op jit(solution)/shard_map/scatter | solution.py:47
  38.6 23.6 %all_to_all.22 = s32[32,1,96]{2,1,0:T(1,128)S(1)} all-to-all(s32[32,1,96]{2,1,0:T(1,128)S(1)} %all_to_all.14), channel_id=1, replica_groups=mesh['dp'=16,'table'=32] {'table'}, dimensions={0} | all-to-all | bytes 24576 | tf_op jit(solution)/shard_map/all_to_all | solution.py:49
  62.2 0.6 fusion.54
  62.9 11.1 %gather_fusion.1 = bf16[3072,256]{1,0:T(8,128)(2,1)S(1)} fusion(bf16[1024,256]{1,0:T(8,128)(2,1)S(1)} %copy-done, s32[3072]{0:T(1024)S(1)} %broadcast_clamp_fusion), kind=kCustom, calls=%fused_computation.1 | custom fusion | bytes 3158016 | tf_op jit(solution)/shard_map/gather | solution.py:51
  73.9 1.5 broadcast_select_fusion
  75.4 4.2 all-to-all-start.1
  79.7 39.1 %all-to-all-done.1 = bf16[32,96,256]{2,1,0:T(8,128)(2,1)S(1)} async-done(((bf16[32,96,256]{2,1,0:T(8,128)(2,1)}), bf16[32,96,256]{2,1,0:T(8,128)(2,1)S(1)}, u32[]{:S(2)}, u32[]{:S(2)}) %all-to-all-start.1) | async-done | bytes 1572896 | tf_op jit(solution)/shard_map/all_to_all | solution.py:53
  118.8 7.5 %gather_fusion.2 = bf16[2048,256]{1,0:T(8,128)(2,1)S(1)} fusion(bf16[3072,256]{1,0:T(8,128)(2,1)S(1)} %bitcast.75, s32[2048]{0:T(1024)S(1)} %broadcast_clamp_fusion.1), kind=kCustom, calls=%fused_computation.2 | custom fusion | bytes 2105344 | tf_op jit(solution)/shard_map/gather | solution.py:55
  126.3 0.4 reshape.316
  126.8 2.8 reduce_sum.88
  129.8 0.2 copy.44
  130.1 0.9 convolution_convert_fusion
  131.4 0.3 convolution_convert_fusion.1
  131.7 58.0 %all-gather.2.cloned.1.call-done = bf16[2048,256]{1,0:T(8,128)(2,1)} async-done(((bf16[128,256]{1,0:T(8,128)(2,1)}), bf16[2048,256]{1,0:T(8,128)(2,1)}) %all-gather.2.cloned.1.call-update) | async-done | bytes 1048592 | tf_op jit(solution)/shard_map/all_gather | solution.py:64
  189.7 1.8 fusion.56
  191.5 0.3 exponential_reduce_fusion
  191.8 1.9 fusion.53
  193.8 1.8 multiply_reduce_fusion.2
  195.6 1.8 fusion.36
  197.4 0.4 multiply_reduce_fusion.1
  197.8 0.3 concatenate.11
  198.1 72.7 %reduce-scatter.2.cloned.1.call-done = f32[128,256]{1,0:T(8,128)} async-done(((f32[2048,256]{1,0:T(8,128)}), f32[128,256]{1,0:T(8,128)}) %reduce-scatter.2.cloned.1.call-update) | async-done | bytes 131088 | tf_op jit(solution)/shard_map/reduce_scatter | solution.py:78
  270.8 1.0 fusion.38
  271.8 0.4 multiply_reduce_fusion
  272.2 0.3 concatenate.12
  272.5 0.2 fusion.28
  272.8 0.7 broadcast_in_dim.40
  273.5 0.4 reshape.359
  274.0 10.7 %scatter_custom_fusion.1 = bf16[3072,256]{1,0:T(8,128)(2,1)} fusion(s32[2048]{0:T(1024)} %bitcast.92, bf16[2048,256]{1,0:T(8,128)(2,1)S(1)} %reshape.359, bf16[]{:T(256)} %constant.43.clone.1), kind=kCustom, calls=%fused_computation.57 | custom fusion | bytes 1573376 | tf_op jit(solution)/shard_map/scatter | solution.py:123
  284.7 21.0 %all-to-all-start.2 = ((bf16[32,96,256]{2,1,0:T(8,128)(2,1)}), bf16[32,96,256]{2,1,0:T(8,128)(2,1)S(1)}, u32[]{:S(2)}, u32[]{:S(2)}) async-start(bf16[32,96,256]{2,1,0:T(8,128)(2,1)} %bitcast.77), calls=%async_computation.3 | async-start | bytes 3145728 | tf_op jit(solution)/shard_map/all_to_all | solution.py:124
  305.7 0.4 convolution_bitcast_fusion
  306.1 0.3 convolution_bitcast_fusion.1
  306.4 1.5 pad_maximum_fusion
  308.0 0.5 broadcast.460
  308.5 0.7 reduce.6
  309.3 37.9 %all-to-all-done.2 = bf16[32,96,256]{2,1,0:T(8,128)(2,1)S(1)} async-done(((bf16[32,96,256]{2,1,0:T(8,128)(2,1)}), bf16[32,96,256]{2,1,0:T(8,128)(2,1)S(1)}, u32[]{:S(2)}, u32[]{:S(2)}) %all-to-all-start.2) | async-done | bytes 1572896 | tf_op jit(solution)/shard_map/all_to_all | solution.py:124
  347.2 18.1 %scatter_custom_fusion.2 = f32[1024,256]{1,0:T(8,128)} fusion(s32[3072]{0:T(1024)S(1)} %bitcast.95, bf16[3072,256]{1,0:T(8,128)(2,1)S(1)} %bitcast.76, f32[]{:T(128)} %constant.33.clone.1), kind=kCustom, calls=%fused_computation.7 | custom fusion | flops 1572864 | bytes 2621444 | tf_op jit(solution)/shard_map/scatter-add | solution.py:136
  365.4 19.7 %scatter_custom_fusion.3 = f32[1024]{0:T(1024)S(1)} fusion(s32[3072]{0:T(1024)S(1)} %bitcast.96, f32[3072]{0:T(1024)S(1)} %reshape.375, f32[]{:T(128)} %constant.33.clone.1), kind=kCustom, calls=%fused_computation.117 | custom fusion | flops 3072 | bytes 4100 | tf_op jit(solution)/shard_map/scatter-add | solution.py:141
  385.2 24.3 %psum.22 = f32[1024]{0:T(1024)S(1)} all-reduce(f32[1024]{0:T(1024)S(1)} %scatter_custom_fusion.3), channel_id=1, replica_groups=mesh['dp'=16,'table'=32] {'dp'}, use_global_device_ids=true, to_apply=%region_18.19 | all-reduce | flops 1024 | bytes 8192 | tf_op jit(solution)/shard_map/psum | solution.py:143
  409.5 186.1 %all-reduce.5.cloned.1.call-done = f32[2,1024,256]{2,1,0:T(8,128)} async-done(((f32[2,1024,256]{2,1,0:T(8,128)}), f32[2,1024,256]{2,1,0:T(8,128)}) %all-reduce.5.cloned.1.call-update) | async-done | bytes 2097168 | tf_op jit(solution)/shard_map/psum | solution.py:115
  595.6 5.3 multiply_add_fusion
  600.9 129.1 %all-reduce.3.cloned.1.call-done = f32[1024,256]{1,0:T(8,128)} async-done(((f32[1024,256]{1,0:T(8,128)}), f32[1024,256]{1,0:T(8,128)}) %all-reduce.3.cloned.1.call-update) | async-done | bytes 1048592 | tf_op jit(solution)/shard_map/psum | solution.py:143
  730.0 3.5 multiply_add_fusion.1
  (64 shorter events, 2.0 us)
Async XLA Ops:
  7.2 55.7 %copy-start = (bf16[1024,256]{1,0:T(8,128)(2,1)S(1)}, bf16[1024,256]{1,0:T(8,128)(2,1)}, u32[]{:S(2)}) copy-start(bf16[1024,256]{1,0:T(8,128)(2,1)} %param.7) | copy-start | bytes 1572868
  7.2 1.4 copy-start.1
  30.4 49.3 %copy-start.9 = (s32[2048,1]{0,1:T(1,128)}, s32[2048,1]{0,1:T(1,128)S(1)}, u32[]{:S(2)}) copy-start(s32[2048,1]{0,1:T(1,128)S(1)} %compare_select_fusion.2) | copy-start | bytes 24580
  75.4 43.4 %all-to-all-start.1 = ((bf16[32,96,256]{2,1,0:T(8,128)(2,1)}), bf16[32,96,256]{2,1,0:T(8,128)(2,1)S(1)}, u32[]{:S(2)}, u32[]{:S(2)}) async-start(bf16[32,96,256]{2,1,0:T(8,128)(2,1)} %broadcast_select_fusion), calls=%async_computation.1 | async-start | bytes 3145728 | tf_op jit(solution)/shard_map/all_to_all | solution.py:53
  79.6 110.1 %all-gather.2.cloned.1.call-start = ((), (), s32[]{:S(2)}) async-start(), calls=%async_computation.4 | async-start | bytes 1114112 | tf_op jit(solution)/shard_map/all_gather | solution.py:64
  126.7 3.3 copy-start.6
  126.8 4.7 copy-start.4
  129.8 1.9 copy-start.3
  131.0 139.8 %reduce-scatter.2.cloned.1.call-start = ((), (), s32[]{:S(2)}) async-start(), calls=%async_computation.5 | async-start | bytes 2228224 | tf_op jit(solution)/shard_map/reduce_scatter | solution.py:78
  191.8 1.9 copy-start.15
  193.7 1.9 copy-start.2
  193.7 3.7 copy-start.5
  197.4 74.4 %copy-start.7 = (bf16[1024,256]{1,0:T(8,128)(2,1)S(1)}, bf16[1024,256]{1,0:T(8,128)(2,1)}, u32[]{:S(2)}) copy-start(bf16[1024,256]{1,0:T(8,128)(2,1)} %param.11) | copy-start | bytes 1572868
  197.4 75.1 %copy-start.12 = (f32[128]{0:T(128)S(1)}, f32[128]{0:T(128)}, u32[]{:S(2)}) copy-start(f32[128]{0:T(128)} %get-tuple-element.18) | copy-start | bytes 1540
  197.4 75.1 %copy-start.13 = (f32[128]{0:T(128)S(1)}, f32[128]{0:T(128)}, u32[]{:S(2)}) copy-start(f32[128]{0:T(128)} %get-tuple-element.19) | copy-start | bytes 1540
  197.4 75.1 %copy-start.14 = (f32[128]{0:T(128)S(1)}, f32[128]{0:T(128)}, u32[]{:S(2)}) copy-start(f32[128]{0:T(128)} %get-tuple-element.16) | copy-start | bytes 1540
  284.7 62.5 %all-to-all-start.2 = ((bf16[32,96,256]{2,1,0:T(8,128)(2,1)}), bf16[32,96,256]{2,1,0:T(8,128)(2,1)S(1)}, u32[]{:S(2)}, u32[]{:S(2)}) async-start(bf16[32,96,256]{2,1,0:T(8,128)(2,1)} %bitcast.77), calls=%async_computation.3 | async-start | bytes 3145728 | tf_op jit(solution)/shard_map/all_to_all | solution.py:124
  305.7 289.9 %all-reduce.5.cloned.1.call-start = ((), (), s32[]{:S(2)}) async-start(), calls=%async_computation.7 | async-start | bytes 4194304 | tf_op jit(solution)/shard_map/psum | solution.py:115
  307.9 57.4 %copy-start.8 = (f32[32,1,96]{2,0,1:T(8,128)S(1)}, f32[32,1,96]{2,0,1:T(8,128)}, u32[]{:S(2)}) copy-start(f32[32,1,96]{2,0,1:T(8,128)} %get-tuple-element.2) | copy-start | bytes 36868
  307.9 287.7 %copy-start.10 = (s32[2,1024]{1,0:T(2,128)S(1)}, s32[2,1024]{1,0:T(2,128)}, u32[]{:S(2)}) copy-start(s32[2,1024]{1,0:T(2,128)} %param.13) | copy-start | bytes 24580
  307.9 422.1 %all-reduce.3.cloned.1.call-start = ((), (), s32[]{:S(2)}) async-start(), calls=%async_computation.6 | async-start | bytes 2097152 | tf_op jit(solution)/shard_map/psum | solution.py:143
  595.6 134.4 %copy-start.11 = (s32[1024]{0:T(1024)S(1)}, s32[1024]{0:T(1024)}, u32[]{:S(2)}) copy-start(s32[1024]{0:T(1024)} %param.12) | copy-start | bytes 12292
Sparse Core Ops, SparseCore 0:
  131.1 58.5 all-gather.1
  193.8 76.9 reduce-scatter.1
  312.0 283.5 all-reduce.4
  599.2 130.7 all-reduce.2
where the time goes:
time: 750 us; the launch traced here: 740 us
  waiting for transfers between devices  523 us (70%)
  other arithmetic  66.9 us (9%)
  local copies, waits for them, and re-layouts  54.5 us (7%)
  blocking collectives  47.9 us (6%)
  starting transfers between devices  25.5 us (3%)
  between operations  14.2 us (2%)
  matrix products  8.09 us (1%)
    psum x1, waiting for transfers between devices, body(): tower_sum = lax.psum(tower_part, ('dp', 'table'))  186 us
    psum x1, waiting for transfers between devices, body(): row_sum, row_count = lax.psum((row_sum, row_count), 'dp')  129 us
    reduce_scatter x1, waiting for transfers between devices, body(): lax.psum_scatter(lax.dot_general(probs, query_vec, (((0,), (0,)), ((), ()...  72.7 us
    all_gather x1, waiting for transfers between devices, body(): all_items = lax.all_gather(item_vec, 'dp', axis=0, tiled=True)  58 us
    all_to_all x1, waiting for transfers between devices, body(): lax.all_to_all(fetched, 'table', split_axis=0, concat_axis=0, tiled=True)  39.1 us
    all_to_all x1, waiting for transfers between devices, body(): lax.all_to_all(grad_out.reshape(shards, capacity, emb_width), 'table', sp...  37.9 us
    psum x1, blocking collectives, body(): row_sum, row_count = lax.psum((row_sum, row_count), 'dp')  24.3 us
    all_to_all x1, blocking collectives, body(): lax.all_to_all(outgoing, 'table', split_axis=0, concat_axis=0, tiled=True)  23.6 us
  transfers between devices with their start and end apart: 6, of which 6 were waited for; matrix products, arithmetic and copies ran while one was open for 7% of the time, Pallas kernels for 0%

commit v1 on v0

--- a/solution.py
+++ b/solution.py
@@ -61,27 +61,35 @@
         jnp.bfloat16
     )
     item_vec = jnp.dot(item_in, item_tower, preferred_element_type=jnp.float32).astype(jnp.bfloat16)
-    all_items = lax.all_gather(item_vec, "dp", axis=0, tiled=True)
+    n_dp = lax.axis_size("dp")
+    dp_index = lax.axis_index("dp")
+    table_index = lax.axis_index("table")
+    both = jnp.concatenate([query_vec, item_vec], axis=1)
+    both = lax.all_to_all(
+        jnp.broadcast_to(both[None], (n_dp,) + both.shape), "dp", 0, 0, tiled=True
+    )
+    all_queries = both[:, :, :out_width].reshape(n_dp * batch, out_width)
+    all_items = both[:, :, out_width:].reshape(n_dp * batch, out_width)
     scores = scale * lax.dot_general(
-        query_vec, all_items, (((1,), (1,)), ((), ())), preferred_element_type=jnp.float32
+        all_queries, all_items, (((1,), (1,)), ((), ())), preferred_element_type=jnp.float32
     )
     peak = jnp.max(scores, axis=1, keepdims=True)
     log_total = peak + jnp.log(jnp.sum(jnp.exp(scores - peak), axis=1, keepdims=True))
-    probs = jnp.exp(scores - log_total).astype(jnp.bfloat16)
+    own = dp_index * batch
+    row_scores = lax.dynamic_slice_in_dim(scores, own, batch, axis=0)
+    row_total = lax.dynamic_slice_in_dim(log_total, own, batch, axis=0)
+    col_scores = lax.dynamic_slice_in_dim(scores, own, batch, axis=1)
+    row_probs = jnp.exp(row_scores - row_total).astype(jnp.bfloat16)
+    col_probs = jnp.exp(col_scores - log_total).astype(jnp.bfloat16)
     query_grad = (
         scale
         * (
-            jnp.dot(probs, all_items, preferred_element_type=jnp.float32)
+            jnp.dot(row_probs, all_items, preferred_element_type=jnp.float32)
             - item_vec.astype(jnp.float32)
         )
     ).astype(jnp.bfloat16)
-    weighted = lax.psum_scatter(
-        lax.dot_general(
-            probs, query_vec, (((0,), (0,)), ((), ())), preferred_element_type=jnp.float32
-        ),
-        "dp",
-        scatter_dimension=0,
-        tiled=True,
+    weighted = lax.dot_general(
+        col_probs, all_queries, (((0,), (0,)), ((), ())), preferred_element_type=jnp.float32
     )
     item_grad = (scale * (weighted - query_vec.astype(jnp.float32))).astype(jnp.bfloat16)
     query_back = lax.dot_general(
@@ -112,7 +120,6 @@
             ),
         ]
     )
-    tower_sum = lax.psum(tower_part, ("dp", "table"))
     back_all = jnp.concatenate(
         [query_back.reshape(batch, feats, emb_width), item_back.reshape(batch, feats, emb_width)],
         axis=1,
@@ -140,12 +147,41 @@
         .at[slot_rows]
         .add((flat_in >= 0).astype(jnp.float32), mode="drop")
     )
-    row_sum, row_count = lax.psum((row_sum, row_count), "dp")
-    row_noise = hashed_noise(row_seeds, emb_width)
-    table_update = row_sum / clip_norm + NOISE_MULT * jnp.where(
-        row_count[:, None] > 0.0, row_noise, 0.0
+    shard_rows = rows_dev // n_dp
+    packed = jnp.concatenate(
+        [
+            row_sum.reshape(n_dp, shard_rows, emb_width),
+            jnp.broadcast_to(row_count.reshape(n_dp, 1, shard_rows, 1), (n_dp, 1, shard_rows, emb_width // shard_rows))
+            .reshape(n_dp, 1, emb_width),
+        ],
+        axis=1,
     )
-    tower_update = tower_sum / clip_norm + NOISE_MULT * hashed_noise(tower_seeds, out_width)
+    packed = jnp.sum(lax.all_to_all(packed, "dp", 0, 0, tiled=True), axis=0)
+    own_sum = packed[:shard_rows]
+    own_count = packed[shard_rows].reshape(shard_rows, emb_width // shard_rows)[:, 0]
+    own_seeds = lax.dynamic_slice_in_dim(row_seeds, dp_index * shard_rows, shard_rows)
+    own_update = own_sum / clip_norm + NOISE_MULT * jnp.where(
+        own_count[:, None] > 0.0, hashed_noise(own_seeds, emb_width), 0.0
+    )
+    table_update = lax.all_to_all(
+        jnp.broadcast_to(own_update[None], (n_dp,) + own_update.shape), "dp", 0, 0, tiled=True
+    ).reshape(rows_dev, emb_width)
+    tower_rows = 2 * hidden_width
+    dp_rows = tower_rows // n_dp
+    part = tower_part.reshape(n_dp, dp_rows, out_width)
+    part = jnp.sum(lax.all_to_all(part, "dp", 0, 0, tiled=True), axis=0)
+    own_rows = dp_rows // shards
+    part = part.reshape(shards, own_rows, out_width)
+    part = jnp.sum(lax.all_to_all(part, "table", 0, 0, tiled=True), axis=0)
+    first_row = dp_index * dp_rows + table_index * own_rows
+    tower_seed_rows = lax.dynamic_slice_in_dim(tower_seeds.reshape(tower_rows), first_row, own_rows)
+    part = part / clip_norm + NOISE_MULT * hashed_noise(tower_seed_rows, out_width)
+    part = lax.all_to_all(
+        jnp.broadcast_to(part[None], (shards,) + part.shape), "table", 0, 0, tiled=True
+    ).reshape(dp_rows, out_width)
+    tower_update = lax.all_to_all(
+        jnp.broadcast_to(part[None], (n_dp,) + part.shape), "dp", 0, 0, tiled=True
+    ).reshape(2, hidden_width, out_width)
     return (table_update, tower_update)
 
 

time: 750 us -> 501 us (0.67)
  waiting for transfers between devices: 523 us -> 264 us
  starting transfers between devices: 25.5 us -> 59.4 us
  blocking collectives: 47.9 us -> 23.6 us
  local copies, waits for them, and re-layouts: 54.5 us -> 70.1 us
  between operations: 14.2 us -> 1.17 us
    psum x2 -> x0, waiting for transfers between devices: 315 us -> none  [the longest x1 186 us: body(): tower_sum = lax.psum(tower_part, ('dp', 'table'))]
    all_to_all x0 -> x7, waiting for transfers between devices: none -> 188 us  [the longest x1 47.9 us: body(): lax.all_to_all(jnp.broadcast_to(part[None], (n_dp,) + part.shape), 'dp',...]
    reduce_scatter x1 -> x0, waiting for transfers between devices: 72.7 us -> none  [body(): lax.psum_scatter(lax.dot_general(probs, query_vec, (((0,), (0,)), ((), ()...]
    all_gather x1 -> x0, waiting for transfers between devices: 58 us -> none  [body(): all_items = lax.all_gather(item_vec, 'dp', axis=0, tiled=True)]
    all_to_all x0 -> x7, starting transfers between devices: none -> 45.8 us  [the longest x1 14 us: body(): lax.all_to_all(jnp.broadcast_to(part[None], (shards,) + part.shape), 'tab...]
    psum x1 -> x0, blocking collectives: 24.3 us -> none  [body(): row_sum, row_count = lax.psum((row_sum, row_count), 'dp')]
    all_to_all x1, starting transfers between devices: 21 us -> 9.39 us  [body(): lax.all_to_all(grad_out.reshape(shards, capacity, emb_width), 'table', sp...]
    add x2, other arithmetic: 8.86 us -> 0.26 us  [the longest x1 0.17 us: body(): own_sum / clip_norm]
  transfers between devices with their start and end apart: 6 -> 9, of which waited for: 6 -> 8; matrix products, arithmetic and copies ran while one was open for 7% -> 12% of each run, Pallas kernels for 0% -> 0%
where the time goes in v1:
time: 501 us; the launch traced here: 499 us
  waiting for transfers between devices  264 us (53%)
  local copies, waits for them, and re-layouts  70.1 us (14%)
  other arithmetic  65.3 us (13%)
  starting transfers between devices  59.4 us (12%)
  blocking collectives  23.6 us (5%)
  matrix products  15.1 us (3%)
    all_to_all x1, waiting for transfers between devices, body(): lax.all_to_all(jnp.broadcast_to(part[None], (n_dp,) + part.shape), 'dp',...  47.9 us
    all_to_all x1, waiting for transfers between devices, body(): lax.all_to_all(jnp.broadcast_to(both[None], (n_dp,) + both.shape), 'dp',...  46.3 us
    all_to_all x1, waiting for transfers between devices, body(): lax.all_to_all(fetched, 'table', split_axis=0, concat_axis=0, tiled=True)  39.2 us
    all_to_all x1, waiting for transfers between devices, body(): lax.all_to_all(grad_out.reshape(shards, capacity, emb_width), 'table', sp...  37 us
    all_to_all x1, waiting for transfers between devices, body(): part = jnp.sum(lax.all_to_all(part, 'dp', 0, 0, tiled=True), axis=0)  29.8 us
    all_to_all x1, waiting for transfers between devices, body(): packed = jnp.sum(lax.all_to_all(packed, 'dp', 0, 0, tiled=True), axis=0)  27.1 us
    all_to_all x1, waiting for transfers between devices, body(): lax.all_to_all(jnp.broadcast_to(own_update[None], (n_dp,) + own_update.sh...  26.4 us
    all_to_all x1, blocking collectives, body(): lax.all_to_all(outgoing, 'table', split_axis=0, concat_axis=0, tiled=True)  23.6 us
  transfers between devices with their start and end apart: 9, of which 8 were waited for; matrix products, arithmetic and copies ran while one was open for 12% of the time, Pallas kernels for 0%

profile of v1, /device:TPU:1, one launch (start us, length us, event | category | flops | bytes accessed | tf_op | source)
XLA Modules:
  0.0 498.6 jit_solution(10317909875429514415)
XLA Ops:
  0.7 1.0 copy.57
  2.0 11.8 %gather_fusion = s32[2048]{0:T(1024)S(1)} fusion(s32[32768]{0:T(1024)S(1)} %copy-done.1, s32[2048]{0:T(1024)S(1)} %broadcast_clamp_fusion.2), kind=kCustom, calls=%fused_computation | custom fusion | bytes 24576 | tf_op jit(solution)/shard_map/gather | solution.py:41
  13.9 9.1 %reduce-window.6 = s32[32,16,128]{2,1,0:T(8,128)S(1)} reduce-window(s32[32,16,128]{2,1,0:T(8,128)S(1)} %fusion.15, s32[]{:T(128)} %constant.42.clone.1), window={size=1x1x128 pad=0_0x0_0x127_0}, to_apply=%region_0.1 | reduce-window | flops 8323072 | bytes 524292 | tf_op jit(solution)/shard_map/reduce-window
  23.9 8.1 %scatter_custom_fusion = s32[3072]{0:T(1024)S(1)} fusion(s32[2048]{0:T(1024)S(1)} %bitcast.109, s32[2048]{0:T(1024)S(1)} %get-tuple-element.8, s32[]{:T(128)} %constant.41.clone.1), kind=kCustom, calls=%fused_computation.107 | custom fusion | bytes 12292 | tf_op jit(solution)/shard_map/scatter | solution.py:47
  32.0 23.6 %all_to_all.57 = s32[32,1,96]{2,1,0:T(1,128)S(1)} all-to-all(s32[32,1,96]{2,1,0:T(1,128)S(1)} %all_to_all.35), channel_id=1, replica_groups=mesh['dp'=16,'table'=32] {'table'}, dimensions={0} | all-to-all | bytes 24576 | tf_op jit(solution)/shard_map/all_to_all | solution.py:49
  56.3 11.1 %gather_fusion.1 = bf16[3072,256]{1,0:T(8,128)(2,1)S(1)} fusion(bf16[1024,256]{1,0:T(8,128)(2,1)S(1)} %copy-done, s32[3072]{0:T(1024)S(1)} %broadcast_clamp_fusion), kind=kCustom, calls=%fused_computation.1 | custom fusion | bytes 3158016 | tf_op jit(solution)/shard_map/gather | solution.py:51
  67.4 1.5 broadcast_select_fusion
  68.8 4.2 all-to-all-start.1
  73.1 39.2 %all-to-all-done.1 = bf16[32,96,256]{2,1,0:T(8,128)(2,1)S(1)} async-done(((bf16[32,96,256]{2,1,0:T(8,128)(2,1)}), bf16[32,96,256]{2,1,0:T(8,128)(2,1)S(1)}, u32[]{:S(2)}, u32[]{:S(2)}) %all-to-all-start.1) | async-done | bytes 1572896 | tf_op jit(solution)/shard_map/all_to_all | solution.py:53
  112.3 7.5 %gather_fusion.2 = bf16[2048,256]{1,0:T(8,128)(2,1)S(1)} fusion(bf16[3072,256]{1,0:T(8,128)(2,1)S(1)} %bitcast.86, s32[2048]{0:T(1024)S(1)} %broadcast_clamp_fusion.1), kind=kCustom, calls=%fused_computation.2 | custom fusion | bytes 2105344 | tf_op jit(solution)/shard_map/gather | solution.py:55
  120.2 2.8 reduce_sum.115
  124.3 1.5 broadcast_in_dim.64
  125.9 7.0 %all-to-all-start.2 = ((bf16[16,128,512]{2,1,0:T(8,128)(2,1)}), bf16[16,128,512]{2,1,0:T(8,128)(2,1)S(1)}, u32[]{:S(2)}, u32[]{:S(2)}) async-start(bf16[16,128,512]{2,1,0:T(8,128)(2,1)} %broadcast_in_dim.64), calls=%async_computation.2 | async-start | bytes 4194304 | tf_op jit(solution)/shard_map/all_to_all | solution.py:68
  132.8 1.7 multiply_reduce_fusion.2
  134.5 46.3 %all-to-all-done.2 = bf16[16,128,512]{2,1,0:T(8,128)(2,1)S(1)} async-done(((bf16[16,128,512]{2,1,0:T(8,128)(2,1)}), bf16[16,128,512]{2,1,0:T(8,128)(2,1)S(1)}, u32[]{:S(2)}, u32[]{:S(2)}) %all-to-all-start.2) | async-done | bytes 2097184 | tf_op jit(solution)/shard_map/all_to_all | solution.py:68
  181.1 8.1 %fusion.56 = (f32[2048]{0:T(1024)S(1)}, f32[2048,2048]{0,1:T(8,128)}) fusion(bf16[2048,256]{1,0:T(8,128)(2,1)S(1)} %bitcast.87, bf16[2048,256]{1,0:T(8,128)(2,1)S(1)} %bitcast.89), kind=kOutput, calls=%fused_computation.131 | convolution fusion | flops 2155870208 | bytes 18882560 | tf_op jit(solution)/shard_map/dot_general | solution.py:73
  189.2 8.1 %exponential_reduce_fusion = f32[2048]{0:T(1024)S(1)} fusion(f32[2048,2048]{0,1:T(8,128)} %get-tuple-element.11, f32[2048]{0:T(1024)S(1)} %get-tuple-element.10), kind=kLoop, calls=%fused_computation.7 | loop fusion | flops 8386560 | bytes 16793600 | tf_op jit(solution)/shard_map/reduce_sum | solution.py:77
  197.2 1.7 fusion.18
  199.1 1.8 fusion.16
  200.9 1.1 multiply_reduce_fusion
  202.0 1.1 multiply_reduce_fusion.1
  203.8 1.5 pad_maximum_fusion
  205.3 6.3 %all-to-all-start.6 = ((f32[16,128,256]{2,1,0:T(8,128)}), f32[16,128,256]{2,1,0:T(8,128)S(1)}, u32[]{:S(2)}, u32[]{:S(2)}) async-start(f32[16,128,256]{2,1,0:T(8,128)} %bitcast.91), calls=%async_computation.6 | async-start | bytes 4194304 | tf_op jit(solution)/shard_map/all_to_all | solution.py:172
  211.6 1.0 concatenate.19
  212.6 1.3 concatenate.18
  213.9 1.3 fusion.6
  215.2 1.7 broadcast_in_dim.65
  216.9 2.2 reshape.499
  219.1 11.0 %scatter_custom_fusion.1 = bf16[3072,256]{1,0:T(8,128)(2,1)} fusion(s32[2048]{0:T(1024)} %bitcast.111, bf16[2048,256]{1,0:T(8,128)(2,1)} %reshape.499, bf16[]{:T(256)} %constant.50.clone.1), kind=kCustom, calls=%fused_computation.28 | custom fusion | bytes 1573376 | tf_op jit(solution)/shard_map/scatter | solution.py:130
  230.1 29.8 %all-to-all-done.6 = f32[16,128,256]{2,1,0:T(8,128)S(1)} async-done(((f32[16,128,256]{2,1,0:T(8,128)}), f32[16,128,256]{2,1,0:T(8,128)S(1)}, u32[]{:S(2)}, u32[]{:S(2)}) %all-to-all-start.6) | async-done | bytes 2097184 | tf_op jit(solution)/shard_map/all_to_all | solution.py:172
  259.8 9.4 %all-to-all-start.3 = ((bf16[32,96,256]{2,1,0:T(8,128)(2,1)}), bf16[32,96,256]{2,1,0:T(8,128)(2,1)}, u32[]{:S(2)}, u32[]{:S(2)}) async-start(bf16[32,96,256]{2,1,0:T(8,128)(2,1)} %bitcast.93), calls=%async_computation.3 | async-start | bytes 3145728 | tf_op jit(solution)/shard_map/all_to_all | solution.py:131
  271.4 37.0 %all-to-all-done.3 = bf16[32,96,256]{2,1,0:T(8,128)(2,1)} async-done(((bf16[32,96,256]{2,1,0:T(8,128)(2,1)}), bf16[32,96,256]{2,1,0:T(8,128)(2,1)}, u32[]{:S(2)}, u32[]{:S(2)}) %all-to-all-start.3) | async-done | bytes 1572896 | tf_op jit(solution)/shard_map/all_to_all | solution.py:131
  308.4 6.1 %all-to-all-start.7 = ((f32[32,4,256]{2,1,0:T(4,128)}), f32[32,4,256]{2,1,0:T(4,128)S(1)}, u32[]{:S(2)}, u32[]{:S(2)}) async-start(f32[32,4,256]{2,1,0:T(4,128)} %reshape.458), calls=%async_computation.7 | async-start | bytes 262144 | tf_op jit(solution)/shard_map/all_to_all | solution.py:175
  314.5 19.6 %scatter_custom_fusion.3 = f32[1024]{0:T(1024)S(1)} fusion(s32[3072]{0:T(1024)S(1)} %bitcast.114, f32[3072]{0:T(1024)S(1)} %reshape.515, f32[]{:T(128)} %constant.40.clone.1), kind=kCustom, calls=%fused_computation.120 | custom fusion | flops 3072 | bytes 4100 | tf_op jit(solution)/shard_map/scatter-add | solution.py:148
  334.4 16.2 %scatter_custom_fusion.2 = f32[1024,256]{1,0:T(8,128)S(1)} fusion(s32[3072]{0:T(1024)S(1)} %bitcast.115, bf16[3072,256]{1,0:T(8,128)(2,1)} %bitcast.27, f32[]{:T(128)} %constant.40.clone.1), kind=kCustom, calls=%fused_computation.9 | custom fusion | flops 1572864 | bytes 2621444 | tf_op jit(solution)/shard_map/scatter-add | solution.py:143
  350.6 1.1 pad_maximum_fusion.1
  351.8 3.7 all-to-all-start.4
  356.5 27.1 %all-to-all-done.4 = f32[16,65,256]{2,1,0:T(8,128)S(1)} async-done(((f32[16,65,256]{2,1,0:T(8,128)}), f32[16,65,256]{2,1,0:T(8,128)S(1)}, u32[]{:S(2)}, u32[]{:S(2)}) %all-to-all-start.4) | async-done | bytes 1064992 | tf_op jit(solution)/shard_map/all_to_all | solution.py:159
  384.3 14.0 %all-to-all-start.8 = ((f32[32,4,256]{2,1,0:T(4,128)}), f32[32,4,256]{2,1,0:T(4,128)S(1)}, u32[]{:S(2)}, u32[]{:S(2)}) async-start(f32[32,4,256]{2,1,0:T(4,128)} %broadcast_in_dim.123), calls=%async_computation.8 | async-start | bytes 262144 | tf_op jit(solution)/shard_map/all_to_all | solution.py:179
  398.8 10.3 %all-to-all-done.8 = f32[32,4,256]{2,1,0:T(4,128)S(1)} async-done(((f32[32,4,256]{2,1,0:T(4,128)}), f32[32,4,256]{2,1,0:T(4,128)S(1)}, u32[]{:S(2)}, u32[]{:S(2)}) %all-to-all-start.8) | async-done | bytes 131104 | tf_op jit(solution)/shard_map/all_to_all | solution.py:179
  409.1 1.1 broadcast_in_dim.122
  410.1 3.7 all-to-all-start.5
  413.9 26.4 %all-to-all-done.5 = f32[16,64,256]{2,1,0:T(8,128)S(1)} async-done(((f32[16,64,256]{2,1,0:T(8,128)}), f32[16,64,256]{2,1,0:T(8,128)S(1)}, u32[]{:S(2)}, u32[]{:S(2)}) %all-to-all-start.5) | async-done | bytes 1048608 | tf_op jit(solution)/shard_map/all_to_all | solution.py:166
  440.3 1.7 broadcast_in_dim.125
  441.9 5.1 %all-to-all-start.9 = ((f32[16,128,256]{2,1,0:T(8,128)}), f32[16,128,256]{2,1,0:T(8,128)S(1)}, u32[]{:S(2)}, u32[]{:S(2)}) async-start(f32[16,128,256]{2,1,0:T(8,128)} %broadcast_in_dim.125), calls=%async_computation.9 | async-start | bytes 4194304 | tf_op jit(solution)/shard_map/all_to_all | solution.py:182
  447.1 47.9 %all-to-all-done.9 = f32[16,128,256]{2,1,0:T(8,128)S(1)} async-done(((f32[16,128,256]{2,1,0:T(8,128)}), f32[16,128,256]{2,1,0:T(8,128)S(1)}, u32[]{:S(2)}, u32[]{:S(2)}) %all-to-all-start.9) | async-done | bytes 2097184 | tf_op jit(solution)/shard_map/all_to_all | solution.py:182
  495.0 2.3 copy.87
  497.2 1.3 copy.88
  (84 shorter events, 9.4 us)
Async XLA Ops:
  0.6 55.7 %copy-start = (bf16[1024,256]{1,0:T(8,128)(2,1)S(1)}, bf16[1024,256]{1,0:T(8,128)(2,1)}, u32[]{:S(2)}) copy-start(bf16[1024,256]{1,0:T(8,128)(2,1)} %param.7) | copy-start | bytes 1572868
  0.6 1.4 copy-start.1
  23.9 49.2 %copy-start.10 = (s32[2048,1]{0,1:T(1,128)}, s32[2048,1]{0,1:T(1,128)S(1)}, u32[]{:S(2)}) copy-start(s32[2048,1]{0,1:T(1,128)S(1)} %compare_select_fusion.2) | copy-start | bytes 24580
  68.8 43.4 %all-to-all-start.1 = ((bf16[32,96,256]{2,1,0:T(8,128)(2,1)}), bf16[32,96,256]{2,1,0:T(8,128)(2,1)S(1)}, u32[]{:S(2)}, u32[]{:S(2)}) async-start(bf16[32,96,256]{2,1,0:T(8,128)(2,1)} %broadcast_select_fusion), calls=%async_computation.1 | async-start | bytes 3145728 | tf_op jit(solution)/shard_map/all_to_all | solution.py:53
  120.2 3.5 copy-start.4
  120.2 3.8 copy-start.6
  123.3 2.6 copy-start.3
  125.9 54.9 %all-to-all-start.2 = ((bf16[16,128,512]{2,1,0:T(8,128)(2,1)}), bf16[16,128,512]{2,1,0:T(8,128)(2,1)S(1)}, u32[]{:S(2)}, u32[]{:S(2)}) async-start(bf16[16,128,512]{2,1,0:T(8,128)(2,1)} %broadcast_in_dim.64), calls=%async_computation.2 | async-start | bytes 4194304 | tf_op jit(solution)/shard_map/all_to_all | solution.py:68
  197.2 3.6 copy-start.5
  199.0 3.0 copy-start.7
  199.1 4.0 copy-start.12
  199.1 4.0 copy-start.13
  205.3 6.3 %copy-start.8 = (f32[128,1024]{1,0:T(8,128)S(1)}, f32[128,1024]{1,0:T(8,128)}, u32[]{:S(2)}) copy-start(f32[128,1024]{1,0:T(8,128)} %get-tuple-element.13) | copy-start | bytes 1572868
  205.3 54.6 %all-to-all-start.6 = ((f32[16,128,256]{2,1,0:T(8,128)}), f32[16,128,256]{2,1,0:T(8,128)S(1)}, u32[]{:S(2)}, u32[]{:S(2)}) async-start(f32[16,128,256]{2,1,0:T(8,128)} %bitcast.91), calls=%async_computation.6 | async-start | bytes 4194304 | tf_op jit(solution)/shard_map/all_to_all | solution.py:172
  259.8 48.5 %all-to-all-start.3 = ((bf16[32,96,256]{2,1,0:T(8,128)(2,1)}), bf16[32,96,256]{2,1,0:T(8,128)(2,1)}, u32[]{:S(2)}, u32[]{:S(2)}) async-start(bf16[32,96,256]{2,1,0:T(8,128)(2,1)} %bitcast.93), calls=%async_computation.3 | async-start | bytes 3145728 | tf_op jit(solution)/shard_map/all_to_all | solution.py:131
  269.2 45.2 %copy-start.9 = (f32[32,1,96]{2,0,1:T(8,128)S(1)}, f32[32,1,96]{2,0,1:T(8,128)}, u32[]{:S(2)}) copy-start(f32[32,1,96]{2,0,1:T(8,128)} %get-tuple-element.2) | copy-start | bytes 36868
  308.4 43.4 %all-to-all-start.7 = ((f32[32,4,256]{2,1,0:T(4,128)}), f32[32,4,256]{2,1,0:T(4,128)S(1)}, u32[]{:S(2)}, u32[]{:S(2)}) async-start(f32[32,4,256]{2,1,0:T(4,128)} %reshape.458), calls=%async_computation.7 | async-start | bytes 262144 | tf_op jit(solution)/shard_map/all_to_all | solution.py:175
  350.6 4.9 copy-start.11
  351.8 31.8 %all-to-all-start.4 = ((f32[16,65,256]{2,1,0:T(8,128)}), f32[16,65,256]{2,1,0:T(8,128)S(1)}, u32[]{:S(2)}, u32[]{:S(2)}) async-start(f32[16,65,256]{2,1,0:T(8,128)} %pad_maximum_fusion.1), calls=%async_computation.4 | async-start | bytes 2359296 | tf_op jit(solution)/shard_map/all_to_all | solution.py:159
  384.3 24.8 %all-to-all-start.8 = ((f32[32,4,256]{2,1,0:T(4,128)}), f32[32,4,256]{2,1,0:T(4,128)S(1)}, u32[]{:S(2)}, u32[]{:S(2)}) async-start(f32[32,4,256]{2,1,0:T(4,128)} %broadcast_in_dim.123), calls=%async_computation.8 | async-start | bytes 262144 | tf_op jit(solution)/shard_map/all_to_all | solution.py:179
  410.1 30.1 %all-to-all-start.5 = ((f32[16,64,256]{2,1,0:T(8,128)}), f32[16,64,256]{2,1,0:T(8,128)S(1)}, u32[]{:S(2)}, u32[]{:S(2)}) async-start(f32[16,64,256]{2,1,0:T(8,128)} %broadcast_in_dim.122), calls=%async_computation.5 | async-start | bytes 2097152 | tf_op jit(solution)/shard_map/all_to_all | solution.py:166
  440.3 1.7 copy-start.2
  441.9 53.1 %all-to-all-start.9 = ((f32[16,128,256]{2,1,0:T(8,128)}), f32[16,128,256]{2,1,0:T(8,128)S(1)}, u32[]{:S(2)}, u32[]{:S(2)}) async-start(f32[16,128,256]{2,1,0:T(8,128)} %broadcast_in_dim.125), calls=%async_computation.9 | async-start | bytes 4194304 | tf_op jit(solution)/shard_map/all_to_all | solution.py:182

commit v2 on v1

--- a/solution.py
+++ b/solution.py
@@ -41,20 +41,36 @@
     positions = row_owner[lookup_ids.reshape(-1)]
     owners = positions // rows_dev
     local_rows = positions - owners * rows_dev
-    one_hot = (owners[:, None] == jnp.arange(shards, dtype=jnp.int32)[None, :]).astype(jnp.int32)
-    ranks = jnp.sum((jnp.cumsum(one_hot, axis=0) - one_hot) * one_hot, axis=1)
+    one_hot = owners[:, None] == jnp.arange(shards, dtype=jnp.int32)[None, :]
+    order = jnp.arange(requests, dtype=jnp.int32)
+    earlier = (order[None, :] < order[:, None]).astype(jnp.bfloat16)
+    before = jnp.dot(earlier, one_hot.astype(jnp.bfloat16), preferred_element_type=jnp.float32)
+    ranks = jnp.sum(jnp.where(one_hot, before, 0.0), axis=1).astype(jnp.int32)
     targets = owners * capacity + ranks
-    outgoing = jnp.full((shards * capacity,), -1, jnp.int32).at[targets].set(local_rows)
+    slots_all = jnp.arange(shards * capacity, dtype=jnp.int32)
+    slot_match = targets[:, None] == slots_all[None, :]
+    outgoing = jnp.max(jnp.where(slot_match, local_rows[:, None], -1), axis=0)
     outgoing = outgoing.reshape(shards, capacity)
     incoming = lax.all_to_all(outgoing, "table", split_axis=0, concat_axis=0, tiled=True)
-    valid = incoming >= 0
-    fetched = id_table[jnp.where(valid, incoming, 0)]
-    fetched = jnp.where(valid[:, :, None], fetched, jnp.zeros((), jnp.bfloat16))
-    returned = lax.all_to_all(fetched, "table", split_axis=0, concat_axis=0, tiled=True)
-    returned, incoming = (returned, incoming)
-    looked = returned.reshape(shards * capacity, emb_width)[targets]
-    pooled = jnp.sum(looked.reshape(batch, slots, bags, emb_width).astype(jnp.float32), axis=2)
-    pooled = pooled.astype(jnp.bfloat16)
+    flat_in = incoming.reshape(-1)
+    row_match = (flat_in[:, None] == jnp.arange(rows_dev, dtype=jnp.int32)[None, :]).astype(
+        jnp.bfloat16
+    )
+    fetched = jnp.dot(row_match, id_table, preferred_element_type=jnp.float32).astype(jnp.bfloat16)
+    returned = lax.all_to_all(
+        fetched.reshape(shards, capacity, emb_width), "table", split_axis=0, concat_axis=0, tiled=True
+    )
+    pair_targets = targets.reshape(batch * slots, bags)
+    pool_match = pair_targets[:, 0:1] == slots_all[None, :]
+    for bag in range(1, bags):
+        pool_match = pool_match | (pair_targets[:, bag : bag + 1] == slots_all[None, :])
+    pool_match = pool_match.astype(jnp.bfloat16)
+    pooled = jnp.dot(
+        pool_match,
+        returned.reshape(shards * capacity, emb_width),
+        preferred_element_type=jnp.float32,
+    )
+    pooled = pooled.astype(jnp.bfloat16).reshape(batch, slots, emb_width)
     query_in = pooled[:, :feats].reshape(batch, hidden_width)
     item_in = pooled[:, feats:].reshape(batch, hidden_width)
     query_vec = jnp.dot(query_in, query_tower, preferred_element_type=jnp.float32).astype(
@@ -125,9 +141,12 @@
         axis=1,
     )
     lookup_grad = (factor[:, None, None] * back_all).astype(jnp.bfloat16)
-    spread = jnp.broadcast_to(lookup_grad[:, :, None, :], (batch, slots, bags, emb_width))
-    spread = spread.reshape(requests, emb_width)
-    grad_out = jnp.zeros((shards * capacity, emb_width), jnp.bfloat16).at[targets].set(spread)
+    grad_out = lax.dot_general(
+        pool_match,
+        lookup_grad.reshape(batch * slots, emb_width),
+        (((0,), (0,)), ((), ())),
+        preferred_element_type=jnp.float32,
+    ).astype(jnp.bfloat16)
     grad_in = lax.all_to_all(
         grad_out.reshape(shards, capacity, emb_width),
         "table",
@@ -135,18 +154,13 @@
         concat_axis=0,
         tiled=True,
     )
-    flat_in = incoming.reshape(-1)
-    slot_rows = jnp.where(flat_in >= 0, flat_in, rows_dev)
-    row_sum = (
-        jnp.zeros((rows_dev, emb_width), jnp.float32)
-        .at[slot_rows]
-        .add(grad_in.reshape(shards * capacity, emb_width).astype(jnp.float32), mode="drop")
-    )
-    row_count = (
-        jnp.zeros((rows_dev,), jnp.float32)
-        .at[slot_rows]
-        .add((flat_in >= 0).astype(jnp.float32), mode="drop")
-    )
+    row_sum = lax.dot_general(
+        row_match,
+        grad_in.reshape(shards * capacity, emb_width),
+        (((0,), (0,)), ((), ())),
+        preferred_element_type=jnp.float32,
+    )
+    row_count = jnp.sum(row_match.astype(jnp.float32), axis=0)
     shard_rows = rows_dev // n_dp
     packed = jnp.concatenate(
         [

time: 501 us -> 441 us (0.88)
  other arithmetic: 65.3 us -> 22.1 us
  local copies, waits for them, and re-layouts: 70.1 us -> 29.6 us
  matrix products: 15.1 us -> 33.2 us
  waiting for transfers between devices: 264 us -> 277 us
  starting transfers between devices: 59.4 us -> 52 us
    scatter-add x2 -> x0, other arithmetic: 35.8 us -> none  [the longest x1 19.6 us: body(): row_count = jnp.zeros((rows_dev,), jnp.float32).at[slot_rows].add((flat_i...]
    scatter x2 -> x0, local copies, waits for them, and re-layouts: 19 us -> none  [the longest x1 11 us: body(): jnp.zeros((shards * capacity, emb_width), jnp.bfloat16).at[targets]]
    gather x2 -> x0, local copies, waits for them, and re-layouts: 18.5 us -> none  [the longest x1 11.1 us: body(): fetched = id_table[jnp.where(valid, incoming, 0)]]
    dot_general x0 -> x5, matrix products: none -> 18.2 us  [the longest x1 6.47 us: body(): lax.dot_general(pool_match, lookup_grad.reshape(batch * slots, emb_width)...]
    another operation x3 -> x0, other arithmetic: 9.41 us -> none
    all_to_all x1, waiting for transfers between devices: 29.8 us -> 38.5 us  [body(): part = jnp.sum(lax.all_to_all(part, 'dp', 0, 0, tiled=True), axis=0)]
    all_to_all x1, starting transfers between devices: 14 us -> 7.2 us  [body(): lax.all_to_all(jnp.broadcast_to(part[None], (shards,) + part.shape), 'tab...]
    all_to_all x1, waiting for transfers between devices: 0.01 us -> 6.35 us  [body(): part = jnp.sum(lax.all_to_all(part, 'table', 0, 0, tiled=True), axis=0)]
  transfers between devices with their start and end apart: 9 -> 9, of which waited for: 8 -> 9; matrix products, arithmetic and copies ran while one was open for 12% -> 5% of each run, Pallas kernels for 0% -> 0%
where the time goes in v2:
time: 441 us; the launch traced here: 439 us
  waiting for transfers between devices  277 us (63%)
  starting transfers between devices  52 us (12%)
  matrix products  33.2 us (8%)
  local copies, waits for them, and re-layouts  29.6 us (7%)
  blocking collectives  23.6 us (5%)
  other arithmetic  22.1 us (5%)
    all_to_all x1, waiting for transfers between devices, body(): lax.all_to_all(jnp.broadcast_to(part[None], (n_dp,) + part.shape), 'dp',...  47.9 us
    all_to_all x1, waiting for transfers between devices, body(): lax.all_to_all(jnp.broadcast_to(both[None], (n_dp,) + both.shape), 'dp',...  45.6 us
    all_to_all x1, waiting for transfers between devices, body(): part = jnp.sum(lax.all_to_all(part, 'dp', 0, 0, tiled=True), axis=0)  38.5 us
    all_to_all x1, waiting for transfers between devices, body(): lax.all_to_all(fetched.reshape(shards, capacity, emb_width), 'table', spl...  37.4 us
    all_to_all x1, waiting for transfers between devices, body(): lax.all_to_all(grad_out.reshape(shards, capacity, emb_width), 'table', sp...  36.7 us
    all_to_all x1, waiting for transfers between devices, body(): packed = jnp.sum(lax.all_to_all(packed, 'dp', 0, 0, tiled=True), axis=0)  27.6 us
    all_to_all x1, waiting for transfers between devices, body(): lax.all_to_all(jnp.broadcast_to(own_update[None], (n_dp,) + own_update.sh...  26.9 us
    all_to_all x1, blocking collectives, body(): lax.all_to_all(outgoing, 'table', split_axis=0, concat_axis=0, tiled=True)  23.6 us
  transfers between devices with their start and end apart: 9, of which 9 were waited for; matrix products, arithmetic and copies ran while one was open for 5% of the time, Pallas kernels for 0%

profile of v2, /device:TPU:1, one launch (start us, length us, event | category | flops | bytes accessed | tf_op | source)
XLA Modules:
  0.0 439.0 jit_solution(10548276898777774445)
XLA Ops:
  0.7 1.0 copy.17
  2.0 11.8 %gather_fusion = s32[2048]{0:T(1024)S(1)} fusion(s32[32768]{0:T(1024)S(1)} %copy-done.1, s32[2048]{0:T(1024)S(1)} %broadcast_clamp_fusion), kind=kCustom, calls=%fused_computation | custom fusion | bytes 24576 | tf_op jit(solution)/shard_map/gather | solution.py:41
  13.8 1.5 fusion.30
  15.4 5.9 %select_reduce_fusion = s32[3072]{0:T(1024)S(1)} fusion(s32[2048]{0:T(1024)S(1)} %get-tuple-element.11, s32[2048]{0:T(1024)S(1)} %get-tuple-element.10), kind=kLoop, calls=%fused_computation.1 | loop fusion | flops 18871296 | bytes 28672 | tf_op jit(solution)/shard_map/reduce_max | solution.py:52
  21.3 23.6 %all_to_all.54 = s32[32,1,96]{2,1,0:T(1,128)S(1)} all-to-all(s32[32,1,96]{2,1,0:T(1,128)S(1)} %all_to_all.33), channel_id=1, replica_groups=mesh['dp'=16,'table'=32] {'table'}, dimensions={0} | all-to-all | bytes 24576 | tf_op jit(solution)/shard_map/all_to_all | solution.py:54
  45.5 0.7 reduce.15
  46.2 3.6 fusion.20
  49.9 4.2 all-to-all-start.1
  55.9 37.4 %all-to-all-done.1 = bf16[32,96,256]{2,1,0:T(8,128)(2,1)S(1)} async-done(((bf16[32,96,256]{2,1,0:T(8,128)(2,1)}), bf16[32,96,256]{2,1,0:T(8,128)(2,1)S(1)}, u32[]{:S(2)}, u32[]{:S(2)}) %all-to-all-start.1) | async-done | bytes 1572896 | tf_op jit(solution)/shard_map/all_to_all | solution.py:60
  93.3 3.3 fusion.25
  97.4 1.5 broadcast_in_dim.49
  98.9 7.0 %all-to-all-start.2 = ((bf16[16,128,512]{2,1,0:T(8,128)(2,1)}), bf16[16,128,512]{2,1,0:T(8,128)(2,1)S(1)}, u32[]{:S(2)}, u32[]{:S(2)}) async-start(bf16[16,128,512]{2,1,0:T(8,128)(2,1)} %broadcast_in_dim.49), calls=%async_computation.2 | async-start | bytes 4194304 | tf_op jit(solution)/shard_map/all_to_all | solution.py:84
  105.9 2.4 multiply_reduce_fusion.3
  108.3 45.6 %all-to-all-done.2 = bf16[16,128,512]{2,1,0:T(8,128)(2,1)S(1)} async-done(((bf16[16,128,512]{2,1,0:T(8,128)(2,1)}), bf16[16,128,512]{2,1,0:T(8,128)(2,1)S(1)}, u32[]{:S(2)}, u32[]{:S(2)}) %all-to-all-start.2) | async-done | bytes 2097184 | tf_op jit(solution)/shard_map/all_to_all | solution.py:84
  154.1 8.1 %fusion.77 = (f32[2048]{0:T(1024)S(1)}, f32[2048,2048]{0,1:T(8,128)}) fusion(bf16[2048,256]{1,0:T(8,128)(2,1)S(1)} %bitcast.51, bf16[2048,256]{1,0:T(8,128)(2,1)S(1)} %bitcast.53), kind=kOutput, calls=%fused_computation.131 | convolution fusion | flops 2155870208 | bytes 18882560 | tf_op jit(solution)/shard_map/dot_general | solution.py:89
  162.2 8.1 %exponential_reduce_fusion = f32[2048]{0:T(1024)S(1)} fusion(f32[2048,2048]{0,1:T(8,128)} %get-tuple-element.13, f32[2048]{0:T(1024)S(1)} %get-tuple-element.12), kind=kLoop, calls=%fused_computation.3 | loop fusion | flops 8386560 | bytes 16793600 | tf_op jit(solution)/shard_map/reduce_sum | solution.py:93
  170.3 1.8 fusion.45
  172.2 1.7 fusion.43
  173.9 1.1 multiply_reduce_fusion
  175.0 1.1 multiply_reduce_fusion.1
  176.9 1.5 pad_maximum_fusion
  178.3 6.3 %all-to-all-start.6 = ((f32[16,128,256]{2,1,0:T(8,128)}), f32[16,128,256]{2,1,0:T(8,128)S(1)}, u32[]{:S(2)}, u32[]{:S(2)}) async-start(f32[16,128,256]{2,1,0:T(8,128)} %bitcast.55), calls=%async_computation.6 | async-start | bytes 4194304 | tf_op jit(solution)/shard_map/all_to_all | solution.py:186
  184.6 2.1 reshape.335
  186.9 1.0 reshape.334
  187.9 6.5 %fusion.17 = bf16[3072,256]{1,0:T(8,128)(2,1)} fusion(s32[1024]{0:T(1024)S(1)} %get-tuple-element.5, s32[1024]{0:T(1024)S(1)} %get-tuple-element.4, f32[128,4,256]{2,1,0:T(4,128)} %reshape.335, f32[128,4,256]{2,1,0:T(4,128)} %reshape.334, f32[1024]{0:T(1024)S(1)} %mul.205), kind=kOutput, calls=%fused_computation.25 | convolution fusion | flops 1621622784 | bytes 2633728 | tf_op jit(solution)/shard_map/dot_general | solution.py:144
  194.4 38.5 %all-to-all-done.6 = f32[16,128,256]{2,1,0:T(8,128)S(1)} async-done(((f32[16,128,256]{2,1,0:T(8,128)}), f32[16,128,256]{2,1,0:T(8,128)S(1)}, u32[]{:S(2)}, u32[]{:S(2)}) %all-to-all-start.6) | async-done | bytes 2097184 | tf_op jit(solution)/shard_map/all_to_all | solution.py:186
  232.9 9.3 %all-to-all-start.3 = ((bf16[32,96,256]{2,1,0:T(8,128)(2,1)}), bf16[32,96,256]{2,1,0:T(8,128)(2,1)}, u32[]{:S(2)}, u32[]{:S(2)}) async-start(bf16[32,96,256]{2,1,0:T(8,128)(2,1)} %bitcast.62), calls=%async_computation.3 | async-start | bytes 3145728 | tf_op jit(solution)/shard_map/all_to_all | solution.py:150
  242.3 1.5 convert_reduce_fusion
  244.1 0.7 reshape.340
  244.8 36.7 %all-to-all-done.3 = bf16[32,96,256]{2,1,0:T(8,128)(2,1)} async-done(((bf16[32,96,256]{2,1,0:T(8,128)(2,1)}), bf16[32,96,256]{2,1,0:T(8,128)(2,1)}, u32[]{:S(2)}, u32[]{:S(2)}) %all-to-all-start.3) | async-done | bytes 1572896 | tf_op jit(solution)/shard_map/all_to_all | solution.py:150
  281.5 6.0 %all-to-all-start.7 = ((f32[32,4,256]{2,1,0:T(4,128)}), f32[32,4,256]{2,1,0:T(4,128)S(1)}, u32[]{:S(2)}, u32[]{:S(2)}) async-start(f32[32,4,256]{2,1,0:T(4,128)} %reshape.340), calls=%async_computation.7 | async-start | bytes 262144 | tf_op jit(solution)/shard_map/all_to_all | solution.py:189
  287.5 3.3 fusion.4
  290.8 1.1 pad_maximum_fusion.1
  291.9 6.4 %all-to-all-done.7 = f32[32,4,256]{2,1,0:T(4,128)S(1)} async-done(((f32[32,4,256]{2,1,0:T(4,128)}), f32[32,4,256]{2,1,0:T(4,128)S(1)}, u32[]{:S(2)}, u32[]{:S(2)}) %all-to-all-start.7) | async-done | bytes 131104 | tf_op jit(solution)/shard_map/all_to_all | solution.py:189
  298.2 3.7 all-to-all-start.4
  302.0 0.8 dynamic_slice.15
  303.0 27.6 %all-to-all-done.4 = f32[16,65,256]{2,1,0:T(8,128)S(1)} async-done(((f32[16,65,256]{2,1,0:T(8,128)}), f32[16,65,256]{2,1,0:T(8,128)S(1)}, u32[]{:S(2)}, u32[]{:S(2)}) %all-to-all-start.4) | async-done | bytes 1064992 | tf_op jit(solution)/shard_map/all_to_all | solution.py:173
  330.6 0.7 broadcast_in_dim.57
  331.2 7.2 %all-to-all-start.8 = ((f32[32,4,256]{2,1,0:T(4,128)}), f32[32,4,256]{2,1,0:T(4,128)S(1)}, u32[]{:S(2)}, u32[]{:S(2)}) async-start(f32[32,4,256]{2,1,0:T(4,128)} %broadcast_in_dim.57), calls=%async_computation.8 | async-start | bytes 262144 | tf_op jit(solution)/shard_map/all_to_all | solution.py:193
  339.0 10.5 %all-to-all-done.8 = f32[32,4,256]{2,1,0:T(4,128)S(1)} async-done(((f32[32,4,256]{2,1,0:T(4,128)}), f32[32,4,256]{2,1,0:T(4,128)S(1)}, u32[]{:S(2)}, u32[]{:S(2)}) %all-to-all-start.8) | async-done | bytes 131104 | tf_op jit(solution)/shard_map/all_to_all | solution.py:193
  349.4 1.1 broadcast_in_dim.56
  350.5 3.7 all-to-all-start.5
  354.2 26.9 %all-to-all-done.5 = f32[16,64,256]{2,1,0:T(8,128)S(1)} async-done(((f32[16,64,256]{2,1,0:T(8,128)}), f32[16,64,256]{2,1,0:T(8,128)S(1)}, u32[]{:S(2)}, u32[]{:S(2)}) %all-to-all-start.5) | async-done | bytes 1048608 | tf_op jit(solution)/shard_map/all_to_all | solution.py:180
  381.1 1.7 broadcast_in_dim.59
  382.8 4.7 %all-to-all-start.9 = ((f32[16,128,256]{2,1,0:T(8,128)}), f32[16,128,256]{2,1,0:T(8,128)S(1)}, u32[]{:S(2)}, u32[]{:S(2)}) async-start(f32[16,128,256]{2,1,0:T(8,128)} %broadcast_in_dim.59), calls=%async_computation.9 | async-start | bytes 4194304 | tf_op jit(solution)/shard_map/all_to_all | solution.py:196
  387.4 47.9 %all-to-all-done.9 = f32[16,128,256]{2,1,0:T(8,128)S(1)} async-done(((f32[16,128,256]{2,1,0:T(8,128)}), f32[16,128,256]{2,1,0:T(8,128)S(1)}, u32[]{:S(2)}, u32[]{:S(2)}) %all-to-all-start.9) | async-done | bytes 2097184 | tf_op jit(solution)/shard_map/all_to_all | solution.py:196
  435.4 2.3 copy.29
  437.6 1.3 copy.30
  (64 shorter events, 5.9 us)
Async XLA Ops:
  0.6 45.6 %copy-start = (bf16[1024,256]{1,0:T(8,128)(2,1)S(1)}, bf16[1024,256]{1,0:T(8,128)(2,1)}, u32[]{:S(2)}) copy-start(bf16[1024,256]{1,0:T(8,128)(2,1)} %param.7) | copy-start | bytes 1572868
  0.6 1.4 copy-start.1
  49.9 43.4 %all-to-all-start.1 = ((bf16[32,96,256]{2,1,0:T(8,128)(2,1)}), bf16[32,96,256]{2,1,0:T(8,128)(2,1)S(1)}, u32[]{:S(2)}, u32[]{:S(2)}) async-start(bf16[32,96,256]{2,1,0:T(8,128)(2,1)} %bitcast.64), calls=%async_computation.1 | async-start | bytes 3145728 | tf_op jit(solution)/shard_map/all_to_all | solution.py:60
  93.3 3.6 copy-start.3
  93.3 3.9 copy-start.5
  96.6 0.8 copy-start.7
  98.9 54.9 %all-to-all-start.2 = ((bf16[16,128,512]{2,1,0:T(8,128)(2,1)}), bf16[16,128,512]{2,1,0:T(8,128)(2,1)S(1)}, u32[]{:S(2)}, u32[]{:S(2)}) async-start(bf16[16,128,512]{2,1,0:T(8,128)(2,1)} %broadcast_in_dim.49), calls=%async_computation.2 | async-start | bytes 4194304 | tf_op jit(solution)/shard_map/all_to_all | solution.py:84
  170.3 3.6 copy-start.4
  170.3 4.7 %copy-start.6 = (bf16[1024,256]{1,0:T(8,128)(2,1)S(1)}, bf16[1024,256]{1,0:T(8,128)(2,1)}, u32[]{:S(2)}) copy-start(bf16[1024,256]{1,0:T(8,128)(2,1)} %param.10) | copy-start | bytes 1572868
  178.3 8.6 %copy-start.8 = (f32[128,1024]{1,0:T(8,128)S(1)}, f32[128,1024]{1,0:T(8,128)}, u32[]{:S(2)}) copy-start(f32[128,1024]{1,0:T(8,128)} %get-tuple-element.17) | copy-start | bytes 1572868
  178.3 54.6 %all-to-all-start.6 = ((f32[16,128,256]{2,1,0:T(8,128)}), f32[16,128,256]{2,1,0:T(8,128)S(1)}, u32[]{:S(2)}, u32[]{:S(2)}) async-start(f32[16,128,256]{2,1,0:T(8,128)} %bitcast.55), calls=%async_computation.6 | async-start | bytes 4194304 | tf_op jit(solution)/shard_map/all_to_all | solution.py:186
  232.9 48.6 %all-to-all-start.3 = ((bf16[32,96,256]{2,1,0:T(8,128)(2,1)}), bf16[32,96,256]{2,1,0:T(8,128)(2,1)}, u32[]{:S(2)}, u32[]{:S(2)}) async-start(bf16[32,96,256]{2,1,0:T(8,128)(2,1)} %bitcast.62), calls=%async_computation.3 | async-start | bytes 3145728 | tf_op jit(solution)/shard_map/all_to_all | solution.py:150
  281.5 16.7 %all-to-all-start.7 = ((f32[32,4,256]{2,1,0:T(4,128)}), f32[32,4,256]{2,1,0:T(4,128)S(1)}, u32[]{:S(2)}, u32[]{:S(2)}) async-start(f32[32,4,256]{2,1,0:T(4,128)} %reshape.340), calls=%async_computation.7 | async-start | bytes 262144 | tf_op jit(solution)/shard_map/all_to_all | solution.py:189
  290.8 11.2 %copy-start.9 = (s32[2,1024]{1,0:T(2,128)S(1)}, s32[2,1024]{1,0:T(2,128)}, u32[]{:S(2)}) copy-start(s32[2,1024]{1,0:T(2,128)} %param.13) | copy-start | bytes 24580
  298.2 32.3 %all-to-all-start.4 = ((f32[16,65,256]{2,1,0:T(8,128)}), f32[16,65,256]{2,1,0:T(8,128)S(1)}, u32[]{:S(2)}, u32[]{:S(2)}) async-start(f32[16,65,256]{2,1,0:T(8,128)} %pad_maximum_fusion.1), calls=%async_computation.4 | async-start | bytes 2359296 | tf_op jit(solution)/shard_map/all_to_all | solution.py:173
  331.2 18.2 %all-to-all-start.8 = ((f32[32,4,256]{2,1,0:T(4,128)}), f32[32,4,256]{2,1,0:T(4,128)S(1)}, u32[]{:S(2)}, u32[]{:S(2)}) async-start(f32[32,4,256]{2,1,0:T(4,128)} %broadcast_in_dim.57), calls=%async_computation.8 | async-start | bytes 262144 | tf_op jit(solution)/shard_map/all_to_all | solution.py:193
  350.5 30.6 %all-to-all-start.5 = ((f32[16,64,256]{2,1,0:T(8,128)}), f32[16,64,256]{2,1,0:T(8,128)S(1)}, u32[]{:S(2)}, u32[]{:S(2)}) async-start(f32[16,64,256]{2,1,0:T(8,128)} %broadcast_in_dim.56), calls=%async_computation.5 | async-start | bytes 2097152 | tf_op jit(solution)/shard_map/all_to_all | solution.py:180
  381.1 1.7 copy-start.2
  382.8 52.6 %all-to-all-start.9 = ((f32[16,128,256]{2,1,0:T(8,128)}), f32[16,128,256]{2,1,0:T(8,128)S(1)}, u32[]{:S(2)}, u32[]{:S(2)}) async-start(f32[16,128,256]{2,1,0:T(8,128)} %broadcast_in_dim.59), calls=%async_computation.9 | async-start | bytes 4194304 | tf_op jit(solution)/shard_map/all_to_all | solution.py:196

commit v3 on v2

--- a/solution.py
+++ b/solution.py
@@ -162,30 +162,28 @@
     )
     row_count = jnp.sum(row_match.astype(jnp.float32), axis=0)
     shard_rows = rows_dev // n_dp
+    tower_rows = 2 * hidden_width
+    dp_rows = tower_rows // n_dp
+    own_rows = dp_rows // shards
+    count_lanes = emb_width // shard_rows
     packed = jnp.concatenate(
         [
+            tower_part.reshape(n_dp, dp_rows, out_width),
             row_sum.reshape(n_dp, shard_rows, emb_width),
-            jnp.broadcast_to(row_count.reshape(n_dp, 1, shard_rows, 1), (n_dp, 1, shard_rows, emb_width // shard_rows))
-            .reshape(n_dp, 1, emb_width),
+            jnp.broadcast_to(
+                row_count.reshape(n_dp, 1, shard_rows, 1), (n_dp, 1, shard_rows, count_lanes)
+            ).reshape(n_dp, 1, emb_width),
         ],
         axis=1,
     )
     packed = jnp.sum(lax.all_to_all(packed, "dp", 0, 0, tiled=True), axis=0)
-    own_sum = packed[:shard_rows]
-    own_count = packed[shard_rows].reshape(shard_rows, emb_width // shard_rows)[:, 0]
+    own_sum = packed[dp_rows : dp_rows + shard_rows]
+    own_count = packed[dp_rows + shard_rows].reshape(shard_rows, count_lanes)[:, 0]
     own_seeds = lax.dynamic_slice_in_dim(row_seeds, dp_index * shard_rows, shard_rows)
     own_update = own_sum / clip_norm + NOISE_MULT * jnp.where(
         own_count[:, None] > 0.0, hashed_noise(own_seeds, emb_width), 0.0
     )
-    table_update = lax.all_to_all(
-        jnp.broadcast_to(own_update[None], (n_dp,) + own_update.shape), "dp", 0, 0, tiled=True
-    ).reshape(rows_dev, emb_width)
-    tower_rows = 2 * hidden_width
-    dp_rows = tower_rows // n_dp
-    part = tower_part.reshape(n_dp, dp_rows, out_width)
-    part = jnp.sum(lax.all_to_all(part, "dp", 0, 0, tiled=True), axis=0)
-    own_rows = dp_rows // shards
-    part = part.reshape(shards, own_rows, out_width)
+    part = packed[:dp_rows].reshape(shards, own_rows, out_width)
     part = jnp.sum(lax.all_to_all(part, "table", 0, 0, tiled=True), axis=0)
     first_row = dp_index * dp_rows + table_index * own_rows
     tower_seed_rows = lax.dynamic_slice_in_dim(tower_seeds.reshape(tower_rows), first_row, own_rows)
@@ -193,9 +191,12 @@
     part = lax.all_to_all(
         jnp.broadcast_to(part[None], (shards,) + part.shape), "table", 0, 0, tiled=True
     ).reshape(dp_rows, out_width)
-    tower_update = lax.all_to_all(
-        jnp.broadcast_to(part[None], (n_dp,) + part.shape), "dp", 0, 0, tiled=True
-    ).reshape(2, hidden_width, out_width)
+    finished = jnp.concatenate([part, own_update], axis=0)
+    finished = lax.all_to_all(
+        jnp.broadcast_to(finished[None], (n_dp,) + finished.shape), "dp", 0, 0, tiled=True
+    )
+    tower_update = finished[:, :dp_rows].reshape(2, hidden_width, out_width)
+    table_update = finished[:, dp_rows:].reshape(rows_dev, emb_width)
     return (table_update, tower_update)
 
 

time: 441 us -> 428 us (0.971)
  blocking collectives: 23.6 us -> 178 us
  waiting for transfers between devices: 277 us -> 140 us
  starting transfers between devices: 52 us -> 32.2 us
  local copies, waits for them, and re-layouts: 29.6 us -> 23.5 us
    all_to_all x0 -> x2, blocking collectives: none -> 155 us  [the longest x1 79.2 us: body(): packed = jnp.sum(lax.all_to_all(packed, 'dp', 0, 0, tiled=True), axis=0)]
    all_to_all x4 -> x0, waiting for transfers between devices: 141 us -> none  [the longest x1 47.9 us: body(): lax.all_to_all(jnp.broadcast_to(part[None], (n_dp,) + part.shape), 'dp',...]
    all_to_all x4 -> x0, starting transfers between devices: 18.3 us -> none  [the longest x1 6.3 us: body(): part = jnp.sum(lax.all_to_all(part, 'dp', 0, 0, tiled=True), axis=0)]
  transfers between devices with their start and end apart: 9 -> 5, of which waited for: 9 -> 5; matrix products, arithmetic and copies ran while one was open for 5% -> 2% of each run, Pallas kernels for 0% -> 0%
where the time goes in v3:
time: 428 us
  blocking collectives  178 us (42%)
  waiting for transfers between devices  140 us (33%)
  starting transfers between devices  32.2 us (8%)
  matrix products  30.5 us (7%)
  local copies, waits for them, and re-layouts  23.5 us (5%)
  other arithmetic  21.9 us (5%)
    all_to_all x1, blocking collectives, body(): packed = jnp.sum(lax.all_to_all(packed, 'dp', 0, 0, tiled=True), axis=0)  79.2 us
    all_to_all x1, blocking collectives, body(): lax.all_to_all(jnp.broadcast_to(finished[None], (n_dp,) + finished.shape)...  75.5 us
    all_to_all x1, waiting for transfers between devices, body(): lax.all_to_all(jnp.broadcast_to(both[None], (n_dp,) + both.shape), 'dp',...  45.6 us
    all_to_all x1, waiting for transfers between devices, body(): lax.all_to_all(fetched.reshape(shards, capacity, emb_width), 'table', spl...  37.4 us
    all_to_all x1, waiting for transfers between devices, body(): lax.all_to_all(grad_out.reshape(shards, capacity, emb_width), 'table', sp...  36.6 us
    all_to_all x1, blocking collectives, body(): lax.all_to_all(outgoing, 'table', split_axis=0, concat_axis=0, tiled=True)  23.6 us
    gather x2, local copies, waits for them, and re-layouts, body(): positions = row_owner[lookup_ids.reshape(-1)]  12.2 us
    all_to_all x1, waiting for transfers between devices, body(): lax.all_to_all(jnp.broadcast_to(part[None], (shards,) + part.shape), 'tab...  10.7 us
  transfers between devices with their start and end apart: 5, of which 5 were waited for; matrix products, arithmetic and copies ran while one was open for 2% of the time, Pallas kernels for 0%

profile of v3, /device:TPU:1, one launch (start us, length us, event | category | flops | bytes accessed | tf_op | source)
XLA Modules:
  0.0 427.6 jit_solution(18304951859315729993)
XLA Ops:
  0.7 1.0 copy.14
  1.7 0.3 reshape.328
  2.0 11.8 %gather_fusion = s32[2048]{0:T(1024)S(1)} fusion(s32[32768]{0:T(1024)S(1)} %copy-done.1, s32[2048]{0:T(1024)S(1)} %broadcast_clamp_fusion), kind=kCustom, calls=%fused_computation | custom fusion | bytes 24576 | tf_op jit(solution)/shard_map/gather | solution.py:41
  13.8 1.5 fusion.30
  15.4 5.9 %select_reduce_fusion = s32[3072]{0:T(1024)S(1)} fusion(s32[2048]{0:T(1024)S(1)} %get-tuple-element.11, s32[2048]{0:T(1024)S(1)} %get-tuple-element.10), kind=kLoop, calls=%fused_computation.1 | loop fusion | flops 18871296 | bytes 28672 | tf_op jit(solution)/shard_map/reduce_max | solution.py:52
  21.3 23.6 %all_to_all.44 = s32[32,1,96]{2,1,0:T(1,128)S(1)} all-to-all(s32[32,1,96]{2,1,0:T(1,128)S(1)} %all_to_all.27), channel_id=1, replica_groups=mesh['dp'=16,'table'=32] {'table'}, dimensions={0} | all-to-all | bytes 24576 | tf_op jit(solution)/shard_map/all_to_all | solution.py:54
  44.9 0.5 broadcast.502
  45.5 0.7 reduce.15
  46.2 3.6 fusion.20
  49.9 4.2 all-to-all-start.1
  54.1 0.5 gather.6
  54.6 0.5 convert_element_type.120
  55.1 0.3 fusion.37
  55.4 0.5 slice_reduce_fusion.1
  55.9 37.4 %all-to-all-done.1 = bf16[32,96,256]{2,1,0:T(8,128)(2,1)S(1)} async-done(((bf16[32,96,256]{2,1,0:T(8,128)(2,1)}), bf16[32,96,256]{2,1,0:T(8,128)(2,1)S(1)}, u32[]{:S(2)}, u32[]{:S(2)}) %all-to-all-start.1) | async-done | bytes 1572896 | tf_op jit(solution)/shard_map/all_to_all | solution.py:60
  93.3 3.3 fusion.25
  97.4 1.5 broadcast_in_dim.45
  98.9 7.0 %all-to-all-start.2 = ((bf16[16,128,512]{2,1,0:T(8,128)(2,1)}), bf16[16,128,512]{2,1,0:T(8,128)(2,1)S(1)}, u32[]{:S(2)}, u32[]{:S(2)}) async-start(bf16[16,128,512]{2,1,0:T(8,128)(2,1)} %broadcast_in_dim.45), calls=%async_computation.2 | async-start | bytes 4194304 | tf_op jit(solution)/shard_map/all_to_all | solution.py:84
  105.9 2.3 multiply_reduce_fusion.3
  108.3 45.6 %all-to-all-done.2 = bf16[16,128,512]{2,1,0:T(8,128)(2,1)S(1)} async-done(((bf16[16,128,512]{2,1,0:T(8,128)(2,1)}), bf16[16,128,512]{2,1,0:T(8,128)(2,1)S(1)}, u32[]{:S(2)}, u32[]{:S(2)}) %all-to-all-start.2) | async-done | bytes 2097184 | tf_op jit(solution)/shard_map/all_to_all | solution.py:84
  153.9 0.3 fusion.75
  154.1 8.1 %fusion.77 = (f32[2048]{0:T(1024)S(1)}, f32[2048,2048]{0,1:T(8,128)}) fusion(bf16[2048,256]{1,0:T(8,128)(2,1)S(1)} %bitcast.51, bf16[2048,256]{1,0:T(8,128)(2,1)S(1)} %bitcast.53), kind=kOutput, calls=%fused_computation.132 | convolution fusion | flops 2155870208 | bytes 18882560 | tf_op jit(solution)/shard_map/dot_general | solution.py:89
  162.2 8.1 %exponential_reduce_fusion = f32[2048]{0:T(1024)S(1)} fusion(f32[2048,2048]{0,1:T(8,128)} %get-tuple-element.13, f32[2048]{0:T(1024)S(1)} %get-tuple-element.12), kind=kLoop, calls=%fused_computation.3 | loop fusion | flops 8386560 | bytes 16793600 | tf_op jit(solution)/shard_map/reduce_sum | solution.py:93
  170.3 1.8 fusion.45
  172.2 1.7 fusion.43
  173.9 0.4 multiply_reduce_fusion
  174.6 0.4 multiply_reduce_fusion.1
  175.4 5.3 %fusion.17 = bf16[3072,256]{1,0:T(8,128)(2,1)} fusion(s32[1024]{0:T(1024)S(1)} %get-tuple-element.5, s32[1024]{0:T(1024)S(1)} %get-tuple-element.4, f32[128,4,256]{2,1,0:T(4,128)S(1)} %reshape.338, f32[128,4,256]{2,1,0:T(4,128)S(1)} %reshape.337, f32[1024]{0:T(1024)S(1)} %mul.208), kind=kOutput, calls=%fused_computation.25 | convolution fusion | flops 1621622784 | bytes 2633728 | tf_op jit(solution)/shard_map/dot_general | solution.py:144
  180.7 9.6 %all-to-all-start.3 = ((bf16[32,96,256]{2,1,0:T(8,128)(2,1)}), bf16[32,96,256]{2,1,0:T(8,128)(2,1)}, u32[]{:S(2)}, u32[]{:S(2)}) async-start(bf16[32,96,256]{2,1,0:T(8,128)(2,1)} %bitcast.10), calls=%async_computation.3 | async-start | bytes 3145728 | tf_op jit(solution)/shard_map/all_to_all | solution.py:150
  190.3 1.5 convert_reduce_fusion
  192.0 0.4 convolution_bitcast_fusion
  192.4 0.4 convolution_bitcast_fusion.1
  192.9 36.6 %all-to-all-done.3 = bf16[32,96,256]{2,1,0:T(8,128)(2,1)} async-done(((bf16[32,96,256]{2,1,0:T(8,128)(2,1)}), bf16[32,96,256]{2,1,0:T(8,128)(2,1)}, u32[]{:S(2)}, u32[]{:S(2)}) %all-to-all-start.3) | async-done | bytes 1572896 | tf_op jit(solution)/shard_map/all_to_all | solution.py:150
  229.6 3.3 fusion.4
  232.8 0.3 pad_maximum_fusion
  233.1 79.2 %all_to_all.45 = f32[16,193,256]{2,1,0:T(8,128)} all-to-all(f32[16,193,256]{2,1,0:T(8,128)S(1)} %pad_maximum_fusion), channel_id=1, replica_groups=mesh['dp'=16,'table'=32] {'dp'}, dimensions={0} | all-to-all | bytes 6324224 | tf_op jit(solution)/shard_map/all_to_all | solution.py:179
  312.3 2.1 reduce_sum.108
  314.5 0.7 reshape.341
  315.2 7.7 %all-to-all-start.5 = ((f32[32,4,256]{2,1,0:T(4,128)}), f32[32,4,256]{2,1,0:T(4,128)S(1)}, u32[]{:S(2)}, u32[]{:S(2)}) async-start(f32[32,4,256]{2,1,0:T(4,128)} %reshape.341), calls=%async_computation.5 | async-start | bytes 262144 | tf_op jit(solution)/shard_map/all_to_all | solution.py:187
  322.9 0.8 dynamic_slice.16
  323.9 9.8 %all-to-all-done.5 = f32[32,4,256]{2,1,0:T(4,128)S(1)} async-done(((f32[32,4,256]{2,1,0:T(4,128)}), f32[32,4,256]{2,1,0:T(4,128)S(1)}, u32[]{:S(2)}, u32[]{:S(2)}) %all-to-all-start.5) | async-done | bytes 131104 | tf_op jit(solution)/shard_map/all_to_all | solution.py:187
  333.8 0.7 broadcast_in_dim.49
  334.5 3.7 all-to-all-start.6
  338.5 10.7 %all-to-all-done.6 = f32[32,4,256]{2,1,0:T(4,128)S(1)} async-done(((f32[32,4,256]{2,1,0:T(4,128)}), f32[32,4,256]{2,1,0:T(4,128)S(1)}, u32[]{:S(2)}, u32[]{:S(2)}) %all-to-all-start.6) | async-done | bytes 131104 | tf_op jit(solution)/shard_map/all_to_all | solution.py:191
  349.3 0.3 broadcast_in_dim.53
  349.6 75.5 %all_to_all.46 = f32[16,192,256]{2,1,0:T(8,128)S(1)} all-to-all(f32[16,192,256]{2,1,0:T(8,128)S(1)} %broadcast_in_dim.53), channel_id=1, replica_groups=mesh['dp'=16,'table'=32] {'dp'}, dimensions={0} | all-to-all | bytes 6291456 | tf_op jit(solution)/shard_map/all_to_all | solution.py:195
  425.1 1.0 slice.60
  426.1 1.5 slice.61
  (54 shorter events, 2.8 us)
Async XLA Ops:
  0.6 45.6 %copy-start = (bf16[1024,256]{1,0:T(8,128)(2,1)S(1)}, bf16[1024,256]{1,0:T(8,128)(2,1)}, u32[]{:S(2)}) copy-start(bf16[1024,256]{1,0:T(8,128)(2,1)} %param.7) | copy-start | bytes 1572868
  0.6 1.4 copy-start.1
  49.9 43.4 %all-to-all-start.1 = ((bf16[32,96,256]{2,1,0:T(8,128)(2,1)}), bf16[32,96,256]{2,1,0:T(8,128)(2,1)S(1)}, u32[]{:S(2)}, u32[]{:S(2)}) async-start(bf16[32,96,256]{2,1,0:T(8,128)(2,1)} %bitcast.62), calls=%async_computation.1 | async-start | bytes 3145728 | tf_op jit(solution)/shard_map/all_to_all | solution.py:60
  93.3 3.6 copy-start.2
  93.3 3.9 copy-start.4
  96.6 0.8 copy-start.6
  98.9 54.9 %all-to-all-start.2 = ((bf16[16,128,512]{2,1,0:T(8,128)(2,1)}), bf16[16,128,512]{2,1,0:T(8,128)(2,1)S(1)}, u32[]{:S(2)}, u32[]{:S(2)}) async-start(bf16[16,128,512]{2,1,0:T(8,128)(2,1)} %broadcast_in_dim.45), calls=%async_computation.2 | async-start | bytes 4194304 | tf_op jit(solution)/shard_map/all_to_all | solution.py:84
  170.3 3.6 copy-start.3
  170.3 4.2 copy-start.5
  180.7 48.8 %all-to-all-start.3 = ((bf16[32,96,256]{2,1,0:T(8,128)(2,1)}), bf16[32,96,256]{2,1,0:T(8,128)(2,1)}, u32[]{:S(2)}, u32[]{:S(2)}) async-start(bf16[32,96,256]{2,1,0:T(8,128)(2,1)} %bitcast.10), calls=%async_computation.3 | async-start | bytes 3145728 | tf_op jit(solution)/shard_map/all_to_all | solution.py:150
  312.3 10.6 %copy-start.7 = (s32[2,1024]{1,0:T(2,128)S(1)}, s32[2,1024]{1,0:T(2,128)}, u32[]{:S(2)}) copy-start(s32[2,1024]{1,0:T(2,128)} %param.13) | copy-start | bytes 24580
  315.2 18.5 %all-to-all-start.5 = ((f32[32,4,256]{2,1,0:T(4,128)}), f32[32,4,256]{2,1,0:T(4,128)S(1)}, u32[]{:S(2)}, u32[]{:S(2)}) async-start(f32[32,4,256]{2,1,0:T(4,128)} %reshape.341), calls=%async_computation.5 | async-start | bytes 262144 | tf_op jit(solution)/shard_map/all_to_all | solution.py:187
  334.5 14.7 %all-to-all-start.6 = ((f32[32,4,256]{2,1,0:T(4,128)}), f32[32,4,256]{2,1,0:T(4,128)S(1)}, u32[]{:S(2)}, u32[]{:S(2)}) async-start(f32[32,4,256]{2,1,0:T(4,128)} %broadcast_in_dim.49), calls=%async_computation.6 | async-start | bytes 262144 | tf_op jit(solution)/shard_map/all_to_all | solution.py:191

commit v4 on v3

--- a/solution.py
+++ b/solution.py
@@ -191,10 +191,10 @@
     part = lax.all_to_all(
         jnp.broadcast_to(part[None], (shards,) + part.shape), "table", 0, 0, tiled=True
     ).reshape(dp_rows, out_width)
-    finished = jnp.concatenate([part, own_update], axis=0)
+    finished = jnp.concatenate([part, own_update], axis=0).astype(jnp.bfloat16)
     finished = lax.all_to_all(
         jnp.broadcast_to(finished[None], (n_dp,) + finished.shape), "dp", 0, 0, tiled=True
-    )
+    ).astype(jnp.float32)
     tower_update = finished[:, :dp_rows].reshape(2, hidden_width, out_width)
     table_update = finished[:, dp_rows:].reshape(rows_dev, emb_width)
     return (table_update, tower_update)

time: 428 us -> 393 us (0.918)
  blocking collectives: 178 us -> 144 us
    all_to_all x1, blocking collectives: 75.5 us -> 41.3 us  [body(): lax.all_to_all(jnp.broadcast_to(finished[None], (n_dp,) + finished.shape)...]
where the time goes in v4:
time: 393 us; the launch traced here: 392 us
  blocking collectives  144 us (37%)
  waiting for transfers between devices  139 us (35%)
  starting transfers between devices  32.2 us (8%)
  matrix products  30.5 us (8%)
  local copies, waits for them, and re-layouts  23.4 us (6%)
  other arithmetic  21.9 us (6%)
    all_to_all x1, blocking collectives, body(): packed = jnp.sum(lax.all_to_all(packed, 'dp', 0, 0, tiled=True), axis=0)  79.2 us
    all_to_all x1, waiting for transfers between devices, body(): lax.all_to_all(jnp.broadcast_to(both[None], (n_dp,) + both.shape), 'dp',...  45.6 us
    all_to_all x1, blocking collectives, body(): lax.all_to_all(jnp.broadcast_to(finished[None], (n_dp,) + finished.shape)...  41.3 us
    all_to_all x1, waiting for transfers between devices, body(): lax.all_to_all(fetched.reshape(shards, capacity, emb_width), 'table', spl...  37.4 us
    all_to_all x1, waiting for transfers between devices, body(): lax.all_to_all(grad_out.reshape(shards, capacity, emb_width), 'table', sp...  36.6 us
    all_to_all x1, blocking collectives, body(): lax.all_to_all(outgoing, 'table', split_axis=0, concat_axis=0, tiled=True)  23.6 us
    gather x2, local copies, waits for them, and re-layouts, body(): positions = row_owner[lookup_ids.reshape(-1)]  12.2 us
    all_to_all x1, waiting for transfers between devices, body(): lax.all_to_all(jnp.broadcast_to(part[None], (shards,) + part.shape), 'tab...  9.76 us
  transfers between devices with their start and end apart: 5, of which 5 were waited for; matrix products, arithmetic and copies ran while one was open for 2% of the time, Pallas kernels for 0%

profile of v4, /device:TPU:1, one launch (start us, length us, event | category | flops | bytes accessed | tf_op | source)
XLA Modules:
  0.0 392.3 jit_solution(7608576259452213260)
XLA Ops:
  0.7 1.0 copy.14
  1.7 0.3 reshape.342
  2.0 11.8 %gather_fusion = s32[2048]{0:T(1024)S(1)} fusion(s32[32768]{0:T(1024)S(1)} %copy-done.1, s32[2048]{0:T(1024)S(1)} %broadcast_clamp_fusion), kind=kCustom, calls=%fused_computation | custom fusion | bytes 24576 | tf_op jit(solution)/shard_map/gather | solution.py:41
  13.8 1.5 fusion.30
  15.4 5.9 %select_reduce_fusion = s32[3072]{0:T(1024)S(1)} fusion(s32[2048]{0:T(1024)S(1)} %get-tuple-element.11, s32[2048]{0:T(1024)S(1)} %get-tuple-element.10), kind=kLoop, calls=%fused_computation.1 | loop fusion | flops 18871296 | bytes 28672 | tf_op jit(solution)/shard_map/reduce_max | solution.py:52
  21.3 23.6 %all_to_all.44 = s32[32,1,96]{2,1,0:T(1,128)S(1)} all-to-all(s32[32,1,96]{2,1,0:T(1,128)S(1)} %all_to_all.27), channel_id=1, replica_groups=mesh['dp'=16,'table'=32] {'table'}, dimensions={0} | all-to-all | bytes 24576 | tf_op jit(solution)/shard_map/all_to_all | solution.py:54
  44.9 0.5 broadcast.501
  45.5 0.7 reduce.15
  46.2 3.6 fusion.20
  49.9 4.2 %all-to-all-start.1 = ((bf16[32,96,256]{2,1,0:T(8,128)(2,1)}), bf16[32,96,256]{2,1,0:T(8,128)(2,1)S(1)}, u32[]{:S(2)}, u32[]{:S(2)}) async-start(bf16[32,96,256]{2,1,0:T(8,128)(2,1)} %bitcast.62), calls=%async_computation.1 | async-start | bytes 3145728 | tf_op jit(solution)/shard_map/all_to_all | solution.py:60
  54.1 0.5 gather.6
  54.6 0.5 convert_element_type.128
  55.1 0.3 fusion.37
  55.4 0.5 slice_reduce_fusion.1
  55.9 37.4 %all-to-all-done.1 = bf16[32,96,256]{2,1,0:T(8,128)(2,1)S(1)} async-done(((bf16[32,96,256]{2,1,0:T(8,128)(2,1)}), bf16[32,96,256]{2,1,0:T(8,128)(2,1)S(1)}, u32[]{:S(2)}, u32[]{:S(2)}) %all-to-all-start.1) | async-done | bytes 1572896 | tf_op jit(solution)/shard_map/all_to_all | solution.py:60
  93.3 3.3 fusion.25
  97.4 1.5 broadcast_in_dim.45
  98.9 7.0 %all-to-all-start.2 = ((bf16[16,128,512]{2,1,0:T(8,128)(2,1)}), bf16[16,128,512]{2,1,0:T(8,128)(2,1)S(1)}, u32[]{:S(2)}, u32[]{:S(2)}) async-start(bf16[16,128,512]{2,1,0:T(8,128)(2,1)} %broadcast_in_dim.45), calls=%async_computation.2 | async-start | bytes 4194304 | tf_op jit(solution)/shard_map/all_to_all | solution.py:84
  105.9 2.3 multiply_reduce_fusion.3
  108.3 45.6 %all-to-all-done.2 = bf16[16,128,512]{2,1,0:T(8,128)(2,1)S(1)} async-done(((bf16[16,128,512]{2,1,0:T(8,128)(2,1)}), bf16[16,128,512]{2,1,0:T(8,128)(2,1)S(1)}, u32[]{:S(2)}, u32[]{:S(2)}) %all-to-all-start.2) | async-done | bytes 2097184 | tf_op jit(solution)/shard_map/all_to_all | solution.py:84
  153.9 0.3 fusion.76
  154.1 8.1 %fusion.78 = (f32[2048]{0:T(1024)S(1)}, f32[2048,2048]{0,1:T(8,128)}) fusion(bf16[2048,256]{1,0:T(8,128)(2,1)S(1)} %bitcast.51, bf16[2048,256]{1,0:T(8,128)(2,1)S(1)} %bitcast.53), kind=kOutput, calls=%fused_computation.133 | convolution fusion | flops 2155870208 | bytes 18882560 | tf_op jit(solution)/shard_map/dot_general | solution.py:89
  162.2 8.1 %exponential_reduce_fusion = f32[2048]{0:T(1024)S(1)} fusion(f32[2048,2048]{0,1:T(8,128)} %get-tuple-element.13, f32[2048]{0:T(1024)S(1)} %get-tuple-element.12), kind=kLoop, calls=%fused_computation.3 | loop fusion | flops 8386560 | bytes 16793600 | tf_op jit(solution)/shard_map/reduce_sum | solution.py:93
  170.3 1.8 fusion.45
  172.2 1.7 fusion.43
  173.9 0.4 multiply_reduce_fusion
  174.3 0.3 reshape.352
  174.6 0.4 multiply_reduce_fusion.1
  175.4 5.3 %fusion.17 = bf16[3072,256]{1,0:T(8,128)(2,1)} fusion(s32[1024]{0:T(1024)S(1)} %get-tuple-element.5, s32[1024]{0:T(1024)S(1)} %get-tuple-element.4, f32[128,4,256]{2,1,0:T(4,128)S(1)} %reshape.352, f32[128,4,256]{2,1,0:T(4,128)S(1)} %reshape.351, f32[1024]{0:T(1024)S(1)} %mul.208), kind=kOutput, calls=%fused_computation.25 | convolution fusion | flops 1621622784 | bytes 2633728 | tf_op jit(solution)/shard_map/dot_general | solution.py:144
  180.7 9.6 %all-to-all-start.3 = ((bf16[32,96,256]{2,1,0:T(8,128)(2,1)}), bf16[32,96,256]{2,1,0:T(8,128)(2,1)}, u32[]{:S(2)}, u32[]{:S(2)}) async-start(bf16[32,96,256]{2,1,0:T(8,128)(2,1)} %bitcast.10), calls=%async_computation.3 | async-start | bytes 3145728 | tf_op jit(solution)/shard_map/all_to_all | solution.py:150
  190.3 1.5 convert_reduce_fusion
  192.0 0.4 convolution_bitcast_fusion
  192.4 0.4 convolution_bitcast_fusion.1
  192.9 36.6 %all-to-all-done.3 = bf16[32,96,256]{2,1,0:T(8,128)(2,1)} async-done(((bf16[32,96,256]{2,1,0:T(8,128)(2,1)}), bf16[32,96,256]{2,1,0:T(8,128)(2,1)}, u32[]{:S(2)}, u32[]{:S(2)}) %all-to-all-start.3) | async-done | bytes 1572896 | tf_op jit(solution)/shard_map/all_to_all | solution.py:150
  229.6 3.3 fusion.4
  232.8 0.3 pad_maximum_fusion
  233.1 79.2 %all_to_all.45 = f32[16,193,256]{2,1,0:T(8,128)} all-to-all(f32[16,193,256]{2,1,0:T(8,128)S(1)} %pad_maximum_fusion), channel_id=1, replica_groups=mesh['dp'=16,'table'=32] {'dp'}, dimensions={0} | all-to-all | bytes 6324224 | tf_op jit(solution)/shard_map/all_to_all | solution.py:179
  312.3 2.1 reduce_sum.108
  314.5 0.7 reshape.355
  315.2 7.7 %all-to-all-start.5 = ((f32[32,4,256]{2,1,0:T(4,128)}), f32[32,4,256]{2,1,0:T(4,128)S(1)}, u32[]{:S(2)}, u32[]{:S(2)}) async-start(f32[32,4,256]{2,1,0:T(4,128)} %reshape.355), calls=%async_computation.5 | async-start | bytes 262144 | tf_op jit(solution)/shard_map/all_to_all | solution.py:187
  323.0 0.8 dynamic_slice.16
  324.0 9.6 %all-to-all-done.5 = f32[32,4,256]{2,1,0:T(4,128)S(1)} async-done(((f32[32,4,256]{2,1,0:T(4,128)}), f32[32,4,256]{2,1,0:T(4,128)S(1)}, u32[]{:S(2)}, u32[]{:S(2)}) %all-to-all-start.5) | async-done | bytes 131104 | tf_op jit(solution)/shard_map/all_to_all | solution.py:187
  333.8 0.6 broadcast_in_dim.49
  334.5 3.7 all-to-all-start.6
  338.4 9.8 %all-to-all-done.6 = bf16[32,4,256]{2,1,0:T(4,128)(2,1)S(1)} async-done(((bf16[32,4,256]{2,1,0:T(4,128)(2,1)}), bf16[32,4,256]{2,1,0:T(4,128)(2,1)S(1)}, u32[]{:S(2)}, u32[]{:S(2)}) %all-to-all-start.6) | async-done | bytes 65568 | tf_op jit(solution)/shard_map/all_to_all | solution.py:191
  348.3 41.3 %all_to_all.46 = bf16[16,192,256]{2,1,0:T(8,128)(2,1)S(1)} all-to-all(bf16[16,192,256]{2,1,0:T(8,128)(2,1)S(1)} %broadcast_in_dim.53), channel_id=1, replica_groups=mesh['dp'=16,'table'=32] {'dp'}, dimensions={0} | all-to-all | bytes 3145728 | tf_op jit(solution)/shard_map/all_to_all | solution.py:195
  389.6 1.1 slice.60
  390.7 1.5 slice.61
  (54 shorter events, 2.7 us)
Async XLA Ops:
  0.6 45.6 %copy-start = (bf16[1024,256]{1,0:T(8,128)(2,1)S(1)}, bf16[1024,256]{1,0:T(8,128)(2,1)}, u32[]{:S(2)}) copy-start(bf16[1024,256]{1,0:T(8,128)(2,1)} %param.7) | copy-start | bytes 1572868
  0.6 1.4 copy-start.1
  49.9 43.4 %all-to-all-start.1 = ((bf16[32,96,256]{2,1,0:T(8,128)(2,1)}), bf16[32,96,256]{2,1,0:T(8,128)(2,1)S(1)}, u32[]{:S(2)}, u32[]{:S(2)}) async-start(bf16[32,96,256]{2,1,0:T(8,128)(2,1)} %bitcast.62), calls=%async_computation.1 | async-start | bytes 3145728 | tf_op jit(solution)/shard_map/all_to_all | solution.py:60
  93.3 3.6 copy-start.2
  93.3 3.9 copy-start.4
  96.6 0.8 copy-start.6
  98.9 54.9 %all-to-all-start.2 = ((bf16[16,128,512]{2,1,0:T(8,128)(2,1)}), bf16[16,128,512]{2,1,0:T(8,128)(2,1)S(1)}, u32[]{:S(2)}, u32[]{:S(2)}) async-start(bf16[16,128,512]{2,1,0:T(8,128)(2,1)} %broadcast_in_dim.45), calls=%async_computation.2 | async-start | bytes 4194304 | tf_op jit(solution)/shard_map/all_to_all | solution.py:84
  170.3 3.6 copy-start.3
  170.3 4.2 %copy-start.5 = (bf16[1024,256]{1,0:T(8,128)(2,1)S(1)}, bf16[1024,256]{1,0:T(8,128)(2,1)}, u32[]{:S(2)}) copy-start(bf16[1024,256]{1,0:T(8,128)(2,1)} %param.10) | copy-start | bytes 1572868
  180.7 48.8 %all-to-all-start.3 = ((bf16[32,96,256]{2,1,0:T(8,128)(2,1)}), bf16[32,96,256]{2,1,0:T(8,128)(2,1)}, u32[]{:S(2)}, u32[]{:S(2)}) async-start(bf16[32,96,256]{2,1,0:T(8,128)(2,1)} %bitcast.10), calls=%async_computation.3 | async-start | bytes 3145728 | tf_op jit(solution)/shard_map/all_to_all | solution.py:150
  312.3 10.6 %copy-start.7 = (s32[2,1024]{1,0:T(2,128)S(1)}, s32[2,1024]{1,0:T(2,128)}, u32[]{:S(2)}) copy-start(s32[2,1024]{1,0:T(2,128)} %param.13) | copy-start | bytes 24580
  315.2 18.5 %all-to-all-start.5 = ((f32[32,4,256]{2,1,0:T(4,128)}), f32[32,4,256]{2,1,0:T(4,128)S(1)}, u32[]{:S(2)}, u32[]{:S(2)}) async-start(f32[32,4,256]{2,1,0:T(4,128)} %reshape.355), calls=%async_computation.5 | async-start | bytes 262144 | tf_op jit(solution)/shard_map/all_to_all | solution.py:187
  334.5 13.7 %all-to-all-start.6 = ((bf16[32,4,256]{2,1,0:T(4,128)(2,1)}), bf16[32,4,256]{2,1,0:T(4,128)(2,1)S(1)}, u32[]{:S(2)}, u32[]{:S(2)}) async-start(bf16[32,4,256]{2,1,0:T(4,128)(2,1)} %broadcast_in_dim.49), calls=%async_computation.6 | async-start | bytes 131072 | tf_op jit(solution)/shard_map/all_to_all | solution.py:191

commit v5 on v4

--- a/solution.py
+++ b/solution.py
@@ -166,9 +166,11 @@
     dp_rows = tower_rows // n_dp
     own_rows = dp_rows // shards
     count_lanes = emb_width // shard_rows
+    tower_slice = lax.psum_scatter(
+        tower_part.reshape(tower_rows, out_width), "dp", scatter_dimension=0, tiled=True
+    )
     packed = jnp.concatenate(
         [
-            tower_part.reshape(n_dp, dp_rows, out_width),
             row_sum.reshape(n_dp, shard_rows, emb_width),
             jnp.broadcast_to(
                 row_count.reshape(n_dp, 1, shard_rows, 1), (n_dp, 1, shard_rows, count_lanes)
@@ -177,13 +179,13 @@
         axis=1,
     )
     packed = jnp.sum(lax.all_to_all(packed, "dp", 0, 0, tiled=True), axis=0)
-    own_sum = packed[dp_rows : dp_rows + shard_rows]
-    own_count = packed[dp_rows + shard_rows].reshape(shard_rows, count_lanes)[:, 0]
+    own_sum = packed[:shard_rows]
+    own_count = packed[shard_rows].reshape(shard_rows, count_lanes)[:, 0]
     own_seeds = lax.dynamic_slice_in_dim(row_seeds, dp_index * shard_rows, shard_rows)
     own_update = own_sum / clip_norm + NOISE_MULT * jnp.where(
         own_count[:, None] > 0.0, hashed_noise(own_seeds, emb_width), 0.0
     )
-    part = packed[:dp_rows].reshape(shards, own_rows, out_width)
+    part = tower_slice.reshape(shards, own_rows, out_width)
     part = jnp.sum(lax.all_to_all(part, "table", 0, 0, tiled=True), axis=0)
     first_row = dp_index * dp_rows + table_index * own_rows
     tower_seed_rows = lax.dynamic_slice_in_dim(tower_seeds.reshape(tower_rows), first_row, own_rows)

time: 393 us -> 399 us (1.015)
  blocking collectives: 144 us -> 68.2 us
  waiting for transfers between devices: 139 us -> 188 us
  starting transfers between devices: 32.2 us -> 50.9 us
  between operations: 1.1 us -> 14.5 us
    all_to_all x1 -> x0, blocking collectives: 79.2 us -> none  [body(): packed = jnp.sum(lax.all_to_all(packed, 'dp', 0, 0, tiled=True), axis=0)]
    reduce_scatter x0 -> x1, waiting for transfers between devices: none -> 60.8 us  [body(): lax.psum_scatter(tower_part.reshape(tower_rows, out_width), 'dp', scatter...]
    all_to_all x1, waiting for transfers between devices: 36.6 us -> 0.01 us  [body(): lax.all_to_all(grad_out.reshape(shards, capacity, emb_width), 'table', sp...]
    all_to_all x0 -> x1, waiting for transfers between devices: none -> 27.1 us  [body(): packed = jnp.sum(lax.all_to_all(packed, 'dp', 0, 0, tiled=True), axis=0)]
    all_to_all x1, starting transfers between devices: 7.71 us -> 21.6 us  [body(): part = jnp.sum(lax.all_to_all(part, 'table', 0, 0, tiled=True), axis=0)]
    all_to_all x0 -> x1, starting transfers between devices: none -> 4.46 us  [body(): packed = jnp.sum(lax.all_to_all(packed, 'dp', 0, 0, tiled=True), axis=0)]
  transfers between devices with their start and end apart: 5 -> 7, of which waited for: 5 -> 6; matrix products, arithmetic and copies ran while one was open for 2% -> 4% of each run, Pallas kernels for 0% -> 0%
where the time goes in v5:
time: 399 us; the launch traced here: 398 us
  waiting for transfers between devices  188 us (47%)
  blocking collectives  68.2 us (17%)
  starting transfers between devices  50.9 us (13%)
  matrix products  29.4 us (7%)
  local copies, waits for them, and re-layouts  24.3 us (6%)
  other arithmetic  22 us (6%)
  between operations  14.5 us (4%)
    reduce_scatter x1, waiting for transfers between devices, body(): lax.psum_scatter(tower_part.reshape(tower_rows, out_width), 'dp', scatter...  60.8 us
    all_to_all x1, waiting for transfers between devices, body(): lax.all_to_all(jnp.broadcast_to(both[None], (n_dp,) + both.shape), 'dp',...  45.3 us
    all_to_all x1, blocking collectives, body(): lax.all_to_all(jnp.broadcast_to(finished[None], (n_dp,) + finished.shape)...  44.6 us
    all_to_all x1, waiting for transfers between devices, body(): lax.all_to_all(fetched.reshape(shards, capacity, emb_width), 'table', spl...  37.4 us
    all_to_all x1, waiting for transfers between devices, body(): packed = jnp.sum(lax.all_to_all(packed, 'dp', 0, 0, tiled=True), axis=0)  27.1 us
    all_to_all x1, blocking collectives, body(): lax.all_to_all(outgoing, 'table', split_axis=0, concat_axis=0, tiled=True)  23.6 us
    all_to_all x1, starting transfers between devices, body(): part = jnp.sum(lax.all_to_all(part, 'table', 0, 0, tiled=True), axis=0)  21.6 us
    gather x2, local copies, waits for them, and re-layouts, body(): positions = row_owner[lookup_ids.reshape(-1)]  12.2 us
  transfers between devices with their start and end apart: 7, of which 6 were waited for; matrix products, arithmetic and copies ran while one was open for 4% of the time, Pallas kernels for 0%

profile of v5, /device:TPU:1, one launch (start us, length us, event | category | flops | bytes accessed | tf_op | source)
XLA Modules:
  0.0 397.6 jit_solution(9355342938557892529)
XLA Ops:
  7.2 1.0 copy.14
  8.2 0.3 reshape.342
  8.6 11.8 %gather_fusion = s32[2048]{0:T(1024)S(1)} fusion(s32[32768]{0:T(1024)S(1)} %copy-done.1, s32[2048]{0:T(1024)S(1)} %broadcast_clamp_fusion), kind=kCustom, calls=%fused_computation | custom fusion | bytes 24576 | tf_op jit(solution)/shard_map/gather | solution.py:41
  20.4 1.5 fusion.30
  21.9 5.9 %select_reduce_fusion = s32[3072]{0:T(1024)S(1)} fusion(s32[2048]{0:T(1024)S(1)} %get-tuple-element.11, s32[2048]{0:T(1024)S(1)} %get-tuple-element.10), kind=kLoop, calls=%fused_computation.1 | loop fusion | flops 18871296 | bytes 28672 | tf_op jit(solution)/shard_map/reduce_max | solution.py:52
  27.9 23.6 %all_to_all.44 = s32[32,1,96]{2,1,0:T(1,128)S(1)} all-to-all(s32[32,1,96]{2,1,0:T(1,128)S(1)} %all_to_all.27), channel_id=1, replica_groups=mesh['dp'=16,'table'=32] {'table'}, dimensions={0} | all-to-all | bytes 24576 | tf_op jit(solution)/shard_map/all_to_all | solution.py:54
  51.5 0.5 broadcast.501
  52.0 0.7 reduce.15
  52.8 3.6 fusion.20
  56.4 4.2 %all-to-all-start.1 = ((bf16[32,96,256]{2,1,0:T(8,128)(2,1)}), bf16[32,96,256]{2,1,0:T(8,128)(2,1)S(1)}, u32[]{:S(2)}, u32[]{:S(2)}) async-start(bf16[32,96,256]{2,1,0:T(8,128)(2,1)} %bitcast.64), calls=%async_computation.1 | async-start | bytes 3145728 | tf_op jit(solution)/shard_map/all_to_all | solution.py:60
  60.6 0.5 gather.6
  61.1 0.5 convert_element_type.128
  61.6 0.3 fusion.37
  61.9 0.5 slice_reduce_fusion.1
  62.4 37.4 %all-to-all-done.1 = bf16[32,96,256]{2,1,0:T(8,128)(2,1)S(1)} async-done(((bf16[32,96,256]{2,1,0:T(8,128)(2,1)}), bf16[32,96,256]{2,1,0:T(8,128)(2,1)S(1)}, u32[]{:S(2)}, u32[]{:S(2)}) %all-to-all-start.1) | async-done | bytes 1572896 | tf_op jit(solution)/shard_map/all_to_all | solution.py:60
  99.8 3.3 fusion.25
  104.0 1.5 broadcast_in_dim.45
  105.5 7.0 %all-to-all-start.2 = ((bf16[16,128,512]{2,1,0:T(8,128)(2,1)}), bf16[16,128,512]{2,1,0:T(8,128)(2,1)S(1)}, u32[]{:S(2)}, u32[]{:S(2)}) async-start(bf16[16,128,512]{2,1,0:T(8,128)(2,1)} %broadcast_in_dim.45), calls=%async_computation.2 | async-start | bytes 4194304 | tf_op jit(solution)/shard_map/all_to_all | solution.py:84
  112.7 2.4 multiply_reduce_fusion.3
  115.1 45.3 %all-to-all-done.2 = bf16[16,128,512]{2,1,0:T(8,128)(2,1)S(1)} async-done(((bf16[16,128,512]{2,1,0:T(8,128)(2,1)}), bf16[16,128,512]{2,1,0:T(8,128)(2,1)S(1)}, u32[]{:S(2)}, u32[]{:S(2)}) %all-to-all-start.2) | async-done | bytes 2097184 | tf_op jit(solution)/shard_map/all_to_all | solution.py:84
  160.4 0.3 fusion.76
  160.7 8.1 %fusion.78 = (f32[2048]{0:T(1024)S(1)}, f32[2048,2048]{0,1:T(8,128)}) fusion(bf16[2048,256]{1,0:T(8,128)(2,1)S(1)} %bitcast.51, bf16[2048,256]{1,0:T(8,128)(2,1)S(1)} %bitcast.53), kind=kOutput, calls=%fused_computation.133 | convolution fusion | flops 2155870208 | bytes 18882560 | tf_op jit(solution)/shard_map/dot_general | solution.py:89
  168.8 8.1 %exponential_reduce_fusion = f32[2048]{0:T(1024)S(1)} fusion(f32[2048,2048]{0,1:T(8,128)} %get-tuple-element.13, f32[2048]{0:T(1024)S(1)} %get-tuple-element.12), kind=kLoop, calls=%fused_computation.3 | loop fusion | flops 8386560 | bytes 16793600 | tf_op jit(solution)/shard_map/reduce_sum | solution.py:93
  176.9 1.8 fusion.45
  178.7 1.7 fusion.43
  180.4 0.4 multiply_reduce_fusion
  180.8 0.4 multiply_reduce_fusion.1
  181.3 0.4 convolution_bitcast_fusion
  181.6 0.4 convolution_bitcast_fusion.1
  182.0 1.5 pad_maximum_fusion
  184.1 5.5 %fusion.17 = bf16[3072,256]{1,0:T(8,128)(2,1)} fusion(s32[1024]{0:T(1024)S(1)} %get-tuple-element.5, s32[1024]{0:T(1024)S(1)} %get-tuple-element.4, f32[128,4,256]{2,1,0:T(4,128)S(1)} %reshape.354, f32[128,4,256]{2,1,0:T(4,128)S(1)} %reshape.353, f32[1024]{0:T(1024)S(1)} %mul.219), kind=kOutput, calls=%fused_computation.25 | convolution fusion | flops 1621622784 | bytes 2633728 | tf_op jit(solution)/shard_map/dot_general | solution.py:144
  189.7 9.7 %all-to-all-start.5 = ((bf16[32,96,256]{2,1,0:T(8,128)(2,1)}), bf16[32,96,256]{2,1,0:T(8,128)(2,1)S(1)}, u32[]{:S(2)}, u32[]{:S(2)}) async-start(bf16[32,96,256]{2,1,0:T(8,128)(2,1)} %bitcast.62), calls=%async_computation.6 | async-start | bytes 3145728 | tf_op jit(solution)/shard_map/all_to_all | solution.py:150
  199.5 1.5 convert_reduce_fusion
  201.2 60.8 %reduce-scatter.2.cloned.1.call-done = f32[128,256]{1,0:T(8,128)} async-done(((f32[2048,256]{1,0:T(8,128)}), f32[128,256]{1,0:T(8,128)}) %reduce-scatter.2.cloned.1.call-update) | async-done | bytes 131088 | tf_op jit(solution)/shard_map/reduce_scatter | solution.py:169
  262.0 1.6 reshape.351
  263.6 21.6 %all-to-all-start.3 = ((f32[32,4,256]{2,1,0:T(4,128)}), f32[32,4,256]{2,1,0:T(4,128)S(1)}, u32[]{:S(2)}, u32[]{:S(2)}) async-start(f32[32,4,256]{2,1,0:T(4,128)} %reshape.351), calls=%async_computation.4 | async-start | bytes 262144 | tf_op jit(solution)/shard_map/all_to_all | solution.py:189
  285.2 1.9 fusion.4
  287.1 8.9 %all-to-all-done.3 = f32[32,4,256]{2,1,0:T(4,128)S(1)} async-done(((f32[32,4,256]{2,1,0:T(4,128)}), f32[32,4,256]{2,1,0:T(4,128)S(1)}, u32[]{:S(2)}, u32[]{:S(2)}) %all-to-all-start.3) | async-done | bytes 131104 | tf_op jit(solution)/shard_map/all_to_all | solution.py:189
  296.2 0.6 broadcast_in_dim.46
  296.8 3.7 all-to-all-start.4
  300.5 1.1 pad_maximum_fusion.1
  301.7 8.8 %all-to-all-done.4 = bf16[32,4,256]{2,1,0:T(4,128)(2,1)S(1)} async-done(((bf16[32,4,256]{2,1,0:T(4,128)(2,1)}), bf16[32,4,256]{2,1,0:T(4,128)(2,1)S(1)}, u32[]{:S(2)}, u32[]{:S(2)}) %all-to-all-start.4) | async-done | bytes 65568 | tf_op jit(solution)/shard_map/all_to_all | solution.py:193
  310.5 4.5 %all-to-all-start.6 = ((f32[16,65,256]{2,1,0:T(8,128)}), f32[16,65,256]{2,1,0:T(8,128)S(1)}, u32[]{:S(2)}, u32[]{:S(2)}) async-start(f32[16,65,256]{2,1,0:T(8,128)} %pad_maximum_fusion.1), calls=%async_computation.7 | async-start | bytes 2359296 | tf_op jit(solution)/shard_map/all_to_all | solution.py:181
  314.9 0.8 dynamic_slice.16
  315.7 27.1 %all-to-all-done.6 = f32[16,65,256]{2,1,0:T(8,128)S(1)} async-done(((f32[16,65,256]{2,1,0:T(8,128)}), f32[16,65,256]{2,1,0:T(8,128)S(1)}, u32[]{:S(2)}, u32[]{:S(2)}) %all-to-all-start.6) | async-done | bytes 1064992 | tf_op jit(solution)/shard_map/all_to_all | solution.py:181
  343.5 44.6 %all_to_all.45 = bf16[16,192,256]{2,1,0:T(8,128)(2,1)S(1)} all-to-all(bf16[16,192,256]{2,1,0:T(8,128)(2,1)S(1)} %broadcast_in_dim.53), channel_id=1, replica_groups=mesh['dp'=16,'table'=32] {'dp'}, dimensions={0} | all-to-all | bytes 3145728 | tf_op jit(solution)/shard_map/all_to_all | solution.py:197
  388.2 1.1 slice.55
  389.2 1.5 slice.56
  (57 shorter events, 3.1 us)
Async XLA Ops:
  7.2 45.6 %copy-start = (bf16[1024,256]{1,0:T(8,128)(2,1)S(1)}, bf16[1024,256]{1,0:T(8,128)(2,1)}, u32[]{:S(2)}) copy-start(bf16[1024,256]{1,0:T(8,128)(2,1)} %param.7) | copy-start | bytes 1572868
  7.2 1.4 copy-start.1
  56.4 43.4 %all-to-all-start.1 = ((bf16[32,96,256]{2,1,0:T(8,128)(2,1)}), bf16[32,96,256]{2,1,0:T(8,128)(2,1)S(1)}, u32[]{:S(2)}, u32[]{:S(2)}) async-start(bf16[32,96,256]{2,1,0:T(8,128)(2,1)} %bitcast.64), calls=%async_computation.1 | async-start | bytes 3145728 | tf_op jit(solution)/shard_map/all_to_all | solution.py:60
  99.8 3.6 copy-start.2
  99.8 3.9 copy-start.4
  103.1 0.8 copy-start.6
  105.5 54.9 %all-to-all-start.2 = ((bf16[16,128,512]{2,1,0:T(8,128)(2,1)}), bf16[16,128,512]{2,1,0:T(8,128)(2,1)S(1)}, u32[]{:S(2)}, u32[]{:S(2)}) async-start(bf16[16,128,512]{2,1,0:T(8,128)(2,1)} %broadcast_in_dim.45), calls=%async_computation.2 | async-start | bytes 4194304 | tf_op jit(solution)/shard_map/all_to_all | solution.py:84
  112.4 149.6 %reduce-scatter.2.cloned.1.call-start = ((), (), s32[]{:S(2)}) async-start(), calls=%async_computation.9 | async-start | bytes 2228224 | tf_op jit(solution)/shard_map/reduce_scatter | solution.py:169
  176.8 3.6 copy-start.3
  176.8 4.0 %copy-start.5 = (bf16[1024,256]{1,0:T(8,128)(2,1)S(1)}, bf16[1024,256]{1,0:T(8,128)(2,1)}, u32[]{:S(2)}) copy-start(bf16[1024,256]{1,0:T(8,128)(2,1)} %param.10) | copy-start | bytes 1572868
  189.6 9.7 %copy-start.7 = (s32[2,1024]{1,0:T(2,128)S(1)}, s32[2,1024]{1,0:T(2,128)}, u32[]{:S(2)}) copy-start(s32[2,1024]{1,0:T(2,128)} %param.13) | copy-start | bytes 24580
  189.7 74.0 %all-to-all-start.5 = ((bf16[32,96,256]{2,1,0:T(8,128)(2,1)}), bf16[32,96,256]{2,1,0:T(8,128)(2,1)S(1)}, u32[]{:S(2)}, u32[]{:S(2)}) async-start(bf16[32,96,256]{2,1,0:T(8,128)(2,1)} %bitcast.62), calls=%async_computation.6 | async-start | bytes 3145728 | tf_op jit(solution)/shard_map/all_to_all | solution.py:150
  263.6 32.4 %all-to-all-start.3 = ((f32[32,4,256]{2,1,0:T(4,128)}), f32[32,4,256]{2,1,0:T(4,128)S(1)}, u32[]{:S(2)}, u32[]{:S(2)}) async-start(f32[32,4,256]{2,1,0:T(4,128)} %reshape.351), calls=%async_computation.4 | async-start | bytes 262144 | tf_op jit(solution)/shard_map/all_to_all | solution.py:189
  296.8 13.7 %all-to-all-start.4 = ((bf16[32,4,256]{2,1,0:T(4,128)(2,1)}), bf16[32,4,256]{2,1,0:T(4,128)(2,1)S(1)}, u32[]{:S(2)}, u32[]{:S(2)}) async-start(bf16[32,4,256]{2,1,0:T(4,128)(2,1)} %broadcast_in_dim.46), calls=%async_computation.5 | async-start | bytes 131072 | tf_op jit(solution)/shard_map/all_to_all | solution.py:193
  310.5 32.4 %all-to-all-start.6 = ((f32[16,65,256]{2,1,0:T(8,128)}), f32[16,65,256]{2,1,0:T(8,128)S(1)}, u32[]{:S(2)}, u32[]{:S(2)}) async-start(f32[16,65,256]{2,1,0:T(8,128)} %pad_maximum_fusion.1), calls=%async_computation.7 | async-start | bytes 2359296 | tf_op jit(solution)/shard_map/all_to_all | solution.py:181
Sparse Core Ops, SparseCore 0:
  183.6 78.4 reduce-scatter.1

commit v6 on v4

--- a/solution.py
+++ b/solution.py
@@ -38,7 +38,24 @@
     clip_norm = 0.9 * math.sqrt(2.0 * hidden_width + 400.0)
     requests = batch * slots * bags
     capacity = 3 * requests // (2 * shards)
-    positions = row_owner[lookup_ids.reshape(-1)]
+    flat_ids = lookup_ids.reshape(-1)
+    lane_width = 128
+    owner_blocks = row_owner.reshape(-1, lane_width)
+    block_match = (
+        (flat_ids // lane_width)[:, None]
+        == jnp.arange(owner_blocks.shape[0], dtype=jnp.int32)[None, :]
+    ).astype(jnp.bfloat16)
+    owner_high = jnp.dot(
+        block_match, (owner_blocks // 256).astype(jnp.bfloat16), preferred_element_type=jnp.float32
+    )
+    owner_low = jnp.dot(
+        block_match, (owner_blocks % 256).astype(jnp.bfloat16), preferred_element_type=jnp.float32
+    )
+    lane_match = (flat_ids % lane_width)[:, None] == jnp.arange(lane_width, dtype=jnp.int32)[None, :]
+    positions = jnp.sum(
+        jnp.where(lane_match, owner_high.astype(jnp.int32) * 256 + owner_low.astype(jnp.int32), 0),
+        axis=1,
+    )
     owners = positions // rows_dev
     local_rows = positions - owners * rows_dev
     one_hot = owners[:, None] == jnp.arange(shards, dtype=jnp.int32)[None, :]
@@ -49,7 +66,18 @@
     targets = owners * capacity + ranks
     slots_all = jnp.arange(shards * capacity, dtype=jnp.int32)
     slot_match = targets[:, None] == slots_all[None, :]
-    outgoing = jnp.max(jnp.where(slot_match, local_rows[:, None], -1), axis=0)
+    row_parts = jnp.stack(
+        [local_rows // 32, local_rows % 32, jnp.ones_like(local_rows)], axis=1
+    ).astype(jnp.bfloat16)
+    slot_parts = lax.dot_general(
+        slot_match.astype(jnp.bfloat16),
+        row_parts,
+        (((0,), (0,)), ((), ())),
+        preferred_element_type=jnp.float32,
+    ).astype(jnp.int32)
+    outgoing = jnp.where(
+        slot_parts[:, 2] > 0, slot_parts[:, 0] * 32 + slot_parts[:, 1], -1
+    )
     outgoing = outgoing.reshape(shards, capacity)
     incoming = lax.all_to_all(outgoing, "table", split_axis=0, concat_axis=0, tiled=True)
     flat_in = incoming.reshape(-1)

time: 393 us -> 384 us (0.977)
  local copies, waits for them, and re-layouts: 23.4 us -> 12.2 us
  matrix products: 30.5 us -> 38.4 us
  other arithmetic: 21.9 us -> 16.2 us
    gather x2 -> x0, local copies, waits for them, and re-layouts: 12.2 us -> none  [body(): positions = row_owner[lookup_ids.reshape(-1)]]
    dot_general x0 -> x3, matrix products: none -> 7.89 us  [the longest x1 4.41 us: body(): lax.dot_general(slot_match.astype(jnp.bfloat16), row_parts, (((0,), (0,))...]
    reduce_max x1 -> x0, other arithmetic: 5.89 us -> none  [body(): outgoing = jnp.max(jnp.where(slot_match, local_rows[:, None], -1), axis=0)]
where the time goes in v6:
time: 384 us; the launch traced here: 383 us
  blocking collectives  144 us (38%)
  waiting for transfers between devices  139 us (36%)
  matrix products  38.4 us (10%)
  starting transfers between devices  32.3 us (8%)
  other arithmetic  16.2 us (4%)
  local copies, waits for them, and re-layouts  12.2 us (3%)
    all_to_all x1, blocking collectives, body(): packed = jnp.sum(lax.all_to_all(packed, 'dp', 0, 0, tiled=True), axis=0)  79.2 us
    all_to_all x1, waiting for transfers between devices, body(): lax.all_to_all(jnp.broadcast_to(both[None], (n_dp,) + both.shape), 'dp',...  45.7 us
    all_to_all x1, blocking collectives, body(): lax.all_to_all(jnp.broadcast_to(finished[None], (n_dp,) + finished.shape)...  41.3 us
    all_to_all x1, waiting for transfers between devices, body(): lax.all_to_all(fetched.reshape(shards, capacity, emb_width), 'table', spl...  37.1 us
    all_to_all x1, waiting for transfers between devices, body(): lax.all_to_all(grad_out.reshape(shards, capacity, emb_width), 'table', sp...  36.6 us
    all_to_all x1, blocking collectives, body(): lax.all_to_all(outgoing, 'table', split_axis=0, concat_axis=0, tiled=True)  23.6 us
    all_to_all x1, waiting for transfers between devices, body(): lax.all_to_all(jnp.broadcast_to(part[None], (shards,) + part.shape), 'tab...  9.76 us
    all_to_all x1, starting transfers between devices, body(): lax.all_to_all(grad_out.reshape(shards, capacity, emb_width), 'table', sp...  9.69 us
  transfers between devices with their start and end apart: 5, of which 5 were waited for; matrix products, arithmetic and copies ran while one was open for 2% of the time, Pallas kernels for 0%

profile of v6, /device:TPU:1, one launch (start us, length us, event | category | flops | bytes accessed | tf_op | source)
XLA Modules:
  0.0 383.2 jit_solution(639930702103262436)
XLA Ops:
  0.6 1.0 copy.18
  1.6 0.3 reshape.512
  1.9 1.6 fusion.26
  3.5 1.9 fusion.31
  5.4 1.5 fusion.37
  7.2 4.4 %fusion.23 = s32[3072,3]{0,1:T(4,128)S(1)} fusion(s32[2048]{0:T(1024)S(1)} %multiply_add_fusion.1, bf16[2048,1]{0,1:T(2,128)(2,1)S(1)} %fusion.98, bf16[2048,1]{0,1:T(2,128)(2,1)S(1)} %get-tuple-element.6, bf16[3]{0:T(256)(128)(2,1)S(1)} %pad.13.clone), kind=kOutput, calls=%fused_computation.27 | convolution fusion | flops 44086272 | bytes 53254 | tf_op jit(solution)/shard_map/dot_general | solution.py:72
  11.7 23.6 %all_to_all.41 = s32[32,1,96]{2,1,0:T(1,128)S(1)} all-to-all(s32[32,1,96]{2,1,0:T(1,128)S(1)} %bitcast.98), channel_id=1, replica_groups=mesh['dp'=16,'table'=32] {'table'}, dimensions={0} | all-to-all | bytes 24576 | tf_op jit(solution)/shard_map/all_to_all | solution.py:82
  35.3 0.5 broadcast.744
  35.8 0.7 reduce.19
  36.6 3.6 fusion.22
  40.2 4.2 %all-to-all-start.1 = ((bf16[32,96,256]{2,1,0:T(8,128)(2,1)}), bf16[32,96,256]{2,1,0:T(8,128)(2,1)S(1)}, u32[]{:S(2)}, u32[]{:S(2)}) async-start(bf16[32,96,256]{2,1,0:T(8,128)(2,1)} %bitcast.92), calls=%async_computation.1 | async-start | bytes 3145728 | tf_op jit(solution)/shard_map/all_to_all | solution.py:88
  44.5 0.5 reduce_sum.113
  44.9 0.5 convert_element_type.150
  45.4 0.3 fusion.46
  45.8 0.5 slice_reduce_fusion.1
  46.3 37.1 %all-to-all-done.1 = bf16[32,96,256]{2,1,0:T(8,128)(2,1)S(1)} async-done(((bf16[32,96,256]{2,1,0:T(8,128)(2,1)}), bf16[32,96,256]{2,1,0:T(8,128)(2,1)S(1)}, u32[]{:S(2)}, u32[]{:S(2)}) %all-to-all-start.1) | async-done | bytes 1572896 | tf_op jit(solution)/shard_map/all_to_all | solution.py:88
  83.4 3.3 fusion.32
  86.9 0.6 copy-done.5
  88.1 1.5 broadcast_in_dim.37
  89.7 6.9 %all-to-all-start.2 = ((bf16[16,128,512]{2,1,0:T(8,128)(2,1)}), bf16[16,128,512]{2,1,0:T(8,128)(2,1)S(1)}, u32[]{:S(2)}, u32[]{:S(2)}) async-start(bf16[16,128,512]{2,1,0:T(8,128)(2,1)} %broadcast_in_dim.37), calls=%async_computation.2 | async-start | bytes 4194304 | tf_op jit(solution)/shard_map/all_to_all | solution.py:112
  96.6 2.4 multiply_reduce_fusion.3
  99.0 45.7 %all-to-all-done.2 = bf16[16,128,512]{2,1,0:T(8,128)(2,1)S(1)} async-done(((bf16[16,128,512]{2,1,0:T(8,128)(2,1)}), bf16[16,128,512]{2,1,0:T(8,128)(2,1)S(1)}, u32[]{:S(2)}, u32[]{:S(2)}) %all-to-all-start.2) | async-done | bytes 2097184 | tf_op jit(solution)/shard_map/all_to_all | solution.py:112
  145.0 8.1 %fusion.121 = (f32[2048]{0:T(1024)S(1)}, f32[2048,2048]{0,1:T(8,128)}) fusion(bf16[2048,256]{1,0:T(8,128)(2,1)S(1)} %bitcast.81, bf16[2048,256]{1,0:T(8,128)(2,1)S(1)} %bitcast.83), kind=kOutput, calls=%fused_computation.199 | convolution fusion | flops 2155870208 | bytes 18882560 | tf_op jit(solution)/shard_map/dot_general | solution.py:117
  153.1 8.1 %exponential_reduce_fusion = f32[2048]{0:T(1024)S(1)} fusion(f32[2048,2048]{0,1:T(8,128)} %get-tuple-element.15, f32[2048]{0:T(1024)S(1)} %get-tuple-element.14), kind=kLoop, calls=%fused_computation.2 | loop fusion | flops 8386560 | bytes 16793600 | tf_op jit(solution)/shard_map/reduce_sum | solution.py:121
  161.2 1.8 fusion.54
  163.0 1.7 fusion.52
  164.8 0.4 multiply_reduce_fusion
  165.4 0.4 multiply_reduce_fusion.1
  166.3 5.3 %fusion.19 = bf16[3072,256]{1,0:T(8,128)(2,1)} fusion(s32[1024]{0:T(1024)S(1)} %get-tuple-element.5, s32[1024]{0:T(1024)S(1)} %get-tuple-element.4, f32[128,4,256]{2,1,0:T(4,128)S(1)} %reshape.523, f32[128,4,256]{2,1,0:T(4,128)S(1)} %reshape.522, f32[1024]{0:T(1024)S(1)} %mul.240), kind=kOutput, calls=%fused_computation.25 | convolution fusion | flops 1621622784 | bytes 2633728 | tf_op jit(solution)/shard_map/dot_general | solution.py:172
  171.5 9.7 %all-to-all-start.3 = ((bf16[32,96,256]{2,1,0:T(8,128)(2,1)}), bf16[32,96,256]{2,1,0:T(8,128)(2,1)}, u32[]{:S(2)}, u32[]{:S(2)}) async-start(bf16[32,96,256]{2,1,0:T(8,128)(2,1)} %bitcast.12), calls=%async_computation.3 | async-start | bytes 3145728 | tf_op jit(solution)/shard_map/all_to_all | solution.py:178
  181.3 1.5 convert_reduce_fusion
  183.0 0.4 convolution_bitcast_fusion
  183.3 0.4 convolution_bitcast_fusion.1
  183.9 36.6 %all-to-all-done.3 = bf16[32,96,256]{2,1,0:T(8,128)(2,1)} async-done(((bf16[32,96,256]{2,1,0:T(8,128)(2,1)}), bf16[32,96,256]{2,1,0:T(8,128)(2,1)}, u32[]{:S(2)}, u32[]{:S(2)}) %all-to-all-start.3) | async-done | bytes 1572896 | tf_op jit(solution)/shard_map/all_to_all | solution.py:178
  220.5 3.3 fusion.6
  223.8 0.3 pad_maximum_fusion
  224.1 79.2 %all_to_all.42 = f32[16,193,256]{2,1,0:T(8,128)} all-to-all(f32[16,193,256]{2,1,0:T(8,128)S(1)} %pad_maximum_fusion), channel_id=1, replica_groups=mesh['dp'=16,'table'=32] {'dp'}, dimensions={0} | all-to-all | bytes 6324224 | tf_op jit(solution)/shard_map/all_to_all | solution.py:207
  303.3 2.1 reduce_sum.124
  305.4 0.7 reshape.526
  306.1 7.7 %all-to-all-start.5 = ((f32[32,4,256]{2,1,0:T(4,128)}), f32[32,4,256]{2,1,0:T(4,128)S(1)}, u32[]{:S(2)}, u32[]{:S(2)}) async-start(f32[32,4,256]{2,1,0:T(4,128)} %reshape.526), calls=%async_computation.5 | async-start | bytes 262144 | tf_op jit(solution)/shard_map/all_to_all | solution.py:215
  313.9 0.8 dynamic_slice.16
  315.0 9.6 %all-to-all-done.5 = f32[32,4,256]{2,1,0:T(4,128)S(1)} async-done(((f32[32,4,256]{2,1,0:T(4,128)}), f32[32,4,256]{2,1,0:T(4,128)S(1)}, u32[]{:S(2)}, u32[]{:S(2)}) %all-to-all-start.5) | async-done | bytes 131104 | tf_op jit(solution)/shard_map/all_to_all | solution.py:215
  324.8 0.6 broadcast_in_dim.45
  325.4 3.7 all-to-all-start.6
  329.3 9.8 %all-to-all-done.6 = bf16[32,4,256]{2,1,0:T(4,128)(2,1)S(1)} async-done(((bf16[32,4,256]{2,1,0:T(4,128)(2,1)}), bf16[32,4,256]{2,1,0:T(4,128)(2,1)S(1)}, u32[]{:S(2)}, u32[]{:S(2)}) %all-to-all-start.6) | async-done | bytes 65568 | tf_op jit(solution)/shard_map/all_to_all | solution.py:219
  339.3 41.3 %all_to_all.43 = bf16[16,192,256]{2,1,0:T(8,128)(2,1)S(1)} all-to-all(bf16[16,192,256]{2,1,0:T(8,128)(2,1)S(1)} %broadcast_in_dim.49), channel_id=1, replica_groups=mesh['dp'=16,'table'=32] {'dp'}, dimensions={0} | all-to-all | bytes 3145728 | tf_op jit(solution)/shard_map/all_to_all | solution.py:223
  380.6 1.1 slice.73
  381.7 1.5 slice.74
  (56 shorter events, 3.4 us)
Async XLA Ops:
  0.6 35.9 %copy-start = (bf16[1024,256]{1,0:T(8,128)(2,1)S(1)}, bf16[1024,256]{1,0:T(8,128)(2,1)}, u32[]{:S(2)}) copy-start(bf16[1024,256]{1,0:T(8,128)(2,1)} %param.7) | copy-start | bytes 1572868
  40.2 43.2 %all-to-all-start.1 = ((bf16[32,96,256]{2,1,0:T(8,128)(2,1)}), bf16[32,96,256]{2,1,0:T(8,128)(2,1)S(1)}, u32[]{:S(2)}, u32[]{:S(2)}) async-start(bf16[32,96,256]{2,1,0:T(8,128)(2,1)} %bitcast.92), calls=%async_computation.1 | async-start | bytes 3145728 | tf_op jit(solution)/shard_map/all_to_all | solution.py:88
  83.4 4.2 %copy-start.1 = (bf16[1024,256]{1,0:T(8,128)(2,1)S(1)}, bf16[1024,256]{1,0:T(8,128)(2,1)}, u32[]{:S(2)}) copy-start(bf16[1024,256]{1,0:T(8,128)(2,1)} %param.11) | copy-start | bytes 1572868
  83.4 4.5 %copy-start.3 = (bf16[1024,256]{1,0:T(8,128)(2,1)S(1)}, bf16[1024,256]{1,0:T(8,128)(2,1)}, u32[]{:S(2)}) copy-start(bf16[1024,256]{1,0:T(8,128)(2,1)} %param.10) | copy-start | bytes 1572868
  86.7 0.8 copy-start.5
  89.7 55.1 %all-to-all-start.2 = ((bf16[16,128,512]{2,1,0:T(8,128)(2,1)}), bf16[16,128,512]{2,1,0:T(8,128)(2,1)S(1)}, u32[]{:S(2)}, u32[]{:S(2)}) async-start(bf16[16,128,512]{2,1,0:T(8,128)(2,1)} %broadcast_in_dim.37), calls=%async_computation.2 | async-start | bytes 4194304 | tf_op jit(solution)/shard_map/all_to_all | solution.py:112
  161.2 3.6 copy-start.2
  161.2 4.2 %copy-start.4 = (bf16[1024,256]{1,0:T(8,128)(2,1)S(1)}, bf16[1024,256]{1,0:T(8,128)(2,1)}, u32[]{:S(2)}) copy-start(bf16[1024,256]{1,0:T(8,128)(2,1)} %param.10) | copy-start | bytes 1572868
  171.5 48.9 %all-to-all-start.3 = ((bf16[32,96,256]{2,1,0:T(8,128)(2,1)}), bf16[32,96,256]{2,1,0:T(8,128)(2,1)}, u32[]{:S(2)}, u32[]{:S(2)}) async-start(bf16[32,96,256]{2,1,0:T(8,128)(2,1)} %bitcast.12), calls=%async_computation.3 | async-start | bytes 3145728 | tf_op jit(solution)/shard_map/all_to_all | solution.py:178
  303.3 10.6 %copy-start.6 = (s32[2,1024]{1,0:T(2,128)S(1)}, s32[2,1024]{1,0:T(2,128)}, u32[]{:S(2)}) copy-start(s32[2,1024]{1,0:T(2,128)} %param.13) | copy-start | bytes 24580
  306.1 18.5 %all-to-all-start.5 = ((f32[32,4,256]{2,1,0:T(4,128)}), f32[32,4,256]{2,1,0:T(4,128)S(1)}, u32[]{:S(2)}, u32[]{:S(2)}) async-start(f32[32,4,256]{2,1,0:T(4,128)} %reshape.526), calls=%async_computation.5 | async-start | bytes 262144 | tf_op jit(solution)/shard_map/all_to_all | solution.py:215
  325.4 13.7 %all-to-all-start.6 = ((bf16[32,4,256]{2,1,0:T(4,128)(2,1)}), bf16[32,4,256]{2,1,0:T(4,128)(2,1)S(1)}, u32[]{:S(2)}, u32[]{:S(2)}) async-start(bf16[32,4,256]{2,1,0:T(4,128)(2,1)} %broadcast_in_dim.45), calls=%async_computation.6 | async-start | bytes 131072 | tf_op jit(solution)/shard_map/all_to_all | solution.py:219

commit v7 on v6

--- a/solution.py
+++ b/solution.py
@@ -190,13 +190,18 @@
     )
     row_count = jnp.sum(row_match.astype(jnp.float32), axis=0)
     shard_rows = rows_dev // n_dp
-    tower_rows = 2 * hidden_width
-    dp_rows = tower_rows // n_dp
-    own_rows = dp_rows // shards
     count_lanes = emb_width // shard_rows
+    core = table_index % 2
+    partner = [(i, i ^ 1) for i in range(shards)]
+    kept = jnp.where(core == 0, tower_part[0], tower_part[1])
+    sent = jnp.where(core == 0, tower_part[1], tower_part[0])
+    chip_sum = kept + lax.ppermute(sent, "table", partner)
+    dp_rows = hidden_width // n_dp
+    chips = shards // 2
+    own_rows = dp_rows // chips
     packed = jnp.concatenate(
         [
-            tower_part.reshape(n_dp, dp_rows, out_width),
+            chip_sum.reshape(n_dp, dp_rows, out_width),
             row_sum.reshape(n_dp, shard_rows, emb_width),
             jnp.broadcast_to(
                 row_count.reshape(n_dp, 1, shard_rows, 1), (n_dp, 1, shard_rows, count_lanes)
@@ -211,20 +216,27 @@
     own_update = own_sum / clip_norm + NOISE_MULT * jnp.where(
         own_count[:, None] > 0.0, hashed_noise(own_seeds, emb_width), 0.0
     )
-    part = packed[:dp_rows].reshape(shards, own_rows, out_width)
+    chunks = packed[:dp_rows].reshape(chips, 1, own_rows, out_width)
+    same_core = jnp.arange(2, dtype=jnp.int32)[None, :, None, None] == core
+    part = jnp.where(same_core, chunks, 0.0).reshape(shards, own_rows, out_width)
     part = jnp.sum(lax.all_to_all(part, "table", 0, 0, tiled=True), axis=0)
-    first_row = dp_index * dp_rows + table_index * own_rows
-    tower_seed_rows = lax.dynamic_slice_in_dim(tower_seeds.reshape(tower_rows), first_row, own_rows)
+    first_row = core * hidden_width + dp_index * dp_rows + (table_index // 2) * own_rows
+    tower_seed_rows = lax.dynamic_slice_in_dim(
+        tower_seeds.reshape(2 * hidden_width), first_row, own_rows
+    )
     part = part / clip_norm + NOISE_MULT * hashed_noise(tower_seed_rows, out_width)
     part = lax.all_to_all(
         jnp.broadcast_to(part[None], (shards,) + part.shape), "table", 0, 0, tiled=True
-    ).reshape(dp_rows, out_width)
+    )
+    part = part.reshape(chips, 2, own_rows, out_width).transpose(1, 0, 2, 3)
+    part = part.reshape(2 * dp_rows, out_width)
     finished = jnp.concatenate([part, own_update], axis=0).astype(jnp.bfloat16)
     finished = lax.all_to_all(
         jnp.broadcast_to(finished[None], (n_dp,) + finished.shape), "dp", 0, 0, tiled=True
     ).astype(jnp.float32)
-    tower_update = finished[:, :dp_rows].reshape(2, hidden_width, out_width)
-    table_update = finished[:, dp_rows:].reshape(rows_dev, emb_width)
+    tower_update = finished[:, : 2 * dp_rows].reshape(n_dp, 2, dp_rows, out_width)
+    tower_update = tower_update.transpose(1, 0, 2, 3).reshape(2, hidden_width, out_width)
+    table_update = finished[:, 2 * dp_rows :].reshape(rows_dev, emb_width)
     return (table_update, tower_update)
 
 

time: 384 us -> 360 us (0.938)
  blocking collectives: 144 us -> 78.9 us
  waiting for transfers between devices: 139 us -> 176 us
    all_to_all x1, blocking collectives: 79.2 us -> 13.1 us  [body(): lax.all_to_all(jnp.broadcast_to(part[None], (shards,) + part.shape), 'tab...]
    all_to_all x1, waiting for transfers between devices: 9.76 us -> 50.8 us  [body(): packed = jnp.sum(lax.all_to_all(packed, 'dp', 0, 0, tiled=True), axis=0)]
    all_to_all x1, waiting for transfers between devices: 36.6 us -> 30.3 us  [body(): lax.all_to_all(grad_out.reshape(shards, capacity, emb_width), 'table', sp...]
  transfers between devices with their start and end apart: 5 -> 6, of which waited for: 5 -> 6; matrix products, arithmetic and copies ran while one was open for 2% -> 3% of each run, Pallas kernels for 0% -> 0%
where the time goes in v7:
time: 360 us; the launch traced here: 359 us
  waiting for transfers between devices  176 us (49%)
  blocking collectives  78.9 us (22%)
  matrix products  39.5 us (11%)
  starting transfers between devices  34.8 us (10%)
  other arithmetic  18.5 us (5%)
  local copies, waits for them, and re-layouts  10.5 us (3%)
    all_to_all x1, waiting for transfers between devices, body(): packed = jnp.sum(lax.all_to_all(packed, 'dp', 0, 0, tiled=True), axis=0)  50.8 us
    all_to_all x1, waiting for transfers between devices, body(): lax.all_to_all(jnp.broadcast_to(both[None], (n_dp,) + both.shape), 'dp',...  45.7 us
    all_to_all x1, blocking collectives, body(): lax.all_to_all(jnp.broadcast_to(finished[None], (n_dp,) + finished.shape)...  42.2 us
    all_to_all x1, waiting for transfers between devices, body(): lax.all_to_all(fetched.reshape(shards, capacity, emb_width), 'table', spl...  37.1 us
    all_to_all x1, waiting for transfers between devices, body(): lax.all_to_all(grad_out.reshape(shards, capacity, emb_width), 'table', sp...  30.3 us
    all_to_all x1, blocking collectives, body(): lax.all_to_all(outgoing, 'table', split_axis=0, concat_axis=0, tiled=True)  23.6 us
    all_to_all x1, blocking collectives, body(): lax.all_to_all(jnp.broadcast_to(part[None], (shards,) + part.shape), 'tab...  13.1 us
    all_to_all x1, waiting for transfers between devices, body(): part = jnp.sum(lax.all_to_all(part, 'table', 0, 0, tiled=True), axis=0)  10.6 us
  transfers between devices with their start and end apart: 6, of which 6 were waited for; matrix products, arithmetic and copies ran while one was open for 3% of the time, Pallas kernels for 0%

profile of v7, /device:TPU:1, one launch (start us, length us, event | category | flops | bytes accessed | tf_op | source)
XLA Modules:
  0.0 358.9 jit_solution(13821846786718625684)
XLA Ops:
  0.6 1.0 copy.29
  1.6 0.3 reshape.526
  1.9 1.6 fusion.26
  3.5 1.9 fusion.31
  5.4 1.5 fusion.37
  7.2 4.4 %fusion.23 = s32[3072,3]{0,1:T(4,128)S(1)} fusion(s32[2048]{0:T(1024)S(1)} %multiply_add_fusion.1, bf16[2048,1]{0,1:T(2,128)(2,1)S(1)} %fusion.100, bf16[2048,1]{0,1:T(2,128)(2,1)S(1)} %get-tuple-element.6, bf16[3]{0:T(256)(128)(2,1)S(1)} %pad.11.clone), kind=kOutput, calls=%fused_computation.27 | convolution fusion | flops 44086272 | bytes 53254 | tf_op jit(solution)/shard_map/dot_general | solution.py:72
  11.7 23.6 %all_to_all.41 = s32[32,1,96]{2,1,0:T(1,128)S(1)} all-to-all(s32[32,1,96]{2,1,0:T(1,128)S(1)} %bitcast.104), channel_id=1, replica_groups=mesh['dp'=16,'table'=32] {'table'}, dimensions={0} | all-to-all | bytes 24576 | tf_op jit(solution)/shard_map/all_to_all | solution.py:82
  35.3 0.5 broadcast.755
  35.8 0.7 reduce.19
  36.6 3.6 %fusion.22 = bf16[3072,256]{1,0:T(8,128)(2,1)} fusion(bf16[1024,256]{1,0:T(8,128)(2,1)S(1)} %copy-done, s32[3072]{0:T(1024)S(1)} %eq.164), kind=kOutput, calls=%fused_computation.26 | convolution fusion | flops 1614544896 | bytes 2109440 | tf_op jit(solution)/shard_map/dot_general | solution.py:87
  40.2 4.2 %all-to-all-start.1 = ((bf16[32,96,256]{2,1,0:T(8,128)(2,1)}), bf16[32,96,256]{2,1,0:T(8,128)(2,1)S(1)}, u32[]{:S(2)}, u32[]{:S(2)}) async-start(bf16[32,96,256]{2,1,0:T(8,128)(2,1)} %bitcast.97), calls=%async_computation.1 | async-start | bytes 3145728 | tf_op jit(solution)/shard_map/all_to_all | solution.py:88
  44.5 0.5 reduce_sum.113
  44.9 0.5 convert_element_type.150
  45.4 0.3 fusion.46
  45.7 0.5 slice_reduce_fusion.1
  46.2 37.1 %all-to-all-done.1 = bf16[32,96,256]{2,1,0:T(8,128)(2,1)S(1)} async-done(((bf16[32,96,256]{2,1,0:T(8,128)(2,1)}), bf16[32,96,256]{2,1,0:T(8,128)(2,1)S(1)}, u32[]{:S(2)}, u32[]{:S(2)}) %all-to-all-start.1) | async-done | bytes 1572896 | tf_op jit(solution)/shard_map/all_to_all | solution.py:88
  83.4 3.3 fusion.32
  87.5 1.5 broadcast_in_dim.114
  89.1 7.0 %all-to-all-start.2 = ((bf16[16,128,512]{2,1,0:T(8,128)(2,1)}), bf16[16,128,512]{2,1,0:T(8,128)(2,1)S(1)}, u32[]{:S(2)}, u32[]{:S(2)}) async-start(bf16[16,128,512]{2,1,0:T(8,128)(2,1)} %broadcast_in_dim.114), calls=%async_computation.2 | async-start | bytes 4194304 | tf_op jit(solution)/shard_map/all_to_all | solution.py:112
  96.0 2.4 multiply_reduce_fusion.3
  98.4 45.7 %all-to-all-done.2 = bf16[16,128,512]{2,1,0:T(8,128)(2,1)S(1)} async-done(((bf16[16,128,512]{2,1,0:T(8,128)(2,1)}), bf16[16,128,512]{2,1,0:T(8,128)(2,1)S(1)}, u32[]{:S(2)}, u32[]{:S(2)}) %all-to-all-start.2) | async-done | bytes 2097184 | tf_op jit(solution)/shard_map/all_to_all | solution.py:112
  144.4 8.1 %fusion.124 = (f32[2048]{0:T(1024)S(1)}, f32[2048,2048]{0,1:T(8,128)}) fusion(bf16[2048,256]{1,0:T(8,128)(2,1)S(1)} %bitcast.85, bf16[2048,256]{1,0:T(8,128)(2,1)S(1)} %bitcast.87), kind=kOutput, calls=%fused_computation.203 | convolution fusion | flops 2155870208 | bytes 18882560 | tf_op jit(solution)/shard_map/dot_general | solution.py:117
  152.5 8.1 %exponential_reduce_fusion = f32[2048]{0:T(1024)S(1)} fusion(f32[2048,2048]{0,1:T(8,128)} %get-tuple-element.17, f32[2048]{0:T(1024)S(1)} %get-tuple-element.16), kind=kLoop, calls=%fused_computation.2 | loop fusion | flops 8386560 | bytes 16793600 | tf_op jit(solution)/shard_map/reduce_sum | solution.py:121
  160.6 1.8 fusion.54
  162.4 1.7 fusion.52
  164.2 0.4 multiply_reduce_fusion
  164.8 0.4 multiply_reduce_fusion.1
  165.7 5.3 %fusion.19 = bf16[3072,256]{1,0:T(8,128)(2,1)} fusion(s32[1024]{0:T(1024)S(1)} %get-tuple-element.5, s32[1024]{0:T(1024)S(1)} %get-tuple-element.4, f32[128,4,256]{2,1,0:T(4,128)S(1)} %reshape.537, f32[128,4,256]{2,1,0:T(4,128)S(1)} %reshape.536, f32[1024]{0:T(1024)S(1)} %mul.243), kind=kOutput, calls=%fused_computation.25 | convolution fusion | flops 1621622784 | bytes 2633728 | tf_op jit(solution)/shard_map/dot_general | solution.py:172
  171.0 9.7 %all-to-all-start.3 = ((bf16[32,96,256]{2,1,0:T(8,128)(2,1)}), bf16[32,96,256]{2,1,0:T(8,128)(2,1)}, u32[]{:S(2)}, u32[]{:S(2)}) async-start(bf16[32,96,256]{2,1,0:T(8,128)(2,1)} %bitcast.10), calls=%async_computation.3 | async-start | bytes 3145728 | tf_op jit(solution)/shard_map/all_to_all | solution.py:178
  180.7 0.4 fusion.78
  181.0 1.3 broadcast_select_fusion
  182.4 2.2 collective-permute-start
  184.6 1.5 convert_reduce_fusion
  186.3 0.9 collective-permute-done
  187.3 2.4 select_add_fusion
  189.6 30.3 %all-to-all-done.3 = bf16[32,96,256]{2,1,0:T(8,128)(2,1)} async-done(((bf16[32,96,256]{2,1,0:T(8,128)(2,1)}), bf16[32,96,256]{2,1,0:T(8,128)(2,1)}, u32[]{:S(2)}, u32[]{:S(2)}) %all-to-all-start.3) | async-done | bytes 1572896 | tf_op jit(solution)/shard_map/all_to_all | solution.py:178
  219.9 3.4 fusion.6
  223.3 1.6 pad_maximum_fusion
  224.9 3.9 %all-to-all-start.4 = ((f32[16,129,256]{2,1,0:T(8,128)}), f32[16,129,256]{2,1,0:T(8,128)S(1)}, u32[]{:S(2)}, u32[]{:S(2)}) async-start(f32[16,129,256]{2,1,0:T(8,128)} %pad_maximum_fusion), calls=%async_computation.4 | async-start | bytes 4456448 | tf_op jit(solution)/shard_map/all_to_all | solution.py:212
  228.9 0.8 dynamic_slice.16
  229.6 50.8 %all-to-all-done.4 = f32[16,129,256]{2,1,0:T(8,128)S(1)} async-done(((f32[16,129,256]{2,1,0:T(8,128)}), f32[16,129,256]{2,1,0:T(8,128)S(1)}, u32[]{:S(2)}, u32[]{:S(2)}) %all-to-all-start.4) | async-done | bytes 2113568 | tf_op jit(solution)/shard_map/all_to_all | solution.py:212
  281.1 0.8 bitcast_select_fusion
  281.8 7.9 %all-to-all-start.5 = ((f32[32,4,256]{2,1,0:T(4,128)}), f32[32,4,256]{2,1,0:T(4,128)S(1)}, u32[]{:S(2)}, u32[]{:S(2)}) async-start(f32[32,4,256]{2,1,0:T(4,128)} %bitcast_select_fusion), calls=%async_computation.5 | async-start | bytes 262144 | tf_op jit(solution)/shard_map/all_to_all | solution.py:222
  289.8 10.6 %all-to-all-done.5 = f32[32,4,256]{2,1,0:T(4,128)S(1)} async-done(((f32[32,4,256]{2,1,0:T(4,128)}), f32[32,4,256]{2,1,0:T(4,128)S(1)}, u32[]{:S(2)}, u32[]{:S(2)}) %all-to-all-start.5) | async-done | bytes 131104 | tf_op jit(solution)/shard_map/all_to_all | solution.py:222
  300.6 13.1 %all_to_all.42 = bf16[32,4,256]{2,1,0:T(4,128)(2,1)S(1)} all-to-all(bf16[32,4,256]{2,1,0:T(4,128)(2,1)S(1)} %broadcast_in_dim.122), channel_id=1, replica_groups=mesh['dp'=16,'table'=32] {'table'}, dimensions={0} | all-to-all | bytes 131072 | tf_op jit(solution)/shard_map/all_to_all | solution.py:228
  314.0 42.2 %all_to_all.43 = bf16[16,192,256]{2,1,0:T(8,128)(2,1)S(1)} all-to-all(bf16[16,192,256]{2,1,0:T(8,128)(2,1)S(1)} %broadcast_in_dim.126), channel_id=1, replica_groups=mesh['dp'=16,'table'=32] {'dp'}, dimensions={0} | all-to-all | bytes 3145728 | tf_op jit(solution)/shard_map/all_to_all | solution.py:234
  356.4 1.5 copy.35
  357.8 1.1 slice.73
  (65 shorter events, 3.8 us)
Async XLA Ops:
  0.6 35.9 %copy-start = (bf16[1024,256]{1,0:T(8,128)(2,1)S(1)}, bf16[1024,256]{1,0:T(8,128)(2,1)}, u32[]{:S(2)}) copy-start(bf16[1024,256]{1,0:T(8,128)(2,1)} %param.7) | copy-start | bytes 1572868
  40.2 43.2 %all-to-all-start.1 = ((bf16[32,96,256]{2,1,0:T(8,128)(2,1)}), bf16[32,96,256]{2,1,0:T(8,128)(2,1)S(1)}, u32[]{:S(2)}, u32[]{:S(2)}) async-start(bf16[32,96,256]{2,1,0:T(8,128)(2,1)} %bitcast.97), calls=%async_computation.1 | async-start | bytes 3145728 | tf_op jit(solution)/shard_map/all_to_all | solution.py:88
  83.4 3.6 %copy-start.2 = (bf16[1024,256]{1,0:T(8,128)(2,1)S(1)}, bf16[1024,256]{1,0:T(8,128)(2,1)}, u32[]{:S(2)}) copy-start(bf16[1024,256]{1,0:T(8,128)(2,1)} %param.11) | copy-start | bytes 1572868
  83.4 3.9 %copy-start.4 = (bf16[1024,256]{1,0:T(8,128)(2,1)S(1)}, bf16[1024,256]{1,0:T(8,128)(2,1)}, u32[]{:S(2)}) copy-start(bf16[1024,256]{1,0:T(8,128)(2,1)} %param.10) | copy-start | bytes 1572868
  86.7 0.8 copy-start.6
  89.1 55.1 %all-to-all-start.2 = ((bf16[16,128,512]{2,1,0:T(8,128)(2,1)}), bf16[16,128,512]{2,1,0:T(8,128)(2,1)S(1)}, u32[]{:S(2)}, u32[]{:S(2)}) async-start(bf16[16,128,512]{2,1,0:T(8,128)(2,1)} %broadcast_in_dim.114), calls=%async_computation.2 | async-start | bytes 4194304 | tf_op jit(solution)/shard_map/all_to_all | solution.py:112
  160.6 3.6 %copy-start.3 = (bf16[1024,256]{1,0:T(8,128)(2,1)S(1)}, bf16[1024,256]{1,0:T(8,128)(2,1)}, u32[]{:S(2)}) copy-start(bf16[1024,256]{1,0:T(8,128)(2,1)} %param.11) | copy-start | bytes 1572868
  160.6 4.2 %copy-start.5 = (bf16[1024,256]{1,0:T(8,128)(2,1)S(1)}, bf16[1024,256]{1,0:T(8,128)(2,1)}, u32[]{:S(2)}) copy-start(bf16[1024,256]{1,0:T(8,128)(2,1)} %param.10) | copy-start | bytes 1572868
  171.0 48.9 %all-to-all-start.3 = ((bf16[32,96,256]{2,1,0:T(8,128)(2,1)}), bf16[32,96,256]{2,1,0:T(8,128)(2,1)}, u32[]{:S(2)}, u32[]{:S(2)}) async-start(bf16[32,96,256]{2,1,0:T(8,128)(2,1)} %bitcast.10), calls=%async_computation.3 | async-start | bytes 3145728 | tf_op jit(solution)/shard_map/all_to_all | solution.py:178
  182.4 4.9 %collective-permute-start = (f32[1024,256]{1,0:T(8,128)}, f32[1024,256]{1,0:T(8,128)}, u32[]{:S(2)}, u32[]{:S(2)}) collective-permute-start(f32[1024,256]{1,0:T(8,128)} %get-tuple-element.26), channel_id=1, source_target_pairs={{0,1},{1,0},{2,3},{3,2},{4,5},{5,4},{6,7},{7,6},{8,9},{9,8},{10,11... | collective-permute-start | bytes 3145736 | tf_op jit(solution)/shard_map/ppermute | solution.py:198
  219.9 3.4 copy-start.1
  224.9 64.8 %copy-start.7 = (s32[2,1024]{1,0:T(2,128)S(1)}, s32[2,1024]{1,0:T(2,128)}, u32[]{:S(2)}) copy-start(s32[2,1024]{1,0:T(2,128)} %param.13) | copy-start | bytes 24580
  224.9 55.6 %all-to-all-start.4 = ((f32[16,129,256]{2,1,0:T(8,128)}), f32[16,129,256]{2,1,0:T(8,128)S(1)}, u32[]{:S(2)}, u32[]{:S(2)}) async-start(f32[16,129,256]{2,1,0:T(8,128)} %pad_maximum_fusion), calls=%async_computation.4 | async-start | bytes 4456448 | tf_op jit(solution)/shard_map/all_to_all | solution.py:212
  281.8 18.6 %all-to-all-start.5 = ((f32[32,4,256]{2,1,0:T(4,128)}), f32[32,4,256]{2,1,0:T(4,128)S(1)}, u32[]{:S(2)}, u32[]{:S(2)}) async-start(f32[32,4,256]{2,1,0:T(4,128)} %bitcast_select_fusion), calls=%async_computation.5 | async-start | bytes 262144 | tf_op jit(solution)/shard_map/all_to_all | solution.py:222

commit v8 on v7

--- a/solution.py
+++ b/solution.py
@@ -228,15 +228,20 @@
     part = lax.all_to_all(
         jnp.broadcast_to(part[None], (shards,) + part.shape), "table", 0, 0, tiled=True
     )
-    part = part.reshape(chips, 2, own_rows, out_width).transpose(1, 0, 2, 3)
-    part = part.reshape(2 * dp_rows, out_width)
+    part = part.reshape(chips, 2, own_rows, out_width)
+    part = jnp.where(core == 0, part[:, 0], part[:, 1]).reshape(dp_rows, out_width)
     finished = jnp.concatenate([part, own_update], axis=0).astype(jnp.bfloat16)
     finished = lax.all_to_all(
         jnp.broadcast_to(finished[None], (n_dp,) + finished.shape), "dp", 0, 0, tiled=True
+    )
+    own_tower = finished[:, :dp_rows].reshape(hidden_width, out_width)
+    other_tower = lax.ppermute(own_tower, "table", partner)
+    tower_update = jnp.where(
+        core == 0,
+        jnp.stack([own_tower, other_tower]),
+        jnp.stack([other_tower, own_tower]),
     ).astype(jnp.float32)
-    tower_update = finished[:, : 2 * dp_rows].reshape(n_dp, 2, dp_rows, out_width)
-    tower_update = tower_update.transpose(1, 0, 2, 3).reshape(2, hidden_width, out_width)
-    table_update = finished[:, 2 * dp_rows :].reshape(rows_dev, emb_width)
+    table_update = finished[:, dp_rows:].reshape(rows_dev, emb_width).astype(jnp.float32)
     return (table_update, tower_update)
 
 

time: 360 us -> 353 us (0.981)
  blocking collectives: 78.9 us -> 67.7 us
  starting transfers between devices: 34.8 us -> 39.3 us
    all_to_all x1, blocking collectives: 42.2 us -> 30.9 us  [body(): lax.all_to_all(jnp.broadcast_to(finished[None], (n_dp,) + finished.shape)...]
    ppermute x0 -> x1, starting transfers between devices: none -> 4.5 us  [body(): other_tower = lax.ppermute(own_tower, 'table', partner)]
  transfers between devices with their start and end apart: 6 -> 7, of which waited for: 6 -> 7; matrix products, arithmetic and copies ran while one was open for 3% -> 3% of each run, Pallas kernels for 0% -> 0%
where the time goes in v8:
time: 353 us; the launch traced here: 352 us
  waiting for transfers between devices  176 us (50%)
  blocking collectives  67.7 us (19%)
  matrix products  39.5 us (11%)
  starting transfers between devices  39.3 us (11%)
  other arithmetic  21.1 us (6%)
  local copies, waits for them, and re-layouts  7.8 us (2%)
    all_to_all x1, waiting for transfers between devices, body(): packed = jnp.sum(lax.all_to_all(packed, 'dp', 0, 0, tiled=True), axis=0)  50.8 us
    all_to_all x1, waiting for transfers between devices, body(): lax.all_to_all(jnp.broadcast_to(both[None], (n_dp,) + both.shape), 'dp',...  45.7 us
    all_to_all x1, waiting for transfers between devices, body(): lax.all_to_all(fetched.reshape(shards, capacity, emb_width), 'table', spl...  37.1 us
    all_to_all x1, blocking collectives, body(): lax.all_to_all(jnp.broadcast_to(finished[None], (n_dp,) + finished.shape)...  30.9 us
    all_to_all x1, waiting for transfers between devices, body(): lax.all_to_all(grad_out.reshape(shards, capacity, emb_width), 'table', sp...  30.3 us
    all_to_all x1, blocking collectives, body(): lax.all_to_all(outgoing, 'table', split_axis=0, concat_axis=0, tiled=True)  23.6 us
    all_to_all x1, blocking collectives, body(): lax.all_to_all(jnp.broadcast_to(part[None], (shards,) + part.shape), 'tab...  13.1 us
    all_to_all x1, waiting for transfers between devices, body(): part = jnp.sum(lax.all_to_all(part, 'table', 0, 0, tiled=True), axis=0)  10.6 us
  transfers between devices with their start and end apart: 7, of which 7 were waited for; matrix products, arithmetic and copies ran while one was open for 3% of the time, Pallas kernels for 0%

profile of v8, /device:TPU:1, one launch (start us, length us, event | category | flops | bytes accessed | tf_op | source)
XLA Modules:
  0.0 352.5 jit_solution(9969928294991287686)
XLA Ops:
  0.6 1.0 copy.23
  1.9 1.6 fusion.26
  3.5 1.9 fusion.31
  5.4 1.5 fusion.37
  7.2 4.4 %fusion.23 = s32[3072,3]{0,1:T(4,128)S(1)} fusion(s32[2048]{0:T(1024)S(1)} %multiply_add_fusion.1, bf16[2048,1]{0,1:T(2,128)(2,1)S(1)} %fusion.102, bf16[2048,1]{0,1:T(2,128)(2,1)S(1)} %get-tuple-element.6, bf16[3]{0:T(256)(128)(2,1)S(1)} %pad.15.clone), kind=kOutput, calls=%fused_computation.27 | convolution fusion | flops 44086272 | bytes 53254 | tf_op jit(solution)/shard_map/dot_general | solution.py:72
  11.7 23.6 %all_to_all.41 = s32[32,1,96]{2,1,0:T(1,128)S(1)} all-to-all(s32[32,1,96]{2,1,0:T(1,128)S(1)} %bitcast.103), channel_id=1, replica_groups=mesh['dp'=16,'table'=32] {'table'}, dimensions={0} | all-to-all | bytes 24576 | tf_op jit(solution)/shard_map/all_to_all | solution.py:82
  35.3 0.5 broadcast.760
  35.8 0.7 reduce.19
  36.6 3.6 %fusion.22 = bf16[3072,256]{1,0:T(8,128)(2,1)} fusion(bf16[1024,256]{1,0:T(8,128)(2,1)S(1)} %copy-done, s32[3072]{0:T(1024)S(1)} %eq.166), kind=kOutput, calls=%fused_computation.26 | convolution fusion | flops 1614544896 | bytes 2109440 | tf_op jit(solution)/shard_map/dot_general | solution.py:87
  40.2 4.2 %all-to-all-start.1 = ((bf16[32,96,256]{2,1,0:T(8,128)(2,1)}), bf16[32,96,256]{2,1,0:T(8,128)(2,1)S(1)}, u32[]{:S(2)}, u32[]{:S(2)}) async-start(bf16[32,96,256]{2,1,0:T(8,128)(2,1)} %bitcast.96), calls=%async_computation.1 | async-start | bytes 3145728 | tf_op jit(solution)/shard_map/all_to_all | solution.py:88
  44.5 0.5 reduce_sum.113
  44.9 0.5 convert_element_type.156
  45.7 0.5 slice_reduce_fusion.1
  46.2 37.1 %all-to-all-done.1 = bf16[32,96,256]{2,1,0:T(8,128)(2,1)S(1)} async-done(((bf16[32,96,256]{2,1,0:T(8,128)(2,1)}), bf16[32,96,256]{2,1,0:T(8,128)(2,1)S(1)}, u32[]{:S(2)}, u32[]{:S(2)}) %all-to-all-start.1) | async-done | bytes 1572896 | tf_op jit(solution)/shard_map/all_to_all | solution.py:88
  83.4 3.3 fusion.32
  87.5 1.5 broadcast_in_dim.114
  89.1 7.0 %all-to-all-start.2 = ((bf16[16,128,512]{2,1,0:T(8,128)(2,1)}), bf16[16,128,512]{2,1,0:T(8,128)(2,1)S(1)}, u32[]{:S(2)}, u32[]{:S(2)}) async-start(bf16[16,128,512]{2,1,0:T(8,128)(2,1)} %broadcast_in_dim.114), calls=%async_computation.2 | async-start | bytes 4194304 | tf_op jit(solution)/shard_map/all_to_all | solution.py:112
  96.0 2.4 multiply_reduce_fusion.3
  98.4 45.7 %all-to-all-done.2 = bf16[16,128,512]{2,1,0:T(8,128)(2,1)S(1)} async-done(((bf16[16,128,512]{2,1,0:T(8,128)(2,1)}), bf16[16,128,512]{2,1,0:T(8,128)(2,1)S(1)}, u32[]{:S(2)}, u32[]{:S(2)}) %all-to-all-start.2) | async-done | bytes 2097184 | tf_op jit(solution)/shard_map/all_to_all | solution.py:112
  144.4 8.1 %fusion.127 = (f32[2048]{0:T(1024)S(1)}, f32[2048,2048]{0,1:T(8,128)}) fusion(bf16[2048,256]{1,0:T(8,128)(2,1)S(1)} %bitcast.84, bf16[2048,256]{1,0:T(8,128)(2,1)S(1)} %bitcast.86), kind=kOutput, calls=%fused_computation.209 | convolution fusion | flops 2155870208 | bytes 18882560 | tf_op jit(solution)/shard_map/dot_general | solution.py:117
  152.5 8.1 %exponential_reduce_fusion = f32[2048]{0:T(1024)S(1)} fusion(f32[2048,2048]{0,1:T(8,128)} %get-tuple-element.19, f32[2048]{0:T(1024)S(1)} %get-tuple-element.18), kind=kLoop, calls=%fused_computation.2 | loop fusion | flops 8386560 | bytes 16793600 | tf_op jit(solution)/shard_map/reduce_sum | solution.py:121
  160.6 1.8 fusion.55
  162.4 1.7 fusion.53
  164.2 0.4 multiply_reduce_fusion
  164.8 0.4 multiply_reduce_fusion.1
  165.7 5.3 %fusion.19 = bf16[3072,256]{1,0:T(8,128)(2,1)} fusion(s32[1024]{0:T(1024)S(1)} %get-tuple-element.5, s32[1024]{0:T(1024)S(1)} %get-tuple-element.4, f32[128,4,256]{2,1,0:T(4,128)S(1)} %reshape.538, f32[128,4,256]{2,1,0:T(4,128)S(1)} %reshape.537, f32[1024]{0:T(1024)S(1)} %mul.243), kind=kOutput, calls=%fused_computation.25 | convolution fusion | flops 1621622784 | bytes 2633728 | tf_op jit(solution)/shard_map/dot_general | solution.py:172
  171.0 9.7 %all-to-all-start.3 = ((bf16[32,96,256]{2,1,0:T(8,128)(2,1)}), bf16[32,96,256]{2,1,0:T(8,128)(2,1)}, u32[]{:S(2)}, u32[]{:S(2)}) async-start(bf16[32,96,256]{2,1,0:T(8,128)(2,1)} %bitcast.10), calls=%async_computation.3 | async-start | bytes 3145728 | tf_op jit(solution)/shard_map/all_to_all | solution.py:178
  180.7 0.4 fusion.79
  181.0 1.3 broadcast_select_fusion
  182.4 2.2 collective-permute-start
  184.6 1.5 convert_reduce_fusion
  186.3 0.9 collective-permute-done
  187.3 2.4 select_add_fusion
  189.6 30.3 %all-to-all-done.3 = bf16[32,96,256]{2,1,0:T(8,128)(2,1)} async-done(((bf16[32,96,256]{2,1,0:T(8,128)(2,1)}), bf16[32,96,256]{2,1,0:T(8,128)(2,1)}, u32[]{:S(2)}, u32[]{:S(2)}) %all-to-all-start.3) | async-done | bytes 1572896 | tf_op jit(solution)/shard_map/all_to_all | solution.py:178
  219.9 3.4 fusion.6
  223.3 1.6 pad_maximum_fusion
  224.9 3.9 %all-to-all-start.4 = ((f32[16,129,256]{2,1,0:T(8,128)}), f32[16,129,256]{2,1,0:T(8,128)S(1)}, u32[]{:S(2)}, u32[]{:S(2)}) async-start(f32[16,129,256]{2,1,0:T(8,128)} %pad_maximum_fusion), calls=%async_computation.4 | async-start | bytes 4456448 | tf_op jit(solution)/shard_map/all_to_all | solution.py:212
  228.9 0.8 dynamic_slice.16
  229.6 50.8 %all-to-all-done.4 = f32[16,129,256]{2,1,0:T(8,128)S(1)} async-done(((f32[16,129,256]{2,1,0:T(8,128)}), f32[16,129,256]{2,1,0:T(8,128)S(1)}, u32[]{:S(2)}, u32[]{:S(2)}) %all-to-all-start.4) | async-done | bytes 2113568 | tf_op jit(solution)/shard_map/all_to_all | solution.py:212
  281.1 0.8 bitcast_select_fusion
  281.8 7.9 %all-to-all-start.5 = ((f32[32,4,256]{2,1,0:T(4,128)}), f32[32,4,256]{2,1,0:T(4,128)S(1)}, u32[]{:S(2)}, u32[]{:S(2)}) async-start(f32[32,4,256]{2,1,0:T(4,128)} %bitcast_select_fusion), calls=%async_computation.5 | async-start | bytes 262144 | tf_op jit(solution)/shard_map/all_to_all | solution.py:222
  289.8 10.6 %all-to-all-done.5 = f32[32,4,256]{2,1,0:T(4,128)S(1)} async-done(((f32[32,4,256]{2,1,0:T(4,128)}), f32[32,4,256]{2,1,0:T(4,128)S(1)}, u32[]{:S(2)}, u32[]{:S(2)}) %all-to-all-start.5) | async-done | bytes 131104 | tf_op jit(solution)/shard_map/all_to_all | solution.py:222
  300.6 13.1 %all_to_all.42 = bf16[32,4,256]{2,1,0:T(4,128)(2,1)S(1)} all-to-all(bf16[32,4,256]{2,1,0:T(4,128)(2,1)S(1)} %broadcast_in_dim.122), channel_id=1, replica_groups=mesh['dp'=16,'table'=32] {'table'}, dimensions={0} | all-to-all | bytes 131072 | tf_op jit(solution)/shard_map/all_to_all | solution.py:228
  313.9 30.9 %all_to_all.43 = bf16[16,128,256]{2,1,0:T(8,128)(2,1)S(1)} all-to-all(bf16[16,128,256]{2,1,0:T(8,128)(2,1)S(1)} %broadcast_in_dim.126), channel_id=1, replica_groups=mesh['dp'=16,'table'=32] {'dp'}, dimensions={0} | all-to-all | bytes 2097152 | tf_op jit(solution)/shard_map/all_to_all | solution.py:234
  345.0 4.5 %collective-permute-start.1 = (bf16[1024,256]{1,0:T(8,128)(2,1)S(1)}, bf16[1024,256]{1,0:T(8,128)(2,1)S(1)}, u32[]{:S(2)}, u32[]{:S(2)}) collective-permute-start(bf16[1024,256]{1,0:T(8,128)(2,1)S(1)} %bitcast.93), channel_id=1, source_target_pairs={{0,1},{1,0},{2,3},{3,2},{4,5},{5,4},{6,7},{7,6},{8,9},{9,8},{10,11... | collective-permute-start | bytes 1572872 | tf_op jit(solution)/shard_map/ppermute | solution.py:238
  349.5 1.1 bitcast_convert_fusion
  350.6 0.4 collective-permute-done.1
  351.0 1.5 fusion.42
  (67 shorter events, 4.2 us)
Async XLA Ops:
  0.6 35.9 %copy-start = (bf16[1024,256]{1,0:T(8,128)(2,1)S(1)}, bf16[1024,256]{1,0:T(8,128)(2,1)}, u32[]{:S(2)}) copy-start(bf16[1024,256]{1,0:T(8,128)(2,1)} %param.7) | copy-start | bytes 1572868
  40.2 43.2 %all-to-all-start.1 = ((bf16[32,96,256]{2,1,0:T(8,128)(2,1)}), bf16[32,96,256]{2,1,0:T(8,128)(2,1)S(1)}, u32[]{:S(2)}, u32[]{:S(2)}) async-start(bf16[32,96,256]{2,1,0:T(8,128)(2,1)} %bitcast.96), calls=%async_computation.1 | async-start | bytes 3145728 | tf_op jit(solution)/shard_map/all_to_all | solution.py:88
  83.4 3.6 %copy-start.2 = (bf16[1024,256]{1,0:T(8,128)(2,1)S(1)}, bf16[1024,256]{1,0:T(8,128)(2,1)}, u32[]{:S(2)}) copy-start(bf16[1024,256]{1,0:T(8,128)(2,1)} %param.11) | copy-start | bytes 1572868
  83.4 3.9 %copy-start.4 = (bf16[1024,256]{1,0:T(8,128)(2,1)S(1)}, bf16[1024,256]{1,0:T(8,128)(2,1)}, u32[]{:S(2)}) copy-start(bf16[1024,256]{1,0:T(8,128)(2,1)} %param.10) | copy-start | bytes 1572868
  86.7 0.8 copy-start.6
  89.1 55.1 %all-to-all-start.2 = ((bf16[16,128,512]{2,1,0:T(8,128)(2,1)}), bf16[16,128,512]{2,1,0:T(8,128)(2,1)S(1)}, u32[]{:S(2)}, u32[]{:S(2)}) async-start(bf16[16,128,512]{2,1,0:T(8,128)(2,1)} %broadcast_in_dim.114), calls=%async_computation.2 | async-start | bytes 4194304 | tf_op jit(solution)/shard_map/all_to_all | solution.py:112
  160.6 3.6 %copy-start.3 = (bf16[1024,256]{1,0:T(8,128)(2,1)S(1)}, bf16[1024,256]{1,0:T(8,128)(2,1)}, u32[]{:S(2)}) copy-start(bf16[1024,256]{1,0:T(8,128)(2,1)} %param.11) | copy-start | bytes 1572868
  160.6 4.2 %copy-start.5 = (bf16[1024,256]{1,0:T(8,128)(2,1)S(1)}, bf16[1024,256]{1,0:T(8,128)(2,1)}, u32[]{:S(2)}) copy-start(bf16[1024,256]{1,0:T(8,128)(2,1)} %param.10) | copy-start | bytes 1572868
  171.0 48.9 %all-to-all-start.3 = ((bf16[32,96,256]{2,1,0:T(8,128)(2,1)}), bf16[32,96,256]{2,1,0:T(8,128)(2,1)}, u32[]{:S(2)}, u32[]{:S(2)}) async-start(bf16[32,96,256]{2,1,0:T(8,128)(2,1)} %bitcast.10), calls=%async_computation.3 | async-start | bytes 3145728 | tf_op jit(solution)/shard_map/all_to_all | solution.py:178
  182.4 4.9 %collective-permute-start = (f32[1024,256]{1,0:T(8,128)}, f32[1024,256]{1,0:T(8,128)}, u32[]{:S(2)}, u32[]{:S(2)}) collective-permute-start(f32[1024,256]{1,0:T(8,128)} %get-tuple-element.28), channel_id=1, source_target_pairs={{0,1},{1,0},{2,3},{3,2},{4,5},{5,4},{6,7},{7,6},{8,9},{9,8},{10,11... | collective-permute-start | bytes 3145736 | tf_op jit(solution)/shard_map/ppermute | solution.py:198
  219.9 3.4 copy-start.1
  224.9 64.8 %copy-start.7 = (s32[2,1024]{1,0:T(2,128)S(1)}, s32[2,1024]{1,0:T(2,128)}, u32[]{:S(2)}) copy-start(s32[2,1024]{1,0:T(2,128)} %param.13) | copy-start | bytes 24580
  224.9 55.6 %all-to-all-start.4 = ((f32[16,129,256]{2,1,0:T(8,128)}), f32[16,129,256]{2,1,0:T(8,128)S(1)}, u32[]{:S(2)}, u32[]{:S(2)}) async-start(f32[16,129,256]{2,1,0:T(8,128)} %pad_maximum_fusion), calls=%async_computation.4 | async-start | bytes 4456448 | tf_op jit(solution)/shard_map/all_to_all | solution.py:212
  281.8 18.6 %all-to-all-start.5 = ((f32[32,4,256]{2,1,0:T(4,128)}), f32[32,4,256]{2,1,0:T(4,128)S(1)}, u32[]{:S(2)}, u32[]{:S(2)}) async-start(f32[32,4,256]{2,1,0:T(4,128)} %bitcast_select_fusion), calls=%async_computation.5 | async-start | bytes 262144 | tf_op jit(solution)/shard_map/all_to_all | solution.py:222
  345.0 6.0 %collective-permute-start.1 = (bf16[1024,256]{1,0:T(8,128)(2,1)S(1)}, bf16[1024,256]{1,0:T(8,128)(2,1)S(1)}, u32[]{:S(2)}, u32[]{:S(2)}) collective-permute-start(bf16[1024,256]{1,0:T(8,128)(2,1)S(1)} %bitcast.93), channel_id=1, source_target_pairs={{0,1},{1,0},{2,3},{3,2},{4,5},{5,4},{6,7},{7,6},{8,9},{9,8},{10,11... | collective-permute-start | bytes 1572872 | tf_op jit(solution)/shard_map/ppermute | solution.py:238

commit v9 on v8

--- a/solution.py
+++ b/solution.py
@@ -114,15 +114,26 @@
     )
     all_queries = both[:, :, :out_width].reshape(n_dp * batch, out_width)
     all_items = both[:, :, out_width:].reshape(n_dp * batch, out_width)
+    contract = (((1,), (1,)), ((), ()))
     scores = scale * lax.dot_general(
-        all_queries, all_items, (((1,), (1,)), ((), ())), preferred_element_type=jnp.float32
+        all_queries, all_items, contract, preferred_element_type=jnp.float32
     )
     peak = jnp.max(scores, axis=1, keepdims=True)
-    log_total = peak + jnp.log(jnp.sum(jnp.exp(scores - peak), axis=1, keepdims=True))
+    again_queries, again_items = lax.optimization_barrier((all_queries, all_items))
+    scores_again = scale * lax.dot_general(
+        again_queries, again_items, contract, preferred_element_type=jnp.float32
+    )
+    log_total = peak + jnp.log(jnp.sum(jnp.exp(scores_again - peak), axis=1, keepdims=True))
     own = dp_index * batch
-    row_scores = lax.dynamic_slice_in_dim(scores, own, batch, axis=0)
+    own_queries = lax.dynamic_slice_in_dim(all_queries, own, batch, axis=0)
+    own_items = lax.dynamic_slice_in_dim(all_items, own, batch, axis=0)
+    row_scores = scale * lax.dot_general(
+        own_queries, all_items, contract, preferred_element_type=jnp.float32
+    )
+    col_scores = scale * lax.dot_general(
+        all_queries, own_items, contract, preferred_element_type=jnp.float32
+    )
     row_total = lax.dynamic_slice_in_dim(log_total, own, batch, axis=0)
-    col_scores = lax.dynamic_slice_in_dim(scores, own, batch, axis=1)
     row_probs = jnp.exp(row_scores - row_total).astype(jnp.bfloat16)
     col_probs = jnp.exp(col_scores - log_total).astype(jnp.bfloat16)
     query_grad = (

time: 353 us -> 344 us (0.975)
  other arithmetic: 21.1 us -> 12.9 us
    reduce_sum x1 -> x0, other arithmetic: 8.08 us -> none  [body(): jnp.sum(jnp.exp(scores - peak), axis=1, keepdims=True)]
    dot_general x1 -> x2, matrix products: 8.1 us -> 5.62 us  [the longest x1 3.23 us: body(): lax.dot_general(again_queries, again_items, contract, preferred_element_t...]
where the time goes in v9:
time: 344 us; the launch traced here: 343 us
  waiting for transfers between devices  176 us (51%)
  blocking collectives  67.7 us (20%)
  starting transfers between devices  39.5 us (11%)
  matrix products  37 us (11%)
  other arithmetic  12.9 us (4%)
  local copies, waits for them, and re-layouts  8.54 us (2%)
    all_to_all x1, waiting for transfers between devices, body(): packed = jnp.sum(lax.all_to_all(packed, 'dp', 0, 0, tiled=True), axis=0)  50.8 us
    all_to_all x1, waiting for transfers between devices, body(): lax.all_to_all(jnp.broadcast_to(both[None], (n_dp,) + both.shape), 'dp',...  45.8 us
    all_to_all x1, waiting for transfers between devices, body(): lax.all_to_all(fetched.reshape(shards, capacity, emb_width), 'table', spl...  37.1 us
    all_to_all x1, blocking collectives, body(): lax.all_to_all(jnp.broadcast_to(finished[None], (n_dp,) + finished.shape)...  31 us
    all_to_all x1, waiting for transfers between devices, body(): lax.all_to_all(grad_out.reshape(shards, capacity, emb_width), 'table', sp...  30 us
    all_to_all x1, blocking collectives, body(): lax.all_to_all(outgoing, 'table', split_axis=0, concat_axis=0, tiled=True)  23.6 us
    all_to_all x1, blocking collectives, body(): lax.all_to_all(jnp.broadcast_to(part[None], (shards,) + part.shape), 'tab...  13.1 us
    all_to_all x1, waiting for transfers between devices, body(): part = jnp.sum(lax.all_to_all(part, 'table', 0, 0, tiled=True), axis=0)  10.6 us
  transfers between devices with their start and end apart: 7, of which 7 were waited for; matrix products, arithmetic and copies ran while one was open for 3% of the time, Pallas kernels for 0%

profile of v9, /device:TPU:1, one launch (start us, length us, event | category | flops | bytes accessed | tf_op | source)
XLA Modules:
  0.0 342.7 jit_solution(5548628192145378703)
XLA Ops:
  0.7 1.0 copy.23
  2.0 1.6 fusion.26
  3.6 1.0 fusion.37
  4.6 1.5 fusion.47
  6.3 4.4 %fusion.23 = s32[3072,3]{0,1:T(4,128)S(1)} fusion(s32[2048]{0:T(1024)S(1)} %multiply_add_fusion.1, bf16[2048,1]{0,1:T(2,128)(2,1)S(1)} %fusion.118, bf16[2048,1]{0,1:T(2,128)(2,1)S(1)} %get-tuple-element.10, bf16[3]{0:T(256)(128)(2,1)S(1)} %pad.15.clone), kind=kOutput, calls=%fused_computation.27 | convolution fusion | flops 44086272 | bytes 53254 | tf_op jit(solution)/shard_map/dot_general | solution.py:72
  10.8 23.6 %all_to_all.41 = s32[32,1,96]{2,1,0:T(1,128)S(1)} all-to-all(s32[32,1,96]{2,1,0:T(1,128)S(1)} %bitcast.111), channel_id=1, replica_groups=mesh['dp'=16,'table'=32] {'table'}, dimensions={0} | all-to-all | bytes 24576 | tf_op jit(solution)/shard_map/all_to_all | solution.py:82
  34.4 0.5 broadcast.766
  34.9 0.7 reduce.19
  35.7 3.6 %fusion.22 = bf16[3072,256]{1,0:T(8,128)(2,1)} fusion(bf16[1024,256]{1,0:T(8,128)(2,1)S(1)} %copy-done, s32[3072]{0:T(1024)S(1)} %eq.166), kind=kOutput, calls=%fused_computation.26 | convolution fusion | flops 1614544896 | bytes 2109440 | tf_op jit(solution)/shard_map/dot_general | solution.py:87
  39.3 4.2 %all-to-all-start.1 = ((bf16[32,96,256]{2,1,0:T(8,128)(2,1)}), bf16[32,96,256]{2,1,0:T(8,128)(2,1)S(1)}, u32[]{:S(2)}, u32[]{:S(2)}) async-start(bf16[32,96,256]{2,1,0:T(8,128)(2,1)} %bitcast.96), calls=%async_computation.1 | async-start | bytes 3145728 | tf_op jit(solution)/shard_map/all_to_all | solution.py:88
  43.6 0.5 reduce_sum.113
  44.1 0.5 convert_element_type.156
  44.9 0.5 slice_reduce_fusion.1
  45.4 37.1 %all-to-all-done.1 = bf16[32,96,256]{2,1,0:T(8,128)(2,1)S(1)} async-done(((bf16[32,96,256]{2,1,0:T(8,128)(2,1)}), bf16[32,96,256]{2,1,0:T(8,128)(2,1)S(1)}, u32[]{:S(2)}, u32[]{:S(2)}) %all-to-all-start.1) | async-done | bytes 1572896 | tf_op jit(solution)/shard_map/all_to_all | solution.py:88
  82.5 3.3 fusion.40
  86.4 0.7 copy-done.4
  87.4 1.5 broadcast_in_dim.114
  88.9 7.0 %all-to-all-start.2 = ((bf16[16,128,512]{2,1,0:T(8,128)(2,1)}), bf16[16,128,512]{2,1,0:T(8,128)(2,1)S(1)}, u32[]{:S(2)}, u32[]{:S(2)}) async-start(bf16[16,128,512]{2,1,0:T(8,128)(2,1)} %broadcast_in_dim.114), calls=%async_computation.2 | async-start | bytes 4194304 | tf_op jit(solution)/shard_map/all_to_all | solution.py:112
  95.8 2.3 multiply_reduce_fusion.4
  98.1 45.8 %all-to-all-done.2 = bf16[16,128,512]{2,1,0:T(8,128)(2,1)S(1)} async-done(((bf16[16,128,512]{2,1,0:T(8,128)(2,1)}), bf16[16,128,512]{2,1,0:T(8,128)(2,1)S(1)}, u32[]{:S(2)}, u32[]{:S(2)}) %all-to-all-start.2) | async-done | bytes 2097184 | tf_op jit(solution)/shard_map/all_to_all | solution.py:112
  144.2 2.4 multiply_reduce_fusion
  146.7 3.2 exponential_reduce_fusion
  150.0 2.7 fusion.67
  152.7 1.7 fusion.65
  154.5 0.4 multiply_reduce_fusion.1
  155.1 0.4 multiply_reduce_fusion.2
  156.0 5.3 %fusion.19 = bf16[3072,256]{1,0:T(8,128)(2,1)} fusion(s32[1024]{0:T(1024)S(1)} %get-tuple-element.9, s32[1024]{0:T(1024)S(1)} %get-tuple-element.8, f32[128,4,256]{2,1,0:T(4,128)S(1)} %reshape.538, f32[128,4,256]{2,1,0:T(4,128)S(1)} %reshape.537, f32[1024]{0:T(1024)S(1)} %mul.259), kind=kOutput, calls=%fused_computation.25 | convolution fusion | flops 1621622784 | bytes 2633728 | tf_op jit(solution)/shard_map/dot_general | solution.py:183
  161.3 9.7 %all-to-all-start.3 = ((bf16[32,96,256]{2,1,0:T(8,128)(2,1)}), bf16[32,96,256]{2,1,0:T(8,128)(2,1)}, u32[]{:S(2)}, u32[]{:S(2)}) async-start(bf16[32,96,256]{2,1,0:T(8,128)(2,1)} %bitcast.10), calls=%async_computation.3 | async-start | bytes 3145728 | tf_op jit(solution)/shard_map/all_to_all | solution.py:189
  171.3 1.3 broadcast_select_fusion
  172.7 2.4 collective-permute-start
  175.1 1.5 convert_reduce_fusion
  176.8 0.9 collective-permute-done
  177.7 2.4 select_add_fusion
  180.1 30.0 %all-to-all-done.3 = bf16[32,96,256]{2,1,0:T(8,128)(2,1)} async-done(((bf16[32,96,256]{2,1,0:T(8,128)(2,1)}), bf16[32,96,256]{2,1,0:T(8,128)(2,1)}, u32[]{:S(2)}, u32[]{:S(2)}) %all-to-all-start.3) | async-done | bytes 1572896 | tf_op jit(solution)/shard_map/all_to_all | solution.py:189
  210.1 3.4 fusion.6
  213.5 1.6 pad_maximum_fusion
  215.1 3.7 %all-to-all-start.4 = ((f32[16,129,256]{2,1,0:T(8,128)}), f32[16,129,256]{2,1,0:T(8,128)S(1)}, u32[]{:S(2)}, u32[]{:S(2)}) async-start(f32[16,129,256]{2,1,0:T(8,128)} %pad_maximum_fusion), calls=%async_computation.4 | async-start | bytes 4456448 | tf_op jit(solution)/shard_map/all_to_all | solution.py:223
  218.9 0.8 dynamic_slice.16
  219.7 50.8 %all-to-all-done.4 = f32[16,129,256]{2,1,0:T(8,128)S(1)} async-done(((f32[16,129,256]{2,1,0:T(8,128)}), f32[16,129,256]{2,1,0:T(8,128)S(1)}, u32[]{:S(2)}, u32[]{:S(2)}) %all-to-all-start.4) | async-done | bytes 2113568 | tf_op jit(solution)/shard_map/all_to_all | solution.py:223
  271.1 0.8 bitcast_select_fusion
  271.9 7.9 %all-to-all-start.5 = ((f32[32,4,256]{2,1,0:T(4,128)}), f32[32,4,256]{2,1,0:T(4,128)S(1)}, u32[]{:S(2)}, u32[]{:S(2)}) async-start(f32[32,4,256]{2,1,0:T(4,128)} %bitcast_select_fusion), calls=%async_computation.5 | async-start | bytes 262144 | tf_op jit(solution)/shard_map/all_to_all | solution.py:233
  280.0 10.6 %all-to-all-done.5 = f32[32,4,256]{2,1,0:T(4,128)S(1)} async-done(((f32[32,4,256]{2,1,0:T(4,128)}), f32[32,4,256]{2,1,0:T(4,128)S(1)}, u32[]{:S(2)}, u32[]{:S(2)}) %all-to-all-start.5) | async-done | bytes 131104 | tf_op jit(solution)/shard_map/all_to_all | solution.py:233
  290.8 13.1 %all_to_all.42 = bf16[32,4,256]{2,1,0:T(4,128)(2,1)S(1)} all-to-all(bf16[32,4,256]{2,1,0:T(4,128)(2,1)S(1)} %broadcast_in_dim.122), channel_id=1, replica_groups=mesh['dp'=16,'table'=32] {'table'}, dimensions={0} | all-to-all | bytes 131072 | tf_op jit(solution)/shard_map/all_to_all | solution.py:239
  304.1 31.0 %all_to_all.43 = bf16[16,128,256]{2,1,0:T(8,128)(2,1)S(1)} all-to-all(bf16[16,128,256]{2,1,0:T(8,128)(2,1)S(1)} %broadcast_in_dim.126), channel_id=1, replica_groups=mesh['dp'=16,'table'=32] {'dp'}, dimensions={0} | all-to-all | bytes 2097152 | tf_op jit(solution)/shard_map/all_to_all | solution.py:245
  335.1 4.5 %collective-permute-start.1 = (bf16[1024,256]{1,0:T(8,128)(2,1)S(1)}, bf16[1024,256]{1,0:T(8,128)(2,1)S(1)}, u32[]{:S(2)}, u32[]{:S(2)}) collective-permute-start(bf16[1024,256]{1,0:T(8,128)(2,1)S(1)} %bitcast.93), channel_id=1, source_target_pairs={{0,1},{1,0},{2,3},{3,2},{4,5},{5,4},{6,7},{7,6},{8,9},{9,8},{10,11... | collective-permute-start | bytes 1572872 | tf_op jit(solution)/shard_map/ppermute | solution.py:249
  339.6 1.1 bitcast_convert_fusion
  340.7 0.4 collective-permute-done.1
  341.2 1.5 fusion.52
  (75 shorter events, 4.6 us)
Async XLA Ops:
  0.6 35.1 %copy-start = (bf16[1024,256]{1,0:T(8,128)(2,1)S(1)}, bf16[1024,256]{1,0:T(8,128)(2,1)}, u32[]{:S(2)}) copy-start(bf16[1024,256]{1,0:T(8,128)(2,1)} %param.7) | copy-start | bytes 1572868
  0.6 2.9 copy-start.11
  39.3 43.2 %all-to-all-start.1 = ((bf16[32,96,256]{2,1,0:T(8,128)(2,1)}), bf16[32,96,256]{2,1,0:T(8,128)(2,1)S(1)}, u32[]{:S(2)}, u32[]{:S(2)}) async-start(bf16[32,96,256]{2,1,0:T(8,128)(2,1)} %bitcast.96), calls=%async_computation.1 | async-start | bytes 3145728 | tf_op jit(solution)/shard_map/all_to_all | solution.py:88
  82.5 3.6 %copy-start.2 = (bf16[1024,256]{1,0:T(8,128)(2,1)S(1)}, bf16[1024,256]{1,0:T(8,128)(2,1)}, u32[]{:S(2)}) copy-start(bf16[1024,256]{1,0:T(8,128)(2,1)} %param.11) | copy-start | bytes 1572868
  85.8 1.5 copy-start.6
  85.9 1.2 copy-start.4
  88.9 55.1 %all-to-all-start.2 = ((bf16[16,128,512]{2,1,0:T(8,128)(2,1)}), bf16[16,128,512]{2,1,0:T(8,128)(2,1)S(1)}, u32[]{:S(2)}, u32[]{:S(2)}) async-start(bf16[16,128,512]{2,1,0:T(8,128)(2,1)} %broadcast_in_dim.114), calls=%async_computation.2 | async-start | bytes 4194304 | tf_op jit(solution)/shard_map/all_to_all | solution.py:112
  144.2 2.4 copy-start.7
  144.2 2.4 copy-start.9
  149.9 2.8 copy-start.8
  150.0 4.5 %copy-start.3 = (bf16[1024,256]{1,0:T(8,128)(2,1)S(1)}, bf16[1024,256]{1,0:T(8,128)(2,1)}, u32[]{:S(2)}) copy-start(bf16[1024,256]{1,0:T(8,128)(2,1)} %param.11) | copy-start | bytes 1572868
  152.7 2.4 copy-start.5
  161.3 48.8 %all-to-all-start.3 = ((bf16[32,96,256]{2,1,0:T(8,128)(2,1)}), bf16[32,96,256]{2,1,0:T(8,128)(2,1)}, u32[]{:S(2)}, u32[]{:S(2)}) async-start(bf16[32,96,256]{2,1,0:T(8,128)(2,1)} %bitcast.10), calls=%async_computation.3 | async-start | bytes 3145728 | tf_op jit(solution)/shard_map/all_to_all | solution.py:189
  172.7 5.0 %collective-permute-start = (f32[1024,256]{1,0:T(8,128)}, f32[1024,256]{1,0:T(8,128)}, u32[]{:S(2)}, u32[]{:S(2)}) collective-permute-start(f32[1024,256]{1,0:T(8,128)} %get-tuple-element.30), channel_id=1, source_target_pairs={{0,1},{1,0},{2,3},{3,2},{4,5},{5,4},{6,7},{7,6},{8,9},{9,8},{10,11... | collective-permute-start | bytes 3145736 | tf_op jit(solution)/shard_map/ppermute | solution.py:209
  210.1 3.4 copy-start.1
  215.1 55.5 %all-to-all-start.4 = ((f32[16,129,256]{2,1,0:T(8,128)}), f32[16,129,256]{2,1,0:T(8,128)S(1)}, u32[]{:S(2)}, u32[]{:S(2)}) async-start(f32[16,129,256]{2,1,0:T(8,128)} %pad_maximum_fusion), calls=%async_computation.4 | async-start | bytes 4456448 | tf_op jit(solution)/shard_map/all_to_all | solution.py:223
  218.8 61.1 %copy-start.10 = (s32[2,1024]{1,0:T(2,128)S(1)}, s32[2,1024]{1,0:T(2,128)}, u32[]{:S(2)}) copy-start(s32[2,1024]{1,0:T(2,128)} %param.13) | copy-start | bytes 24580
  271.9 18.7 %all-to-all-start.5 = ((f32[32,4,256]{2,1,0:T(4,128)}), f32[32,4,256]{2,1,0:T(4,128)S(1)}, u32[]{:S(2)}, u32[]{:S(2)}) async-start(f32[32,4,256]{2,1,0:T(4,128)} %bitcast_select_fusion), calls=%async_computation.5 | async-start | bytes 262144 | tf_op jit(solution)/shard_map/all_to_all | solution.py:233
  335.1 6.0 %collective-permute-start.1 = (bf16[1024,256]{1,0:T(8,128)(2,1)S(1)}, bf16[1024,256]{1,0:T(8,128)(2,1)S(1)}, u32[]{:S(2)}, u32[]{:S(2)}) collective-permute-start(bf16[1024,256]{1,0:T(8,128)(2,1)S(1)} %bitcast.93), channel_id=1, source_target_pairs={{0,1},{1,0},{2,3},{3,2},{4,5},{5,4},{6,7},{7,6},{8,9},{9,8},{10,11... | collective-permute-start | bytes 1572872 | tf_op jit(solution)/shard_map/ppermute | solution.py:249

commit v10 on v9

--- a/solution.py
+++ b/solution.py
@@ -180,10 +180,12 @@
         axis=1,
     )
     lookup_grad = (factor[:, None, None] * back_all).astype(jnp.bfloat16)
-    grad_out = lax.dot_general(
-        pool_match,
+    pool_match_t = slots_all[:, None] == pair_targets[None, :, 0]
+    for bag in range(1, bags):
+        pool_match_t = pool_match_t | (slots_all[:, None] == pair_targets[None, :, bag])
+    grad_out = jnp.dot(
+        pool_match_t.astype(jnp.bfloat16),
         lookup_grad.reshape(batch * slots, emb_width),
-        (((0,), (0,)), ((), ())),
         preferred_element_type=jnp.float32,
     ).astype(jnp.bfloat16)
     grad_in = lax.all_to_all(
@@ -193,10 +195,12 @@
         concat_axis=0,
         tiled=True,
     )
-    row_sum = lax.dot_general(
-        row_match,
+    row_match_t = (jnp.arange(rows_dev, dtype=jnp.int32)[:, None] == flat_in[None, :]).astype(
+        jnp.bfloat16
+    )
+    row_sum = jnp.dot(
+        row_match_t,
         grad_in.reshape(shards * capacity, emb_width),
-        (((0,), (0,)), ((), ())),
         preferred_element_type=jnp.float32,
     )
     row_count = jnp.sum(row_match.astype(jnp.float32), axis=0)

time: 344 us -> 343 us (level)
  no operation moved by 1% of the time
where the time goes in v10:
time: 343 us; the launch traced here: 342 us
  waiting for transfers between devices  176 us (51%)
  blocking collectives  67.7 us (20%)
  starting transfers between devices  39.4 us (11%)
  matrix products  36.2 us (11%)
  other arithmetic  12.9 us (4%)
  local copies, waits for them, and re-layouts  8.54 us (2%)
    all_to_all x1, waiting for transfers between devices, body(): packed = jnp.sum(lax.all_to_all(packed, 'dp', 0, 0, tiled=True), axis=0)  50.8 us
    all_to_all x1, waiting for transfers between devices, body(): lax.all_to_all(jnp.broadcast_to(both[None], (n_dp,) + both.shape), 'dp',...  45.8 us
    all_to_all x1, waiting for transfers between devices, body(): lax.all_to_all(fetched.reshape(shards, capacity, emb_width), 'table', spl...  37.1 us
    all_to_all x1, blocking collectives, body(): lax.all_to_all(jnp.broadcast_to(finished[None], (n_dp,) + finished.shape)...  31 us
    all_to_all x1, waiting for transfers between devices, body(): lax.all_to_all(grad_out.reshape(shards, capacity, emb_width), 'table', sp...  30.3 us
    all_to_all x1, blocking collectives, body(): lax.all_to_all(outgoing, 'table', split_axis=0, concat_axis=0, tiled=True)  23.6 us
    all_to_all x1, blocking collectives, body(): lax.all_to_all(jnp.broadcast_to(part[None], (shards,) + part.shape), 'tab...  13.1 us
    all_to_all x1, waiting for transfers between devices, body(): part = jnp.sum(lax.all_to_all(part, 'table', 0, 0, tiled=True), axis=0)  10.6 us
  transfers between devices with their start and end apart: 7, of which 7 were waited for; matrix products, arithmetic and copies ran while one was open for 3% of the time, Pallas kernels for 0%

profile of v10, /device:TPU:1, one launch (start us, length us, event | category | flops | bytes accessed | tf_op | source)
XLA Modules:
  0.0 341.9 jit_solution(10056832017190654312)
XLA Ops:
  0.7 1.0 copy.23
  2.0 1.6 fusion.27
  3.6 1.0 fusion.38
  4.6 1.5 fusion.48
  6.3 4.4 %fusion.24 = s32[3072,3]{0,1:T(4,128)S(1)} fusion(s32[2048]{0:T(1024)S(1)} %multiply_add_fusion.1, bf16[2048,1]{0,1:T(2,128)(2,1)S(1)} %fusion.119, bf16[2048,1]{0,1:T(2,128)(2,1)S(1)} %get-tuple-element.10, bf16[3]{0:T(256)(128)(2,1)S(1)} %pad.15.clone), kind=kOutput, calls=%fused_computation.30 | convolution fusion | flops 44086272 | bytes 53254 | tf_op jit(solution)/shard_map/dot_general | solution.py:72
  10.8 23.6 %all_to_all.41 = s32[32,1,96]{2,1,0:T(1,128)S(1)} all-to-all(s32[32,1,96]{2,1,0:T(1,128)S(1)} %bitcast.111), channel_id=1, replica_groups=mesh['dp'=16,'table'=32] {'table'}, dimensions={0} | all-to-all | bytes 24576 | tf_op jit(solution)/shard_map/all_to_all | solution.py:82
  34.4 0.5 broadcast.764
  34.9 0.7 reduce.19
  35.7 3.6 %fusion.23 = bf16[3072,256]{1,0:T(8,128)(2,1)} fusion(bf16[1024,256]{1,0:T(8,128)(2,1)S(1)} %copy-done, s32[3072]{0:T(1024)S(1)} %eq.194), kind=kOutput, calls=%fused_computation.29 | convolution fusion | flops 1614544896 | bytes 2109440 | tf_op jit(solution)/shard_map/dot_general | solution.py:87
  39.3 4.2 %all-to-all-start.1 = ((bf16[32,96,256]{2,1,0:T(8,128)(2,1)}), bf16[32,96,256]{2,1,0:T(8,128)(2,1)S(1)}, u32[]{:S(2)}, u32[]{:S(2)}) async-start(bf16[32,96,256]{2,1,0:T(8,128)(2,1)} %bitcast.96), calls=%async_computation.1 | async-start | bytes 3145728 | tf_op jit(solution)/shard_map/all_to_all | solution.py:88
  43.6 0.5 reduce_sum.113
  44.1 0.5 convert_element_type.158
  44.9 0.5 slice_reduce_fusion.1
  45.4 37.1 %all-to-all-done.1 = bf16[32,96,256]{2,1,0:T(8,128)(2,1)S(1)} async-done(((bf16[32,96,256]{2,1,0:T(8,128)(2,1)}), bf16[32,96,256]{2,1,0:T(8,128)(2,1)S(1)}, u32[]{:S(2)}, u32[]{:S(2)}) %all-to-all-start.1) | async-done | bytes 1572896 | tf_op jit(solution)/shard_map/all_to_all | solution.py:88
  82.5 3.3 fusion.41
  86.4 0.7 copy-done.4
  87.4 1.5 broadcast_in_dim.72
  88.9 7.0 %all-to-all-start.2 = ((bf16[16,128,512]{2,1,0:T(8,128)(2,1)}), bf16[16,128,512]{2,1,0:T(8,128)(2,1)S(1)}, u32[]{:S(2)}, u32[]{:S(2)}) async-start(bf16[16,128,512]{2,1,0:T(8,128)(2,1)} %broadcast_in_dim.72), calls=%async_computation.2 | async-start | bytes 4194304 | tf_op jit(solution)/shard_map/all_to_all | solution.py:112
  95.8 2.3 multiply_reduce_fusion.4
  98.1 45.8 %all-to-all-done.2 = bf16[16,128,512]{2,1,0:T(8,128)(2,1)S(1)} async-done(((bf16[16,128,512]{2,1,0:T(8,128)(2,1)}), bf16[16,128,512]{2,1,0:T(8,128)(2,1)S(1)}, u32[]{:S(2)}, u32[]{:S(2)}) %all-to-all-start.2) | async-done | bytes 2097184 | tf_op jit(solution)/shard_map/all_to_all | solution.py:112
  144.2 2.4 multiply_reduce_fusion
  146.7 3.2 exponential_reduce_fusion
  150.0 2.7 fusion.68
  152.7 1.7 fusion.66
  154.5 0.4 multiply_reduce_fusion.1
  155.1 0.4 multiply_reduce_fusion.2
  156.0 4.5 %fusion.20 = bf16[3072,256]{1,0:T(8,128)(2,1)} fusion(s32[1024]{0:T(1024)S(1)} %get-tuple-element.9, s32[1024]{0:T(1024)S(1)} %get-tuple-element.8, f32[128,4,256]{2,1,0:T(4,128)S(1)} %reshape.542, f32[128,4,256]{2,1,0:T(4,128)S(1)} %reshape.541, f32[1024]{0:T(1024)S(1)} %mul.259), kind=kOutput, calls=%fused_computation.28 | convolution fusion | flops 1621622784 | bytes 2633728 | tf_op jit(solution)/shard_map/dot_general | solution.py:186
  160.5 9.7 %all-to-all-start.3 = ((bf16[32,96,256]{2,1,0:T(8,128)(2,1)}), bf16[32,96,256]{2,1,0:T(8,128)(2,1)}, u32[]{:S(2)}, u32[]{:S(2)}) async-start(bf16[32,96,256]{2,1,0:T(8,128)(2,1)} %bitcast.10), calls=%async_computation.3 | async-start | bytes 3145728 | tf_op jit(solution)/shard_map/all_to_all | solution.py:191
  170.5 1.3 broadcast_select_fusion
  171.8 2.4 collective-permute-start
  174.3 1.5 convert_reduce_fusion
  176.0 0.7 collective-permute-done
  176.7 2.4 select_add_fusion
  179.1 30.3 %all-to-all-done.3 = bf16[32,96,256]{2,1,0:T(8,128)(2,1)} async-done(((bf16[32,96,256]{2,1,0:T(8,128)(2,1)}), bf16[32,96,256]{2,1,0:T(8,128)(2,1)}, u32[]{:S(2)}, u32[]{:S(2)}) %all-to-all-start.3) | async-done | bytes 1572896 | tf_op jit(solution)/shard_map/all_to_all | solution.py:191
  209.4 3.3 fusion.7
  212.8 1.6 pad_maximum_fusion
  214.4 3.7 %all-to-all-start.4 = ((f32[16,129,256]{2,1,0:T(8,128)}), f32[16,129,256]{2,1,0:T(8,128)S(1)}, u32[]{:S(2)}, u32[]{:S(2)}) async-start(f32[16,129,256]{2,1,0:T(8,128)} %pad_maximum_fusion), calls=%async_computation.4 | async-start | bytes 4456448 | tf_op jit(solution)/shard_map/all_to_all | solution.py:227
  218.2 0.8 dynamic_slice.16
  219.0 50.8 %all-to-all-done.4 = f32[16,129,256]{2,1,0:T(8,128)S(1)} async-done(((f32[16,129,256]{2,1,0:T(8,128)}), f32[16,129,256]{2,1,0:T(8,128)S(1)}, u32[]{:S(2)}, u32[]{:S(2)}) %all-to-all-start.4) | async-done | bytes 2113568 | tf_op jit(solution)/shard_map/all_to_all | solution.py:227
  270.4 0.8 bitcast_select_fusion
  271.2 7.9 %all-to-all-start.5 = ((f32[32,4,256]{2,1,0:T(4,128)}), f32[32,4,256]{2,1,0:T(4,128)S(1)}, u32[]{:S(2)}, u32[]{:S(2)}) async-start(f32[32,4,256]{2,1,0:T(4,128)} %bitcast_select_fusion), calls=%async_computation.5 | async-start | bytes 262144 | tf_op jit(solution)/shard_map/all_to_all | solution.py:237
  279.2 10.6 %all-to-all-done.5 = f32[32,4,256]{2,1,0:T(4,128)S(1)} async-done(((f32[32,4,256]{2,1,0:T(4,128)}), f32[32,4,256]{2,1,0:T(4,128)S(1)}, u32[]{:S(2)}, u32[]{:S(2)}) %all-to-all-start.5) | async-done | bytes 131104 | tf_op jit(solution)/shard_map/all_to_all | solution.py:237
  290.0 13.1 %all_to_all.42 = bf16[32,4,256]{2,1,0:T(4,128)(2,1)S(1)} all-to-all(bf16[32,4,256]{2,1,0:T(4,128)(2,1)S(1)} %broadcast_in_dim.125), channel_id=1, replica_groups=mesh['dp'=16,'table'=32] {'table'}, dimensions={0} | all-to-all | bytes 131072 | tf_op jit(solution)/shard_map/all_to_all | solution.py:243
  303.3 31.0 %all_to_all.43 = bf16[16,128,256]{2,1,0:T(8,128)(2,1)S(1)} all-to-all(bf16[16,128,256]{2,1,0:T(8,128)(2,1)S(1)} %broadcast_in_dim.129), channel_id=1, replica_groups=mesh['dp'=16,'table'=32] {'dp'}, dimensions={0} | all-to-all | bytes 2097152 | tf_op jit(solution)/shard_map/all_to_all | solution.py:249
  334.3 4.5 %collective-permute-start.1 = (bf16[1024,256]{1,0:T(8,128)(2,1)S(1)}, bf16[1024,256]{1,0:T(8,128)(2,1)S(1)}, u32[]{:S(2)}, u32[]{:S(2)}) collective-permute-start(bf16[1024,256]{1,0:T(8,128)(2,1)S(1)} %bitcast.93), channel_id=1, source_target_pairs={{0,1},{1,0},{2,3},{3,2},{4,5},{5,4},{6,7},{7,6},{8,9},{9,8},{10,11... | collective-permute-start | bytes 1572872 | tf_op jit(solution)/shard_map/ppermute | solution.py:253
  338.8 1.1 bitcast_convert_fusion
  339.9 0.4 collective-permute-done.1
  340.4 1.5 fusion.53
  (75 shorter events, 4.6 us)
Async XLA Ops:
  0.6 35.1 %copy-start = (bf16[1024,256]{1,0:T(8,128)(2,1)S(1)}, bf16[1024,256]{1,0:T(8,128)(2,1)}, u32[]{:S(2)}) copy-start(bf16[1024,256]{1,0:T(8,128)(2,1)} %param.7) | copy-start | bytes 1572868
  0.6 2.9 copy-start.11
  39.3 43.2 %all-to-all-start.1 = ((bf16[32,96,256]{2,1,0:T(8,128)(2,1)}), bf16[32,96,256]{2,1,0:T(8,128)(2,1)S(1)}, u32[]{:S(2)}, u32[]{:S(2)}) async-start(bf16[32,96,256]{2,1,0:T(8,128)(2,1)} %bitcast.96), calls=%async_computation.1 | async-start | bytes 3145728 | tf_op jit(solution)/shard_map/all_to_all | solution.py:88
  82.5 3.6 %copy-start.2 = (bf16[1024,256]{1,0:T(8,128)(2,1)S(1)}, bf16[1024,256]{1,0:T(8,128)(2,1)}, u32[]{:S(2)}) copy-start(bf16[1024,256]{1,0:T(8,128)(2,1)} %param.11) | copy-start | bytes 1572868
  85.8 1.5 copy-start.6
  85.9 1.2 copy-start.4
  88.9 55.1 %all-to-all-start.2 = ((bf16[16,128,512]{2,1,0:T(8,128)(2,1)}), bf16[16,128,512]{2,1,0:T(8,128)(2,1)S(1)}, u32[]{:S(2)}, u32[]{:S(2)}) async-start(bf16[16,128,512]{2,1,0:T(8,128)(2,1)} %broadcast_in_dim.72), calls=%async_computation.2 | async-start | bytes 4194304 | tf_op jit(solution)/shard_map/all_to_all | solution.py:112
  144.2 2.4 copy-start.7
  144.2 2.4 copy-start.9
  149.9 2.8 copy-start.8
  150.0 4.5 %copy-start.3 = (bf16[1024,256]{1,0:T(8,128)(2,1)S(1)}, bf16[1024,256]{1,0:T(8,128)(2,1)}, u32[]{:S(2)}) copy-start(bf16[1024,256]{1,0:T(8,128)(2,1)} %param.11) | copy-start | bytes 1572868
  152.7 2.4 copy-start.5
  160.5 48.9 %all-to-all-start.3 = ((bf16[32,96,256]{2,1,0:T(8,128)(2,1)}), bf16[32,96,256]{2,1,0:T(8,128)(2,1)}, u32[]{:S(2)}, u32[]{:S(2)}) async-start(bf16[32,96,256]{2,1,0:T(8,128)(2,1)} %bitcast.10), calls=%async_computation.3 | async-start | bytes 3145728 | tf_op jit(solution)/shard_map/all_to_all | solution.py:191
  171.8 4.9 %collective-permute-start = (f32[1024,256]{1,0:T(8,128)}, f32[1024,256]{1,0:T(8,128)}, u32[]{:S(2)}, u32[]{:S(2)}) collective-permute-start(f32[1024,256]{1,0:T(8,128)} %get-tuple-element.30), channel_id=1, source_target_pairs={{0,1},{1,0},{2,3},{3,2},{4,5},{5,4},{6,7},{7,6},{8,9},{9,8},{10,11... | collective-permute-start | bytes 3145736 | tf_op jit(solution)/shard_map/ppermute | solution.py:213
  209.4 3.4 copy-start.1
  214.4 55.5 %all-to-all-start.4 = ((f32[16,129,256]{2,1,0:T(8,128)}), f32[16,129,256]{2,1,0:T(8,128)S(1)}, u32[]{:S(2)}, u32[]{:S(2)}) async-start(f32[16,129,256]{2,1,0:T(8,128)} %pad_maximum_fusion), calls=%async_computation.4 | async-start | bytes 4456448 | tf_op jit(solution)/shard_map/all_to_all | solution.py:227
  218.1 61.0 %copy-start.10 = (s32[2,1024]{1,0:T(2,128)S(1)}, s32[2,1024]{1,0:T(2,128)}, u32[]{:S(2)}) copy-start(s32[2,1024]{1,0:T(2,128)} %param.13) | copy-start | bytes 24580
  271.2 18.6 %all-to-all-start.5 = ((f32[32,4,256]{2,1,0:T(4,128)}), f32[32,4,256]{2,1,0:T(4,128)S(1)}, u32[]{:S(2)}, u32[]{:S(2)}) async-start(f32[32,4,256]{2,1,0:T(4,128)} %bitcast_select_fusion), calls=%async_computation.5 | async-start | bytes 262144 | tf_op jit(solution)/shard_map/all_to_all | solution.py:237
  334.3 6.0 %collective-permute-start.1 = (bf16[1024,256]{1,0:T(8,128)(2,1)S(1)}, bf16[1024,256]{1,0:T(8,128)(2,1)S(1)}, u32[]{:S(2)}, u32[]{:S(2)}) collective-permute-start(bf16[1024,256]{1,0:T(8,128)(2,1)S(1)} %bitcast.93), channel_id=1, source_target_pairs={{0,1},{1,0},{2,3},{3,2},{4,5},{5,4},{6,7},{7,6},{8,9},{9,8},{10,11... | collective-permute-start | bytes 1572872 | tf_op jit(solution)/shard_map/ppermute | solution.py:253

commit v11 on v10

--- a/solution.py
+++ b/solution.py
@@ -67,17 +67,12 @@
     slots_all = jnp.arange(shards * capacity, dtype=jnp.int32)
     slot_match = targets[:, None] == slots_all[None, :]
     row_parts = jnp.stack(
-        [local_rows // 32, local_rows % 32, jnp.ones_like(local_rows)], axis=1
-    ).astype(jnp.bfloat16)
-    slot_parts = lax.dot_general(
-        slot_match.astype(jnp.bfloat16),
-        row_parts,
-        (((0,), (0,)), ((), ())),
-        preferred_element_type=jnp.float32,
+        [local_rows // 32, local_rows % 32, jnp.ones_like(local_rows)], axis=0
+    ).astype(jnp.bfloat16)
+    slot_parts = jnp.dot(
+        row_parts, slot_match.astype(jnp.bfloat16), preferred_element_type=jnp.float32
     ).astype(jnp.int32)
-    outgoing = jnp.where(
-        slot_parts[:, 2] > 0, slot_parts[:, 0] * 32 + slot_parts[:, 1], -1
-    )
+    outgoing = jnp.where(slot_parts[2] > 0, slot_parts[0] * 32 + slot_parts[1], -1)
     outgoing = outgoing.reshape(shards, capacity)
     incoming = lax.all_to_all(outgoing, "table", split_axis=0, concat_axis=0, tiled=True)
     flat_in = incoming.reshape(-1)

time: 343 us -> 343 us (level)
  no operation moved by 1% of the time
where the time goes in v11:
time: 343 us; the launch traced here: 342 us
  waiting for transfers between devices  176 us (51%)
  blocking collectives  67.7 us (20%)
  starting transfers between devices  39.4 us (11%)
  matrix products  36.3 us (11%)
  other arithmetic  12.9 us (4%)
  local copies, waits for them, and re-layouts  8.54 us (2%)
    all_to_all x1, waiting for transfers between devices, body(): packed = jnp.sum(lax.all_to_all(packed, 'dp', 0, 0, tiled=True), axis=0)  50.8 us
    all_to_all x1, waiting for transfers between devices, body(): lax.all_to_all(jnp.broadcast_to(both[None], (n_dp,) + both.shape), 'dp',...  45.8 us
    all_to_all x1, waiting for transfers between devices, body(): lax.all_to_all(fetched.reshape(shards, capacity, emb_width), 'table', spl...  37.1 us
    all_to_all x1, blocking collectives, body(): lax.all_to_all(jnp.broadcast_to(finished[None], (n_dp,) + finished.shape)...  31 us
    all_to_all x1, waiting for transfers between devices, body(): lax.all_to_all(grad_out.reshape(shards, capacity, emb_width), 'table', sp...  30.3 us
    all_to_all x1, blocking collectives, body(): lax.all_to_all(outgoing, 'table', split_axis=0, concat_axis=0, tiled=True)  23.6 us
    all_to_all x1, blocking collectives, body(): lax.all_to_all(jnp.broadcast_to(part[None], (shards,) + part.shape), 'tab...  13.1 us
    all_to_all x1, waiting for transfers between devices, body(): part = jnp.sum(lax.all_to_all(part, 'table', 0, 0, tiled=True), axis=0)  10.6 us
  transfers between devices with their start and end apart: 7, of which 7 were waited for; matrix products, arithmetic and copies ran while one was open for 3% of the time, Pallas kernels for 0%

profile of v11, /device:TPU:1, one launch (start us, length us, event | category | flops | bytes accessed | tf_op | source)
XLA Modules:
  0.0 342.0 jit_solution(9400017170612954729)
XLA Ops:
  0.7 1.0 copy.23
  2.0 1.6 fusion.27
  3.6 1.0 fusion.38
  4.6 1.5 fusion.48
  6.3 4.5 %fusion.24 = s32[3,3072]{1,0:T(4,128)S(1)} fusion(s32[2048]{0:T(1024)S(1)} %multiply_add_fusion.1, bf16[1,2048]{1,0:T(2,128)(2,1)S(1)} %fusion.119, bf16[1,2048]{1,0:T(2,128)(2,1)S(1)} %get-tuple-element.10, bf16[3]{0:T(256)(128)(2,1)S(1)} %pad.15.clone), kind=kOutput, calls=%fused_computation.30 | convolution fusion | flops 44086272 | bytes 53254 | tf_op jit(solution)/shard_map/dot_general | solution.py:72
  10.9 23.6 %all_to_all.41 = s32[32,1,96]{2,1,0:T(1,128)S(1)} all-to-all(s32[32,1,96]{2,1,0:T(1,128)S(1)} %bitcast.111), channel_id=1, replica_groups=mesh['dp'=16,'table'=32] {'table'}, dimensions={0} | all-to-all | bytes 24576 | tf_op jit(solution)/shard_map/all_to_all | solution.py:77
  34.5 0.5 broadcast.782
  35.0 0.7 reduce.19
  35.8 3.6 %fusion.23 = bf16[3072,256]{1,0:T(8,128)(2,1)} fusion(bf16[1024,256]{1,0:T(8,128)(2,1)S(1)} %copy-done, s32[3072]{0:T(1024)S(1)} %eq.194), kind=kOutput, calls=%fused_computation.29 | convolution fusion | flops 1614544896 | bytes 2109440 | tf_op jit(solution)/shard_map/dot_general | solution.py:82
  39.4 4.2 %all-to-all-start.1 = ((bf16[32,96,256]{2,1,0:T(8,128)(2,1)}), bf16[32,96,256]{2,1,0:T(8,128)(2,1)S(1)}, u32[]{:S(2)}, u32[]{:S(2)}) async-start(bf16[32,96,256]{2,1,0:T(8,128)(2,1)} %bitcast.96), calls=%async_computation.1 | async-start | bytes 3145728 | tf_op jit(solution)/shard_map/all_to_all | solution.py:83
  43.7 0.5 reduce_sum.113
  44.2 0.5 convert_element_type.158
  45.0 0.5 slice_reduce_fusion.1
  45.5 37.1 %all-to-all-done.1 = bf16[32,96,256]{2,1,0:T(8,128)(2,1)S(1)} async-done(((bf16[32,96,256]{2,1,0:T(8,128)(2,1)}), bf16[32,96,256]{2,1,0:T(8,128)(2,1)S(1)}, u32[]{:S(2)}, u32[]{:S(2)}) %all-to-all-start.1) | async-done | bytes 1572896 | tf_op jit(solution)/shard_map/all_to_all | solution.py:83
  82.6 3.3 fusion.41
  86.5 0.7 copy-done.4
  87.5 1.5 broadcast_in_dim.72
  89.0 7.0 %all-to-all-start.2 = ((bf16[16,128,512]{2,1,0:T(8,128)(2,1)}), bf16[16,128,512]{2,1,0:T(8,128)(2,1)S(1)}, u32[]{:S(2)}, u32[]{:S(2)}) async-start(bf16[16,128,512]{2,1,0:T(8,128)(2,1)} %broadcast_in_dim.72), calls=%async_computation.2 | async-start | bytes 4194304 | tf_op jit(solution)/shard_map/all_to_all | solution.py:107
  96.0 2.3 multiply_reduce_fusion.4
  98.2 45.8 %all-to-all-done.2 = bf16[16,128,512]{2,1,0:T(8,128)(2,1)S(1)} async-done(((bf16[16,128,512]{2,1,0:T(8,128)(2,1)}), bf16[16,128,512]{2,1,0:T(8,128)(2,1)S(1)}, u32[]{:S(2)}, u32[]{:S(2)}) %all-to-all-start.2) | async-done | bytes 2097184 | tf_op jit(solution)/shard_map/all_to_all | solution.py:107
  144.3 2.4 multiply_reduce_fusion
  146.7 3.2 exponential_reduce_fusion
  150.1 2.7 fusion.68
  152.8 1.7 fusion.66
  154.6 0.4 multiply_reduce_fusion.1
  155.2 0.4 multiply_reduce_fusion.2
  156.1 4.5 %fusion.20 = bf16[3072,256]{1,0:T(8,128)(2,1)} fusion(s32[1024]{0:T(1024)S(1)} %get-tuple-element.9, s32[1024]{0:T(1024)S(1)} %get-tuple-element.8, f32[128,4,256]{2,1,0:T(4,128)S(1)} %reshape.557, f32[128,4,256]{2,1,0:T(4,128)S(1)} %reshape.556, f32[1024]{0:T(1024)S(1)} %mul.259), kind=kOutput, calls=%fused_computation.28 | convolution fusion | flops 1621622784 | bytes 2633728 | tf_op jit(solution)/shard_map/dot_general | solution.py:181
  160.5 9.7 %all-to-all-start.3 = ((bf16[32,96,256]{2,1,0:T(8,128)(2,1)}), bf16[32,96,256]{2,1,0:T(8,128)(2,1)}, u32[]{:S(2)}, u32[]{:S(2)}) async-start(bf16[32,96,256]{2,1,0:T(8,128)(2,1)} %bitcast.10), calls=%async_computation.3 | async-start | bytes 3145728 | tf_op jit(solution)/shard_map/all_to_all | solution.py:186
  170.6 1.3 broadcast_select_fusion
  171.9 2.4 collective-permute-start
  174.4 1.5 convert_reduce_fusion
  176.1 0.7 collective-permute-done
  176.8 2.4 select_add_fusion
  179.2 30.3 %all-to-all-done.3 = bf16[32,96,256]{2,1,0:T(8,128)(2,1)} async-done(((bf16[32,96,256]{2,1,0:T(8,128)(2,1)}), bf16[32,96,256]{2,1,0:T(8,128)(2,1)}, u32[]{:S(2)}, u32[]{:S(2)}) %all-to-all-start.3) | async-done | bytes 1572896 | tf_op jit(solution)/shard_map/all_to_all | solution.py:186
  209.5 3.3 fusion.7
  212.9 1.6 pad_maximum_fusion
  214.5 3.7 %all-to-all-start.4 = ((f32[16,129,256]{2,1,0:T(8,128)}), f32[16,129,256]{2,1,0:T(8,128)S(1)}, u32[]{:S(2)}, u32[]{:S(2)}) async-start(f32[16,129,256]{2,1,0:T(8,128)} %pad_maximum_fusion), calls=%async_computation.4 | async-start | bytes 4456448 | tf_op jit(solution)/shard_map/all_to_all | solution.py:222
  218.3 0.8 dynamic_slice.16
  219.1 50.8 %all-to-all-done.4 = f32[16,129,256]{2,1,0:T(8,128)S(1)} async-done(((f32[16,129,256]{2,1,0:T(8,128)}), f32[16,129,256]{2,1,0:T(8,128)S(1)}, u32[]{:S(2)}, u32[]{:S(2)}) %all-to-all-start.4) | async-done | bytes 2113568 | tf_op jit(solution)/shard_map/all_to_all | solution.py:222
  270.5 0.8 bitcast_select_fusion
  271.3 7.9 %all-to-all-start.5 = ((f32[32,4,256]{2,1,0:T(4,128)}), f32[32,4,256]{2,1,0:T(4,128)S(1)}, u32[]{:S(2)}, u32[]{:S(2)}) async-start(f32[32,4,256]{2,1,0:T(4,128)} %bitcast_select_fusion), calls=%async_computation.5 | async-start | bytes 262144 | tf_op jit(solution)/shard_map/all_to_all | solution.py:232
  279.3 10.6 %all-to-all-done.5 = f32[32,4,256]{2,1,0:T(4,128)S(1)} async-done(((f32[32,4,256]{2,1,0:T(4,128)}), f32[32,4,256]{2,1,0:T(4,128)S(1)}, u32[]{:S(2)}, u32[]{:S(2)}) %all-to-all-start.5) | async-done | bytes 131104 | tf_op jit(solution)/shard_map/all_to_all | solution.py:232
  290.1 13.1 %all_to_all.42 = bf16[32,4,256]{2,1,0:T(4,128)(2,1)S(1)} all-to-all(bf16[32,4,256]{2,1,0:T(4,128)(2,1)S(1)} %broadcast_in_dim.125), channel_id=1, replica_groups=mesh['dp'=16,'table'=32] {'table'}, dimensions={0} | all-to-all | bytes 131072 | tf_op jit(solution)/shard_map/all_to_all | solution.py:238
  303.4 31.0 %all_to_all.43 = bf16[16,128,256]{2,1,0:T(8,128)(2,1)S(1)} all-to-all(bf16[16,128,256]{2,1,0:T(8,128)(2,1)S(1)} %broadcast_in_dim.129), channel_id=1, replica_groups=mesh['dp'=16,'table'=32] {'dp'}, dimensions={0} | all-to-all | bytes 2097152 | tf_op jit(solution)/shard_map/all_to_all | solution.py:244
  334.4 4.5 %collective-permute-start.1 = (bf16[1024,256]{1,0:T(8,128)(2,1)S(1)}, bf16[1024,256]{1,0:T(8,128)(2,1)S(1)}, u32[]{:S(2)}, u32[]{:S(2)}) collective-permute-start(bf16[1024,256]{1,0:T(8,128)(2,1)S(1)} %bitcast.93), channel_id=1, source_target_pairs={{0,1},{1,0},{2,3},{3,2},{4,5},{5,4},{6,7},{7,6},{8,9},{9,8},{10,11... | collective-permute-start | bytes 1572872 | tf_op jit(solution)/shard_map/ppermute | solution.py:248
  338.9 1.1 bitcast_convert_fusion
  340.0 0.4 collective-permute-done.1
  340.5 1.5 fusion.53
  (75 shorter events, 4.6 us)
Async XLA Ops:
  0.6 35.2 %copy-start = (bf16[1024,256]{1,0:T(8,128)(2,1)S(1)}, bf16[1024,256]{1,0:T(8,128)(2,1)}, u32[]{:S(2)}) copy-start(bf16[1024,256]{1,0:T(8,128)(2,1)} %param.7) | copy-start | bytes 1572868
  0.6 2.9 copy-start.11
  39.4 43.2 %all-to-all-start.1 = ((bf16[32,96,256]{2,1,0:T(8,128)(2,1)}), bf16[32,96,256]{2,1,0:T(8,128)(2,1)S(1)}, u32[]{:S(2)}, u32[]{:S(2)}) async-start(bf16[32,96,256]{2,1,0:T(8,128)(2,1)} %bitcast.96), calls=%async_computation.1 | async-start | bytes 3145728 | tf_op jit(solution)/shard_map/all_to_all | solution.py:83
  82.6 3.6 %copy-start.2 = (bf16[1024,256]{1,0:T(8,128)(2,1)S(1)}, bf16[1024,256]{1,0:T(8,128)(2,1)}, u32[]{:S(2)}) copy-start(bf16[1024,256]{1,0:T(8,128)(2,1)} %param.11) | copy-start | bytes 1572868
  85.9 1.5 copy-start.6
  86.0 1.2 copy-start.4
  89.0 55.1 %all-to-all-start.2 = ((bf16[16,128,512]{2,1,0:T(8,128)(2,1)}), bf16[16,128,512]{2,1,0:T(8,128)(2,1)S(1)}, u32[]{:S(2)}, u32[]{:S(2)}) async-start(bf16[16,128,512]{2,1,0:T(8,128)(2,1)} %broadcast_in_dim.72), calls=%async_computation.2 | async-start | bytes 4194304 | tf_op jit(solution)/shard_map/all_to_all | solution.py:107
  144.3 2.4 copy-start.7
  144.3 2.4 copy-start.9
  150.0 2.8 copy-start.8
  150.1 4.5 %copy-start.3 = (bf16[1024,256]{1,0:T(8,128)(2,1)S(1)}, bf16[1024,256]{1,0:T(8,128)(2,1)}, u32[]{:S(2)}) copy-start(bf16[1024,256]{1,0:T(8,128)(2,1)} %param.11) | copy-start | bytes 1572868
  152.8 2.4 copy-start.5
  160.5 48.9 %all-to-all-start.3 = ((bf16[32,96,256]{2,1,0:T(8,128)(2,1)}), bf16[32,96,256]{2,1,0:T(8,128)(2,1)}, u32[]{:S(2)}, u32[]{:S(2)}) async-start(bf16[32,96,256]{2,1,0:T(8,128)(2,1)} %bitcast.10), calls=%async_computation.3 | async-start | bytes 3145728 | tf_op jit(solution)/shard_map/all_to_all | solution.py:186
  171.9 4.9 %collective-permute-start = (f32[1024,256]{1,0:T(8,128)}, f32[1024,256]{1,0:T(8,128)}, u32[]{:S(2)}, u32[]{:S(2)}) collective-permute-start(f32[1024,256]{1,0:T(8,128)} %get-tuple-element.30), channel_id=1, source_target_pairs={{0,1},{1,0},{2,3},{3,2},{4,5},{5,4},{6,7},{7,6},{8,9},{9,8},{10,11... | collective-permute-start | bytes 3145736 | tf_op jit(solution)/shard_map/ppermute | solution.py:208
  209.5 3.4 copy-start.1
  214.5 55.5 %all-to-all-start.4 = ((f32[16,129,256]{2,1,0:T(8,128)}), f32[16,129,256]{2,1,0:T(8,128)S(1)}, u32[]{:S(2)}, u32[]{:S(2)}) async-start(f32[16,129,256]{2,1,0:T(8,128)} %pad_maximum_fusion), calls=%async_computation.4 | async-start | bytes 4456448 | tf_op jit(solution)/shard_map/all_to_all | solution.py:222
  218.2 61.0 %copy-start.10 = (s32[2,1024]{1,0:T(2,128)S(1)}, s32[2,1024]{1,0:T(2,128)}, u32[]{:S(2)}) copy-start(s32[2,1024]{1,0:T(2,128)} %param.13) | copy-start | bytes 24580
  271.3 18.6 %all-to-all-start.5 = ((f32[32,4,256]{2,1,0:T(4,128)}), f32[32,4,256]{2,1,0:T(4,128)S(1)}, u32[]{:S(2)}, u32[]{:S(2)}) async-start(f32[32,4,256]{2,1,0:T(4,128)} %bitcast_select_fusion), calls=%async_computation.5 | async-start | bytes 262144 | tf_op jit(solution)/shard_map/all_to_all | solution.py:232
  334.4 6.0 %collective-permute-start.1 = (bf16[1024,256]{1,0:T(8,128)(2,1)S(1)}, bf16[1024,256]{1,0:T(8,128)(2,1)S(1)}, u32[]{:S(2)}, u32[]{:S(2)}) collective-permute-start(bf16[1024,256]{1,0:T(8,128)(2,1)S(1)} %bitcast.93), channel_id=1, source_target_pairs={{0,1},{1,0},{2,3},{3,2},{4,5},{5,4},{6,7},{7,6},{8,9},{9,8},{10,11... | collective-permute-start | bytes 1572872 | tf_op jit(solution)/shard_map/ppermute | solution.py:248

commit v12 on v11

--- a/solution.py
+++ b/solution.py
@@ -246,10 +246,8 @@
     )
     own_tower = finished[:, :dp_rows].reshape(hidden_width, out_width)
     other_tower = lax.ppermute(own_tower, "table", partner)
-    tower_update = jnp.where(
-        core == 0,
-        jnp.stack([own_tower, other_tower]),
-        jnp.stack([other_tower, own_tower]),
+    tower_update = lax.dynamic_slice_in_dim(
+        jnp.stack([own_tower, other_tower, own_tower]), core, 2, axis=0
     ).astype(jnp.float32)
     table_update = finished[:, dp_rows:].reshape(rows_dev, emb_width).astype(jnp.float32)
     return (table_update, tower_update)

time: 343 us -> 343 us (level)
  no operation moved by 1% of the time
where the time goes in v12:
time: 343 us; the launch traced here: 342 us
  waiting for transfers between devices  176 us (51%)
  blocking collectives  67.7 us (20%)
  starting transfers between devices  39.4 us (11%)
  matrix products  36.3 us (11%)
  other arithmetic  13.4 us (4%)
  local copies, waits for them, and re-layouts  8.54 us (2%)
    all_to_all x1, waiting for transfers between devices, body(): packed = jnp.sum(lax.all_to_all(packed, 'dp', 0, 0, tiled=True), axis=0)  50.8 us
    all_to_all x1, waiting for transfers between devices, body(): lax.all_to_all(jnp.broadcast_to(both[None], (n_dp,) + both.shape), 'dp',...  45.8 us
    all_to_all x1, waiting for transfers between devices, body(): lax.all_to_all(fetched.reshape(shards, capacity, emb_width), 'table', spl...  37.1 us
    all_to_all x1, blocking collectives, body(): lax.all_to_all(jnp.broadcast_to(finished[None], (n_dp,) + finished.shape)...  31 us
    all_to_all x1, waiting for transfers between devices, body(): lax.all_to_all(grad_out.reshape(shards, capacity, emb_width), 'table', sp...  30.3 us
    all_to_all x1, blocking collectives, body(): lax.all_to_all(outgoing, 'table', split_axis=0, concat_axis=0, tiled=True)  23.6 us
    all_to_all x1, blocking collectives, body(): lax.all_to_all(jnp.broadcast_to(part[None], (shards,) + part.shape), 'tab...  13.1 us
    all_to_all x1, waiting for transfers between devices, body(): part = jnp.sum(lax.all_to_all(part, 'table', 0, 0, tiled=True), axis=0)  10.6 us
  transfers between devices with their start and end apart: 7, of which 7 were waited for; matrix products, arithmetic and copies ran while one was open for 3% of the time, Pallas kernels for 0%

profile of v12, /device:TPU:1, one launch (start us, length us, event | category | flops | bytes accessed | tf_op | source)
XLA Modules:
  0.0 342.4 jit_solution(17875553077562518639)
XLA Ops:
  0.7 1.0 copy.23
  2.0 1.6 fusion.27
  3.6 1.0 fusion.38
  4.6 1.5 fusion.48
  6.3 4.5 %fusion.24 = s32[3,3072]{1,0:T(4,128)S(1)} fusion(s32[2048]{0:T(1024)S(1)} %multiply_add_fusion.1, bf16[1,2048]{1,0:T(2,128)(2,1)S(1)} %fusion.121, bf16[1,2048]{1,0:T(2,128)(2,1)S(1)} %get-tuple-element.10, bf16[3]{0:T(256)(128)(2,1)S(1)} %pad.14.clone), kind=kOutput, calls=%fused_computation.30 | convolution fusion | flops 44086272 | bytes 53254 | tf_op jit(solution)/shard_map/dot_general | solution.py:72
  10.9 23.6 %all_to_all.41 = s32[32,1,96]{2,1,0:T(1,128)S(1)} all-to-all(s32[32,1,96]{2,1,0:T(1,128)S(1)} %bitcast.111), channel_id=1, replica_groups=mesh['dp'=16,'table'=32] {'table'}, dimensions={0} | all-to-all | bytes 24576 | tf_op jit(solution)/shard_map/all_to_all | solution.py:77
  34.5 0.5 broadcast.782
  35.0 0.7 reduce.19
  35.8 3.6 %fusion.23 = bf16[3072,256]{1,0:T(8,128)(2,1)} fusion(bf16[1024,256]{1,0:T(8,128)(2,1)S(1)} %copy-done, s32[3072]{0:T(1024)S(1)} %eq.193), kind=kOutput, calls=%fused_computation.29 | convolution fusion | flops 1614544896 | bytes 2109440 | tf_op jit(solution)/shard_map/dot_general | solution.py:82
  39.4 4.2 %all-to-all-start.1 = ((bf16[32,96,256]{2,1,0:T(8,128)(2,1)}), bf16[32,96,256]{2,1,0:T(8,128)(2,1)S(1)}, u32[]{:S(2)}, u32[]{:S(2)}) async-start(bf16[32,96,256]{2,1,0:T(8,128)(2,1)} %bitcast.96), calls=%async_computation.1 | async-start | bytes 3145728 | tf_op jit(solution)/shard_map/all_to_all | solution.py:83
  43.7 0.5 reduce_sum.113
  44.2 0.5 convert_element_type.158
  45.0 0.5 slice_reduce_fusion.1
  45.5 37.1 %all-to-all-done.1 = bf16[32,96,256]{2,1,0:T(8,128)(2,1)S(1)} async-done(((bf16[32,96,256]{2,1,0:T(8,128)(2,1)}), bf16[32,96,256]{2,1,0:T(8,128)(2,1)S(1)}, u32[]{:S(2)}, u32[]{:S(2)}) %all-to-all-start.1) | async-done | bytes 1572896 | tf_op jit(solution)/shard_map/all_to_all | solution.py:83
  82.6 3.3 fusion.41
  86.5 0.7 copy-done.4
  87.5 1.5 broadcast_in_dim.72
  89.0 7.0 %all-to-all-start.2 = ((bf16[16,128,512]{2,1,0:T(8,128)(2,1)}), bf16[16,128,512]{2,1,0:T(8,128)(2,1)S(1)}, u32[]{:S(2)}, u32[]{:S(2)}) async-start(bf16[16,128,512]{2,1,0:T(8,128)(2,1)} %broadcast_in_dim.72), calls=%async_computation.2 | async-start | bytes 4194304 | tf_op jit(solution)/shard_map/all_to_all | solution.py:107
  96.0 2.3 multiply_reduce_fusion.4
  98.2 45.8 %all-to-all-done.2 = bf16[16,128,512]{2,1,0:T(8,128)(2,1)S(1)} async-done(((bf16[16,128,512]{2,1,0:T(8,128)(2,1)}), bf16[16,128,512]{2,1,0:T(8,128)(2,1)S(1)}, u32[]{:S(2)}, u32[]{:S(2)}) %all-to-all-start.2) | async-done | bytes 2097184 | tf_op jit(solution)/shard_map/all_to_all | solution.py:107
  144.3 2.4 multiply_reduce_fusion
  146.7 3.2 exponential_reduce_fusion
  150.1 2.7 fusion.70
  152.8 1.7 fusion.68
  154.6 0.4 multiply_reduce_fusion.1
  155.2 0.4 multiply_reduce_fusion.2
  156.1 4.5 %fusion.20 = bf16[3072,256]{1,0:T(8,128)(2,1)} fusion(s32[1024]{0:T(1024)S(1)} %get-tuple-element.9, s32[1024]{0:T(1024)S(1)} %get-tuple-element.8, f32[128,4,256]{2,1,0:T(4,128)S(1)} %reshape.557, f32[128,4,256]{2,1,0:T(4,128)S(1)} %reshape.556, f32[1024]{0:T(1024)S(1)} %mul.259), kind=kOutput, calls=%fused_computation.28 | convolution fusion | flops 1621622784 | bytes 2633728 | tf_op jit(solution)/shard_map/dot_general | solution.py:181
  160.5 9.7 %all-to-all-start.3 = ((bf16[32,96,256]{2,1,0:T(8,128)(2,1)}), bf16[32,96,256]{2,1,0:T(8,128)(2,1)}, u32[]{:S(2)}, u32[]{:S(2)}) async-start(bf16[32,96,256]{2,1,0:T(8,128)(2,1)} %bitcast.10), calls=%async_computation.3 | async-start | bytes 3145728 | tf_op jit(solution)/shard_map/all_to_all | solution.py:186
  170.6 1.3 broadcast_select_fusion
  171.9 2.4 collective-permute-start
  174.4 1.5 convert_reduce_fusion
  176.1 0.7 collective-permute-done
  176.8 2.4 select_add_fusion
  179.2 30.3 %all-to-all-done.3 = bf16[32,96,256]{2,1,0:T(8,128)(2,1)} async-done(((bf16[32,96,256]{2,1,0:T(8,128)(2,1)}), bf16[32,96,256]{2,1,0:T(8,128)(2,1)}, u32[]{:S(2)}, u32[]{:S(2)}) %all-to-all-start.3) | async-done | bytes 1572896 | tf_op jit(solution)/shard_map/all_to_all | solution.py:186
  209.5 3.3 fusion.7
  212.9 1.6 pad_maximum_fusion
  214.5 3.7 %all-to-all-start.4 = ((f32[16,129,256]{2,1,0:T(8,128)}), f32[16,129,256]{2,1,0:T(8,128)S(1)}, u32[]{:S(2)}, u32[]{:S(2)}) async-start(f32[16,129,256]{2,1,0:T(8,128)} %pad_maximum_fusion), calls=%async_computation.4 | async-start | bytes 4456448 | tf_op jit(solution)/shard_map/all_to_all | solution.py:222
  218.3 0.8 dynamic_slice.19
  219.1 50.8 %all-to-all-done.4 = f32[16,129,256]{2,1,0:T(8,128)S(1)} async-done(((f32[16,129,256]{2,1,0:T(8,128)}), f32[16,129,256]{2,1,0:T(8,128)S(1)}, u32[]{:S(2)}, u32[]{:S(2)}) %all-to-all-start.4) | async-done | bytes 2113568 | tf_op jit(solution)/shard_map/all_to_all | solution.py:222
  270.5 0.8 bitcast_select_fusion
  271.3 7.9 %all-to-all-start.5 = ((f32[32,4,256]{2,1,0:T(4,128)}), f32[32,4,256]{2,1,0:T(4,128)S(1)}, u32[]{:S(2)}, u32[]{:S(2)}) async-start(f32[32,4,256]{2,1,0:T(4,128)} %bitcast_select_fusion), calls=%async_computation.5 | async-start | bytes 262144 | tf_op jit(solution)/shard_map/all_to_all | solution.py:232
  279.3 10.6 %all-to-all-done.5 = f32[32,4,256]{2,1,0:T(4,128)S(1)} async-done(((f32[32,4,256]{2,1,0:T(4,128)}), f32[32,4,256]{2,1,0:T(4,128)S(1)}, u32[]{:S(2)}, u32[]{:S(2)}) %all-to-all-start.5) | async-done | bytes 131104 | tf_op jit(solution)/shard_map/all_to_all | solution.py:232
  290.1 13.1 %all_to_all.42 = bf16[32,4,256]{2,1,0:T(4,128)(2,1)S(1)} all-to-all(bf16[32,4,256]{2,1,0:T(4,128)(2,1)S(1)} %broadcast_in_dim.125), channel_id=1, replica_groups=mesh['dp'=16,'table'=32] {'table'}, dimensions={0} | all-to-all | bytes 131072 | tf_op jit(solution)/shard_map/all_to_all | solution.py:238
  303.4 31.0 %all_to_all.43 = bf16[16,128,256]{2,1,0:T(8,128)(2,1)S(1)} all-to-all(bf16[16,128,256]{2,1,0:T(8,128)(2,1)S(1)} %broadcast_in_dim.129), channel_id=1, replica_groups=mesh['dp'=16,'table'=32] {'dp'}, dimensions={0} | all-to-all | bytes 2097152 | tf_op jit(solution)/shard_map/all_to_all | solution.py:244
  334.4 4.5 %collective-permute-start.1 = (bf16[1024,256]{1,0:T(8,128)(2,1)S(1)}, bf16[1024,256]{1,0:T(8,128)(2,1)S(1)}, u32[]{:S(2)}, u32[]{:S(2)}) collective-permute-start(bf16[1024,256]{1,0:T(8,128)(2,1)S(1)} %bitcast.93), channel_id=1, source_target_pairs={{0,1},{1,0},{2,3},{3,2},{4,5},{5,4},{6,7},{7,6},{8,9},{9,8},{10,11... | collective-permute-start | bytes 1572872 | tf_op jit(solution)/shard_map/ppermute | solution.py:248
  339.0 1.1 bitcast_convert_fusion
  340.0 0.4 collective-permute-done.1
  340.5 1.9 fusion.53
  (75 shorter events, 4.6 us)
Async XLA Ops:
  0.6 35.2 %copy-start = (bf16[1024,256]{1,0:T(8,128)(2,1)S(1)}, bf16[1024,256]{1,0:T(8,128)(2,1)}, u32[]{:S(2)}) copy-start(bf16[1024,256]{1,0:T(8,128)(2,1)} %param.7) | copy-start | bytes 1572868
  0.6 2.9 copy-start.11
  39.4 43.2 %all-to-all-start.1 = ((bf16[32,96,256]{2,1,0:T(8,128)(2,1)}), bf16[32,96,256]{2,1,0:T(8,128)(2,1)S(1)}, u32[]{:S(2)}, u32[]{:S(2)}) async-start(bf16[32,96,256]{2,1,0:T(8,128)(2,1)} %bitcast.96), calls=%async_computation.1 | async-start | bytes 3145728 | tf_op jit(solution)/shard_map/all_to_all | solution.py:83
  82.6 3.6 %copy-start.2 = (bf16[1024,256]{1,0:T(8,128)(2,1)S(1)}, bf16[1024,256]{1,0:T(8,128)(2,1)}, u32[]{:S(2)}) copy-start(bf16[1024,256]{1,0:T(8,128)(2,1)} %param.11) | copy-start | bytes 1572868
  85.9 1.5 copy-start.6
  86.0 1.2 copy-start.4
  89.0 55.1 %all-to-all-start.2 = ((bf16[16,128,512]{2,1,0:T(8,128)(2,1)}), bf16[16,128,512]{2,1,0:T(8,128)(2,1)S(1)}, u32[]{:S(2)}, u32[]{:S(2)}) async-start(bf16[16,128,512]{2,1,0:T(8,128)(2,1)} %broadcast_in_dim.72), calls=%async_computation.2 | async-start | bytes 4194304 | tf_op jit(solution)/shard_map/all_to_all | solution.py:107
  144.3 2.4 copy-start.7
  144.3 2.4 copy-start.9
  150.0 2.8 copy-start.8
  150.1 4.5 %copy-start.3 = (bf16[1024,256]{1,0:T(8,128)(2,1)S(1)}, bf16[1024,256]{1,0:T(8,128)(2,1)}, u32[]{:S(2)}) copy-start(bf16[1024,256]{1,0:T(8,128)(2,1)} %param.11) | copy-start | bytes 1572868
  152.8 2.4 copy-start.5
  160.5 48.9 %all-to-all-start.3 = ((bf16[32,96,256]{2,1,0:T(8,128)(2,1)}), bf16[32,96,256]{2,1,0:T(8,128)(2,1)}, u32[]{:S(2)}, u32[]{:S(2)}) async-start(bf16[32,96,256]{2,1,0:T(8,128)(2,1)} %bitcast.10), calls=%async_computation.3 | async-start | bytes 3145728 | tf_op jit(solution)/shard_map/all_to_all | solution.py:186
  171.9 4.9 %collective-permute-start = (f32[1024,256]{1,0:T(8,128)}, f32[1024,256]{1,0:T(8,128)}, u32[]{:S(2)}, u32[]{:S(2)}) collective-permute-start(f32[1024,256]{1,0:T(8,128)} %get-tuple-element.30), channel_id=1, source_target_pairs={{0,1},{1,0},{2,3},{3,2},{4,5},{5,4},{6,7},{7,6},{8,9},{9,8},{10,11... | collective-permute-start | bytes 3145736 | tf_op jit(solution)/shard_map/ppermute | solution.py:208
  209.5 3.4 copy-start.1
  214.5 55.5 %all-to-all-start.4 = ((f32[16,129,256]{2,1,0:T(8,128)}), f32[16,129,256]{2,1,0:T(8,128)S(1)}, u32[]{:S(2)}, u32[]{:S(2)}) async-start(f32[16,129,256]{2,1,0:T(8,128)} %pad_maximum_fusion), calls=%async_computation.4 | async-start | bytes 4456448 | tf_op jit(solution)/shard_map/all_to_all | solution.py:222
  218.2 61.0 %copy-start.10 = (s32[2,1024]{1,0:T(2,128)S(1)}, s32[2,1024]{1,0:T(2,128)}, u32[]{:S(2)}) copy-start(s32[2,1024]{1,0:T(2,128)} %param.13) | copy-start | bytes 24580
  271.3 18.6 %all-to-all-start.5 = ((f32[32,4,256]{2,1,0:T(4,128)}), f32[32,4,256]{2,1,0:T(4,128)S(1)}, u32[]{:S(2)}, u32[]{:S(2)}) async-start(f32[32,4,256]{2,1,0:T(4,128)} %bitcast_select_fusion), calls=%async_computation.5 | async-start | bytes 262144 | tf_op jit(solution)/shard_map/all_to_all | solution.py:232
  334.4 6.0 %collective-permute-start.1 = (bf16[1024,256]{1,0:T(8,128)(2,1)S(1)}, bf16[1024,256]{1,0:T(8,128)(2,1)S(1)}, u32[]{:S(2)}, u32[]{:S(2)}) collective-permute-start(bf16[1024,256]{1,0:T(8,128)(2,1)S(1)} %bitcast.93), channel_id=1, source_target_pairs={{0,1},{1,0},{2,3},{3,2},{4,5},{5,4},{6,7},{7,6},{8,9},{9,8},{10,11... | collective-permute-start | bytes 1572872 | tf_op jit(solution)/shard_map/ppermute | solution.py:248
